TPU v7x, 512 devices: a whole 4x8x8 slice. The times are simulated.
512 devices in a mesh: seq: 64 (over x, z, core), mp: 8 (over y).
Axes of the slice: x: 4, y: 8, z: 8, core: 2. Of those that a mesh axis runs over, the one named last changes fastest.
Arguments:
- q_new: bfloat16 [16384, 3072], P('seq', 'mp'), may hold values from -100 to 100
- k_new: bfloat16 [16384, 3072], P('seq', 'mp'), may hold values from -100 to 100
- v_new: bfloat16 [16384, 3072], P('seq', 'mp'), may hold values from -6 to 6
- q_gain: float32 [3072], P('mp'), may hold values from 0.1 to 1.9
- k_gain: float32 [3072], P('mp'), may hold values from 0.1 to 1.9
- cache_k: bfloat16 [1024, 128, 3072], P('seq', None, 'mp'), may hold values from -300 to 300
- cache_v: bfloat16 [1024, 128, 3072], P('seq', None, 'mp'), may hold values from -6 to 6
- new_count: int32 [64, 2], replicated, may hold values from 1 to 192, 256 in all within a row
- prefix_blocks: int32 [128], replicated, may hold values from 0 to 64, as said below
- block_req: int32 [1024], replicated, may hold values from 0 to 127, as said below
Outputs:
- attended: bfloat16 [16384, 3072], P('seq', 'mp')
Inputs may be any that keep to these rules, and one draw needn't show every extreme that they name: Pool rows s * 16 .. (s + 1) * 16 - 1 lie on index s of seq; these blocks belong to requests of 16 different indices of seq (block_req // 2); exactly one request, the same on every index, owns one block on every index of seq (64 blocks in all). prefix_blocks[r] is the number of pool blocks b with block_req[b] = r.
All inputs are finite; a program needn't handle non-finite values.
Results may differ from a plain program's by a relative error of at most 0.015.
Values may be sent and summed in bfloat16 or wider, within the bound.
No kernel may reach another device: no remote copies, remote signals or barrier semaphores. Data moves between devices by JAX's collectives and lax.ppermute only.
A program may use at most 128 MiB of HBM per device.

v0:
```python
import jax
import jax.numpy as jnp
from jax import lax
from jax.sharding import PartitionSpec as P

HD = 128


NEGATIVE = -1e30


def rotate(field, position):
    half = field.shape[-1] // 2
    freq = 500000.0 ** (-(jnp.arange(half, dtype=jnp.float32) / half))
    angle = position.astype(jnp.float32)[:, None] * freq[None, :]
    cosine = jnp.cos(angle)[:, None, :]
    sine = jnp.sin(angle)[:, None, :]
    first = field[..., :half]
    second = field[..., half:]
    return jnp.concatenate([first * cosine - second * sine, second * cosine + first * sine], -1)


def token_meta(counts, prefix, first_req, block_len, tokens_here):
    cumul = jnp.cumsum(counts, axis=1)
    starts = cumul - counts
    order = jnp.arange(tokens_here, dtype=jnp.int32)
    local = jnp.sum((order[None, :, None] >= cumul[:, None, :]).astype(jnp.int32), -1)
    picker = (
        local[:, :, None] == jnp.arange(counts.shape[1], dtype=jnp.int32)[None, None, :]
    ).astype(jnp.int32)
    offset = order[None, :] - jnp.sum(picker * starts[:, None, :], -1)
    before = jnp.sum(picker * prefix[:, None, :], -1)
    return (first_req[:, None] + local, before * block_len + offset)


def update(carry, queries, keys_in, values_in, query_req, key_req):
    best, total, accum = carry
    scores = jnp.einsum(
        "thd,khd->htk", queries, keys_in, preferred_element_type=jnp.float32
    ) * queries.shape[-1] ** (-0.5)
    allowed = (query_req[:, None] == key_req[None, :])[None]
    scores = jnp.where(allowed, scores, NEGATIVE)
    fresh = jnp.maximum(best, jnp.max(scores, -1))
    weights = jnp.where(allowed, jnp.exp(scores - fresh[..., None]), 0.0)
    factor = jnp.exp(best - fresh)
    total = total * factor + jnp.sum(weights, -1)
    accum = accum * factor[..., None] + jnp.einsum(
        "htk,khd->htd", weights.astype(jnp.bfloat16), values_in, preferred_element_type=jnp.float32
    )
    return (fresh, total, accum)


def guarded(carry, queries, keys_in, values_in, query_req, key_req):
    return update(carry, queries, keys_in, values_in, query_req, key_req)


def shards(
    q_new, k_new, v_new, q_gain, k_gain, cache_k, cache_v, new_count, prefix_blocks, block_req
):
    tokens_here = q_new.shape[0]
    width_all = q_new.shape[1] * lax.axis_size("mp")
    heads_here = q_new.shape[1] // HD
    block_len = cache_k.shape[1]
    blocks_here = cache_k.shape[0]
    slots = lax.axis_size("seq")
    device = lax.axis_index("seq")
    per_dev = new_count.shape[1]
    query_f = q_new.astype(jnp.float32)
    key_f = k_new.astype(jnp.float32)
    square_q, square_k = lax.psum(
        (jnp.sum(query_f * query_f, -1), jnp.sum(key_f * key_f, -1)), "mp"
    )
    first_all = jnp.arange(slots, dtype=jnp.int32) * per_dev
    req_all, pos_all = token_meta(
        new_count, prefix_blocks.reshape(slots, per_dev), first_all, block_len, tokens_here
    )
    query_req = lax.dynamic_index_in_dim(req_all, device, 0, keepdims=False)
    position = lax.dynamic_index_in_dim(pos_all, device, 0, keepdims=False)
    normed_q = query_f * lax.rsqrt(square_q / width_all + 1e-06)[:, None] * q_gain
    normed_k = key_f * lax.rsqrt(square_k / width_all + 1e-06)[:, None] * k_gain
    queries = rotate(normed_q.reshape(tokens_here, heads_here, HD), position).astype(jnp.bfloat16)
    keys_here = rotate(normed_k.reshape(tokens_here, heads_here, HD), position).astype(jnp.bfloat16)
    values_here = v_new.reshape(tokens_here, heads_here, HD)
    scores = jnp.einsum(
        "thd,shd->hts", queries, keys_here, preferred_element_type=jnp.float32
    ) * HD ** (-0.5)
    order = jnp.arange(tokens_here, dtype=jnp.int32)
    allowed = (query_req[:, None] == query_req[None, :]) & (order[:, None] >= order[None, :])
    scores = jnp.where(allowed[None], scores, NEGATIVE)
    best = jnp.max(scores, -1)
    weights = jnp.where(allowed[None], jnp.exp(scores - best[..., None]), 0.0)
    total = jnp.sum(weights, -1)
    accum = jnp.einsum(
        "hts,shd->htd",
        weights.astype(jnp.bfloat16),
        values_here,
        preferred_element_type=jnp.float32,
    )
    carry = (best, total, accum)
    owner_table = block_req.reshape(slots, blocks_here)
    dest_table = owner_table // per_dev
    targets = jnp.arange(slots, dtype=jnp.int32)
    mine = lax.dynamic_index_in_dim(dest_table, device, 0, keepdims=False)
    hit = mine[None, :] == targets[:, None]
    arrive = dest_table == device
    picks = jnp.sum(jnp.where(hit, jnp.arange(blocks_here, dtype=jnp.int32)[None, :], 0), 1)
    present = jnp.any(hit, 1)[:, None, None]
    send_keys = jnp.where(present, jnp.take(cache_k, picks, axis=0), jnp.zeros((), jnp.bfloat16))
    send_values = jnp.where(present, jnp.take(cache_v, picks, axis=0), jnp.zeros((), jnp.bfloat16))
    got_keys, got_values = (
        lax.all_to_all(send_keys, "seq", split_axis=0, concat_axis=0, tiled=True),
        lax.all_to_all(send_values, "seq", split_axis=0, concat_axis=0, tiled=True),
    )
    slot_req = jnp.where(jnp.any(arrive, 1), jnp.sum(jnp.where(arrive, owner_table, 0), 1), -1)
    group = 8
    rounds = slots // group
    keys_all = got_keys.reshape(rounds, group * block_len, heads_here, HD)
    values_all = got_values.reshape(rounds, group * block_len, heads_here, HD)
    owners_all = jnp.repeat(slot_req, block_len).reshape(rounds, group * block_len)

    def visit(state, item):
        group_keys, group_values, group_req = item
        return (guarded(state, queries, group_keys, group_values, query_req, group_req), None)

    carry, _ = lax.scan(visit, carry, (keys_all, values_all, owners_all))
    best, total, accum = carry
    result = (accum / total[..., None]).astype(jnp.bfloat16)
    return jnp.transpose(result, (1, 0, 2)).reshape(tokens_here, heads_here * HD)


def solution(mesh):
    return jax.shard_map(
        shards,
        mesh=mesh,
        in_specs=(
            P("seq", "mp"),
            P("seq", "mp"),
            P("seq", "mp"),
            P("mp"),
            P("mp"),
            P("seq", None, "mp"),
            P("seq", None, "mp"),
            P(),
            P(),
            P(),
        ),
        out_specs=P("seq", "mp"),
        check_vma=False,
    )
```

profile of v0, /device:TPU:1, one launch (start us, length us, event | category | flops | bytes accessed | tf_op | source)
XLA Modules:
  0.0 390.9 jit_solution(7086043832742869696)
XLA Ops:
  0.0 0.9 reshape.183
  1.4 4.1 %gather_fusion = bf16[64,128,384]{2,1,0:T(8,128)(2,1)} fusion(bf16[16,128,384]{2,1,0:T(8,128)(2,1)S(1)} %copy-done, s32[1024]{0:T(1024)S(1)} %pad_clamp_fusion), kind=kCustom, calls=%fused_computation.clone | custom fusion | bytes 12583168 | tf_op jit(solution)/shard_map/jit(_take)/gather | solution.py:108
  5.5 4.1 %gather_fusion.1 = bf16[64,128,384]{2,1,0:T(8,128)(2,1)} fusion(bf16[16,128,384]{2,1,0:T(8,128)(2,1)S(1)} %copy-done.2, s32[1024]{0:T(1024)S(1)} %pad_clamp_fusion), kind=kCustom, calls=%fused_computation.1.clone | custom fusion | bytes 12583168 | tf_op jit(solution)/shard_map/jit(_take)/gather | solution.py:109
  9.6 8.9 %select_select_fusion = (bf16[64,128,384]{2,1,0:T(8,128)(2,1)}, bf16[64,128,384]{2,1,0:T(8,128)(2,1)S(1)}) fusion(bf16[64,128,384]{2,1,0:T(8,128)(2,1)} %gather_fusion.1, pred[64]{0:T(512)(128)(4,1)S(1)} %compare_and_fusion, pred[64]{0:T(512)(128)(4,1)S(1)} %fusion.36, bf16[64,128,384]{2,1,0:T(8,128)(2,1)} %gather_fusion), kind=kLoop, calls=%fused_computation.24 | loop fusion | flops 12582912 | bytes 25165952 | tf_op jit(solution)/shard_map/jit(_where)/select_n | solution.py:109
  18.5 155.8 %all_to_all.10 = bf16[64,128,384]{2,1,0:T(8,128)(2,1)} all-to-all(bf16[64,128,384]{2,1,0:T(8,128)(2,1)S(1)} %get-tuple-element.116), channel_id=1, replica_groups=mesh['seq'=64,'mp'=8] {'seq'}, dimensions={0} | all-to-all | bytes 12582912 | tf_op jit(solution)/shard_map/all_to_all | solution.py:111
  174.3 6.1 %all-to-all-start.1 = ((bf16[64,128,384]{2,1,0:T(8,128)(2,1)}), bf16[64,128,384]{2,1,0:T(8,128)(2,1)}, u32[]{:S(2)}, u32[]{:S(2)}) async-start(bf16[64,128,384]{2,1,0:T(8,128)(2,1)} %get-tuple-element.115), calls=%async_computation.1 | async-start | bytes 12582912 | tf_op jit(solution)/shard_map/all_to_all | solution.py:112
  181.2 15.6 %all-reduce = (f32[256]{0:T(256)S(1)}, f32[256]{0:T(256)S(1)}) all-reduce(f32[256]{0:T(256)S(1)} %fusion.22, f32[256]{0:T(256)S(1)} %fusion.24), channel_id=1, replica_groups=mesh['seq'=64,'mp'=8] {'mp'}, use_global_device_ids=true, to_apply=%region_3.0 | all-reduce | flops 512 | bytes 4096 | tf_op jit(solution)/shard_map/psum | solution.py:70
  201.8 16.6 %reshape.209 = bf16[8,1024,3,128]{3,2,1,0:T(4,128)(2,1)} reshape(bf16[64,128,384]{2,1,0:T(8,128)(2,1)} %all_to_all.10) | data formatting | bytes 12582912 | tf_op jit(solution)/shard_map/reshape | solution.py:117
  218.5 7.6 %copy.51 = bf16[8,1024,3,128]{3,1,2,0:T(8,128)(2,1)} copy(bf16[8,1024,3,128]{3,2,1,0:T(4,128)(2,1)} %reshape.209) | data formatting | bytes 12582912 | tf_op jit(solution)/shard_map/while | solution.py:125
  226.0 95.2 %all-to-all-done.1 = bf16[64,128,384]{2,1,0:T(8,128)(2,1)} async-done(((bf16[64,128,384]{2,1,0:T(8,128)(2,1)}), bf16[64,128,384]{2,1,0:T(8,128)(2,1)}, u32[]{:S(2)}, u32[]{:S(2)}) %all-to-all-start.1) | async-done | bytes 6291488 | tf_op jit(solution)/shard_map/all_to_all | solution.py:112
  321.2 16.6 %reshape.210 = bf16[8,1024,3,128]{3,2,1,0:T(4,128)(2,1)} reshape(bf16[64,128,384]{2,1,0:T(8,128)(2,1)} %all-to-all-done.1) | data formatting | bytes 12582912 | tf_op jit(solution)/shard_map/reshape | solution.py:118
  337.9 7.7 %copy.52 = bf16[8,1024,3,128]{3,1,2,0:T(8,128)(2,1)} copy(bf16[8,1024,3,128]{3,2,1,0:T(4,128)(2,1)} %reshape.210) | data formatting | bytes 12582912 | tf_op jit(solution)/shard_map/while | solution.py:125
  345.6 43.8 %while.14 = (s32[]{:T(128)}, f32[3,256]{1,0:T(4,128)S(1)}, f32[3,256]{1,0:T(4,128)S(1)}, f32[3,256,128]{2,1,0:T(8,128)S(1)}, s32[256]{0:T(256)S(1)}, /*index=5*/...) while((s32[]{:T(128)}, f32[3,256]{1,0:T(4,128)S(1)}, ...), condition=%wide.region_17.19_spmd, body=%wide.region_14.18_spmd.sunk | while | flops 413337088 | bytes 13105257 | solution.py:125
  345.8 1.8 fusion.58
  347.7 0.8 fusion.59
  348.5 2.5 fusion.60
  351.3 1.8 fusion.58
  353.2 0.8 fusion.59
  354.0 2.5 fusion.60
  356.8 1.8 fusion.58
  358.6 0.8 fusion.59
  359.5 2.5 fusion.60
  362.3 1.8 fusion.58
  365.0 2.5 fusion.60
  367.7 1.8 fusion.58
  370.4 2.5 fusion.60
  373.2 1.8 fusion.58
  375.9 2.5 fusion.60
  378.7 1.8 fusion.58
  381.4 2.5 fusion.60
  384.1 1.8 fusion.58
  386.9 2.5 fusion.60
  (112 shorter events, 13.6 us)
Async XLA Ops:
  0.0 1.4 copy-start
  1.4 4.1 %copy-start.2 = (bf16[16,128,384]{2,1,0:T(8,128)(2,1)S(1)}, bf16[16,128,384]{2,1,0:T(8,128)(2,1)}, u32[]{:S(2)}) copy-start(bf16[16,128,384]{2,1,0:T(8,128)(2,1)} %param.20) | copy-start | bytes 4718596
  174.3 6.2 %copy-start.6 = (s32[64,2]{0,1:T(2,128)S(1)}, s32[64,2]{0,1:T(2,128)}, u32[]{:S(2)}) copy-start(s32[64,2]{0,1:T(2,128)} %param.21) | copy-start | bytes 1540
  174.3 6.2 %copy-start.9 = (s32[128]{0:T(128)S(1)}, s32[128]{0:T(128)}, u32[]{:S(2)}) copy-start(s32[128]{0:T(128)} %param.22) | copy-start | bytes 1540
  174.3 6.4 %copy-start.3 = (bf16[256,384]{1,0:T(8,128)(2,1)S(1)}, bf16[256,384]{1,0:T(8,128)(2,1)}, u32[]{:S(2)}) copy-start(bf16[256,384]{1,0:T(8,128)(2,1)} %param.14) | copy-start | bytes 589828
  174.3 6.6 %copy-start.4 = (bf16[256,384]{1,0:T(8,128)(2,1)S(1)}, bf16[256,384]{1,0:T(8,128)(2,1)}, u32[]{:S(2)}) copy-start(bf16[256,384]{1,0:T(8,128)(2,1)} %param.15) | copy-start | bytes 589828
  174.3 22.6 %copy-start.7 = (f32[384]{0:T(512)S(1)}, f32[384]{0:T(512)}, u32[]{:S(2)}) copy-start(f32[384]{0:T(512)} %param.17) | copy-start | bytes 4612
  174.3 147.0 %all-to-all-start.1 = ((bf16[64,128,384]{2,1,0:T(8,128)(2,1)}), bf16[64,128,384]{2,1,0:T(8,128)(2,1)}, u32[]{:S(2)}, u32[]{:S(2)}) async-start(bf16[64,128,384]{2,1,0:T(8,128)(2,1)} %get-tuple-element.115), calls=%async_computation.1 | async-start | bytes 12582912 | tf_op jit(solution)/shard_map/all_to_all | solution.py:112
  180.4 16.9 %copy-start.8 = (f32[384]{0:T(512)S(1)}, f32[384]{0:T(512)}, u32[]{:S(2)}) copy-start(f32[384]{0:T(512)} %param.18) | copy-start | bytes 4612
  180.7 17.8 %copy-start.5 = (bf16[256,384]{1,0:T(8,128)(2,1)S(1)}, bf16[256,384]{1,0:T(8,128)(2,1)}, u32[]{:S(2)}) copy-start(bf16[256,384]{1,0:T(8,128)(2,1)} %param.16) | copy-start | bytes 589828
  389.4 1.5 copy-start.1
where the time goes:
time: 393 us; the launch traced here: 391 us
  blocking collectives  171 us (44%)
  waiting for transfers between devices  95.2 us (24%)
  local copies, waits for them, and re-layouts  61.6 us (16%)
  matrix products  35.5 us (9%)
  other arithmetic  20.3 us (5%)
  starting transfers between devices  6.14 us (2%)
    all_to_all x1, blocking collectives, shards(): lax.all_to_all(send_keys, 'seq', split_axis=0, concat_axis=0, tiled=True)  156 us
    all_to_all x1, waiting for transfers between devices, shards(): lax.all_to_all(send_values, 'seq', split_axis=0, concat_axis=0, tiled=True)  95.2 us
    dot_general x8, matrix products, update(): jnp.einsum('htk,khd->htd', weights.astype(jnp.bfloat16), values_in, prefe...  20 us
    reshape x1, local copies, waits for them, and re-layouts, shards(): keys_all = got_keys.reshape(rounds, group * block_len, heads_here, HD)  16.6 us
    reshape x1, local copies, waits for them, and re-layouts, shards(): values_all = got_values.reshape(rounds, group * block_len, heads_here, HD)  16.6 us
    psum x1, blocking collectives, shards(): lax.psum((jnp.sum(query_f * query_f, -1), jnp.sum(key_f * key_f, -1)), 'mp')  15.6 us
    while x3, local copies, waits for them, and re-layouts, shards(): carry, _ = lax.scan(visit, carry, (keys_all, values_all, owners_all))  15.5 us
    dot_general x8, matrix products, update(): jnp.einsum('thd,khd->htk', queries, keys_in, preferred_element_type=jnp.f...  14.8 us
  transfers between devices with their start and end apart: 1, of which 1 were waited for; matrix products, arithmetic and copies ran while one was open for 8% of the time, Pallas kernels for 0%

commit v1 on v0

v1 whole, which is shorter than its diff:
```python
import jax
import jax.numpy as jnp
from jax import lax
from jax.sharding import PartitionSpec as P

HD = 128


NEGATIVE = -1e30

CAPACITIES = (24, 32, 64)


def rotate(field, position):
    half = field.shape[-1] // 2
    freq = 500000.0 ** (-(jnp.arange(half, dtype=jnp.float32) / half))
    angle = position.astype(jnp.float32)[:, None] * freq[None, :]
    cosine = jnp.cos(angle)[:, None, :]
    sine = jnp.sin(angle)[:, None, :]
    first = field[..., :half]
    second = field[..., half:]
    return jnp.concatenate([first * cosine - second * sine, second * cosine + first * sine], -1)


def token_meta(counts, prefix, first_req, block_len, tokens_here):
    cumul = jnp.cumsum(counts, axis=1)
    starts = cumul - counts
    order = jnp.arange(tokens_here, dtype=jnp.int32)
    local = jnp.sum((order[None, :, None] >= cumul[:, None, :]).astype(jnp.int32), -1)
    picker = (
        local[:, :, None] == jnp.arange(counts.shape[1], dtype=jnp.int32)[None, None, :]
    ).astype(jnp.int32)
    offset = order[None, :] - jnp.sum(picker * starts[:, None, :], -1)
    before = jnp.sum(picker * prefix[:, None, :], -1)
    return (first_req[:, None] + local, before * block_len + offset)


def partial(queries, keys_in, values_in, allowed):
    scores = jnp.einsum(
        "thd,khd->htk", queries, keys_in, preferred_element_type=jnp.float32
    ) * queries.shape[-1] ** (-0.5)
    scores = jnp.where(allowed[None], scores, NEGATIVE)
    best = jnp.max(scores, -1)
    weights = jnp.where(allowed[None], jnp.exp(scores - best[..., None]), 0.0)
    total = jnp.sum(weights, -1)
    accum = jnp.einsum(
        "htk,khd->htd", weights.astype(jnp.bfloat16), values_in, preferred_element_type=jnp.float32
    )
    return best, total, accum


def shards(
    q_new, k_new, v_new, q_gain, k_gain, cache_k, cache_v, new_count, prefix_blocks, block_req
):
    tokens_here = q_new.shape[0]
    width_here = q_new.shape[1]
    width_all = width_here * lax.axis_size("mp")
    heads_here = width_here // HD
    block_len = cache_k.shape[1]
    blocks_here = cache_k.shape[0]
    slots = lax.axis_size("seq")
    device = lax.axis_index("seq")
    per_dev = new_count.shape[1]
    rows = block_len // slots
    pool = block_req.shape[0]

    stacked = jnp.concatenate([cache_k, cache_v], -1).reshape(
        blocks_here, slots, rows, 2 * width_here
    )
    spread = lax.all_to_all(stacked, "seq", split_axis=1, concat_axis=1, tiled=True)
    pieces = spread.reshape(blocks_here * slots, rows, 2 * width_here)

    query_f = q_new.astype(jnp.float32)
    key_f = k_new.astype(jnp.float32)
    square_q, square_k = lax.psum(
        (jnp.sum(query_f * query_f, -1), jnp.sum(key_f * key_f, -1)), "mp"
    )
    first_all = jnp.arange(slots, dtype=jnp.int32) * per_dev
    req_all, pos_all = token_meta(
        new_count, prefix_blocks.reshape(slots, per_dev), first_all, block_len, tokens_here
    )
    query_req = lax.dynamic_index_in_dim(req_all, device, 0, keepdims=False)
    position = lax.dynamic_index_in_dim(pos_all, device, 0, keepdims=False)
    normed_q = query_f * lax.rsqrt(square_q / width_all + 1e-06)[:, None] * q_gain
    normed_k = key_f * lax.rsqrt(square_k / width_all + 1e-06)[:, None] * k_gain
    queries = rotate(normed_q.reshape(tokens_here, heads_here, HD), position).astype(jnp.bfloat16)
    keys_here = rotate(normed_k.reshape(tokens_here, heads_here, HD), position).astype(jnp.bfloat16)
    values_here = v_new.reshape(tokens_here, heads_here, HD)

    order = jnp.arange(tokens_here, dtype=jnp.int32)
    causal = (query_req[:, None] == query_req[None, :]) & (order[:, None] >= order[None, :])
    own = partial(queries, keys_here, values_here, causal)

    hot = jnp.argmax(prefix_blocks).astype(jnp.int32)
    hot_dev = hot // per_dev
    hot_queries = lax.psum(
        jnp.where(device == hot_dev, queries, jnp.zeros((), jnp.bfloat16)), "seq"
    )
    owner_here = lax.dynamic_index_in_dim(
        block_req.reshape(slots, blocks_here), device, 0, keepdims=False
    )
    hot_slot = jnp.argmax(owner_here == hot).astype(jnp.int32)
    hot_keys = lax.dynamic_index_in_dim(cache_k, hot_slot, 0, keepdims=False)
    hot_values = lax.dynamic_index_in_dim(cache_v, hot_slot, 0, keepdims=False)
    hot_scores = jnp.einsum(
        "thd,khd->htk",
        hot_queries,
        hot_keys.reshape(block_len, heads_here, HD),
        preferred_element_type=jnp.float32,
    ) * HD ** (-0.5)
    hot_best = lax.pmax(jnp.max(hot_scores, -1), "seq")
    hot_weights = jnp.exp(hot_scores - hot_best[..., None])
    hot_total, hot_accum = lax.psum(
        (
            jnp.sum(hot_weights, -1),
            jnp.einsum(
                "htk,khd->htd",
                hot_weights.astype(jnp.bfloat16),
                hot_values.reshape(block_len, heads_here, HD),
                preferred_element_type=jnp.float32,
            ),
        ),
        "seq",
    )

    dest = block_req // per_dev
    onehot = (dest[:, None] == jnp.arange(slots, dtype=jnp.int32)[None, :]) & (
        block_req != hot
    )[:, None]
    rank = jnp.sum(jnp.where(onehot, jnp.cumsum(onehot.astype(jnp.int32), 0) - 1, 0), 1)
    counts = jnp.sum(onehot.astype(jnp.int32), 0)
    widest = CAPACITIES[-1]
    match = onehot.T[:, None, :] & (
        rank[None, None, :] == jnp.arange(widest, dtype=jnp.int32)[None, :, None]
    )
    ids = jnp.arange(pool, dtype=jnp.int32)
    table = jnp.sum(jnp.where(match, ids[None, None, :], 0), -1)
    present = jnp.any(match, -1)
    tags = jnp.where(present, block_req[table], -1)
    mine_tags = lax.dynamic_index_in_dim(tags, device, 0, keepdims=False)
    source = (table % blocks_here) * slots + table // blocks_here

    def cached(capacity):
        def run(pieces, source, present, mine_tags, queries, query_req):
            pick = source[:, :capacity].reshape(-1)
            send = jnp.where(
                present[:, :capacity, None, None],
                jnp.take(pieces, pick, axis=0).reshape(slots, capacity, rows, 2 * width_here),
                jnp.zeros((), jnp.bfloat16),
            )
            got = lax.all_to_all(send, "seq", split_axis=0, concat_axis=0, tiled=True)
            got = got.reshape(slots * capacity * rows, 2, heads_here, HD)
            key_req = jnp.broadcast_to(
                mine_tags[None, :capacity, None], (slots, capacity, rows)
            ).reshape(-1)
            allowed = query_req[:, None] == key_req[None, :]
            return partial(queries, got[:, 0], got[:, 1], allowed)

        return run

    level = jnp.sum((jnp.max(counts) > jnp.array(CAPACITIES[:-1], jnp.int32)).astype(jnp.int32))
    far = lax.switch(
        level,
        [cached(c) for c in CAPACITIES],
        pieces,
        source,
        present,
        mine_tags,
        queries,
        query_req,
    )

    hot_here = query_req == hot
    hot_best = jnp.where(hot_here[None, :], hot_best, NEGATIVE)
    hot_total = jnp.where(hot_here[None, :], hot_total, 0.0)
    hot_accum = jnp.where(hot_here[None, :, None], hot_accum, 0.0)
    parts = (own, far, (hot_best, hot_total, hot_accum))
    best = jnp.maximum(jnp.maximum(own[0], far[0]), hot_best)
    total = 0.0
    accum = 0.0
    for part_best, part_total, part_accum in parts:
        factor = jnp.exp(part_best - best)
        total = total + part_total * factor
        accum = accum + part_accum * factor[..., None]
    result = (accum / total[..., None]).astype(jnp.bfloat16)
    return jnp.transpose(result, (1, 0, 2)).reshape(tokens_here, heads_here * HD)


def solution(mesh):
    return jax.shard_map(
        shards,
        mesh=mesh,
        in_specs=(
            P("seq", "mp"),
            P("seq", "mp"),
            P("seq", "mp"),
            P("mp"),
            P("mp"),
            P("seq", None, "mp"),
            P("seq", None, "mp"),
            P(),
            P(),
            P(),
        ),
        out_specs=P("seq", "mp"),
        check_vma=False,
    )
```

time: 393 us -> 784 us (1.99)
  waiting for transfers between devices: 95.2 us -> 279 us
  blocking collectives: 171 us -> 269 us
  local copies, waits for them, and re-layouts: 61.6 us -> 102 us
  other arithmetic: 20.3 us -> 54.3 us
  between operations: 0.26 us -> 19.3 us
  matrix products: 35.5 us -> 18.6 us
  starting transfers between devices: 6.14 us -> 22 us
  loops' own time: 0.44 us -> 12.4 us
    all_to_all x1 -> x0, blocking collectives: 156 us -> none  [shards(): lax.all_to_all(send_keys, 'seq', split_axis=0, concat_axis=0, tiled=True)]
    psum x0 -> x2, waiting for transfers between devices: none -> 141 us  [the longest x1 140 us: shards(): lax.psum(jnp.where(device == hot_dev, queries, jnp.zeros((), jnp.bfloat16...]
    psum x0 -> x1, blocking collectives: none -> 128 us  [shards(): lax.psum((jnp.sum(hot_weights, -1), jnp.einsum('htk,khd->htd', hot_weight...]
    pmax x0 -> x1, blocking collectives: none -> 126 us  [shards(): hot_best = lax.pmax(jnp.max(hot_scores, -1), 'seq')]
    all_to_all x1 -> x2, waiting for transfers between devices: 95.2 us -> 138 us  [the longest x1 138 us: run(): got = lax.all_to_all(send, 'seq', split_axis=0, concat_axis=0, tiled=True)]
    gather x2 -> x3, local copies, waits for them, and re-layouts: 8.16 us -> 44.7 us  [the longest x1 28 us: run(): jnp.take(pieces, pick, axis=0)]
    dot_general x18 -> x5, matrix products: 35.5 us -> 8.11 us  [the longest x2 4.22 us: partial(): jnp.einsum('thd,khd->htk', queries, keys_in, preferred_element_type=jnp.f...]
    another operation x1 -> x5, other arithmetic: 0.21 us -> 20.3 us
  transfers between devices with their start and end apart: 1 -> 4, of which waited for: 1 -> 2; matrix products, arithmetic and copies ran while one was open for 8% -> 20% of each run, Pallas kernels for 0% -> 0%
where the time goes in v1:
time: 784 us; the launch traced here: 776 us
  waiting for transfers between devices  279 us (36%)
  blocking collectives  269 us (34%)
  local copies, waits for them, and re-layouts  102 us (13%)
  other arithmetic  54.3 us (7%)
  starting transfers between devices  22 us (3%)
  between operations  19.3 us (2%)
  matrix products  18.6 us (2%)
  loops' own time  12.4 us (2%)
    psum x1, waiting for transfers between devices, shards(): lax.psum(jnp.where(device == hot_dev, queries, jnp.zeros((), jnp.bfloat16...  140 us
    all_to_all x1, waiting for transfers between devices, run(): got = lax.all_to_all(send, 'seq', split_axis=0, concat_axis=0, tiled=True)  138 us
    psum x1, blocking collectives, shards(): lax.psum((jnp.sum(hot_weights, -1), jnp.einsum('htk,khd->htd', hot_weight...  128 us
    pmax x1, blocking collectives, shards(): hot_best = lax.pmax(jnp.max(hot_scores, -1), 'seq')  126 us
    gather x1, local copies, waits for them, and re-layouts, run(): jnp.take(pieces, pick, axis=0)  28 us
    reshape x1, local copies, waits for them, and re-layouts, run(): got = got.reshape(slots * capacity * rows, 2, heads_here, HD)  20.3 us
    another operation x3, other arithmetic  18.3 us
    gather x2, local copies, waits for them, and re-layouts, shards(): tags = jnp.where(present, block_req[table], -1)  16.8 us
  transfers between devices with their start and end apart: 4, of which 2 were waited for; matrix products, arithmetic and copies ran while one was open for 20% of the time, Pallas kernels for 0%

profile of v1, /device:TPU:1, one launch (start us, length us, event | category | flops | bytes accessed | tf_op | source)
XLA Modules:
  0.0 776.2 jit_solution(5354796531627445981)
XLA Ops:
  6.5 2.3 copy.137
  8.9 2.3 copy.138
  11.6 5.0 copy.139
  16.5 15.1 %all-to-all-start.3 = ((bf16[16,64,2,768]{3,2,0,1:T(2,128)(2,1)}), bf16[16,64,2,768]{3,2,0,1:T(2,128)(2,1)}, u32[]{:S(2)}, u32[]{:S(2)}) async-start(bf16[16,64,2,768]{3,2,0,1:T(2,128)(2,1)} %copy.139), calls=%async_computation.3 | async-start | bytes 6291456 | tf_op jit(solution)/shard_map/all_to_all | solution.py:70
  33.3 15.5 %all-reduce = (f32[256]{0:T(256)S(1)}, f32[256]{0:T(256)S(1)}) all-reduce(f32[256]{0:T(256)S(1)} %fusion.52, f32[256]{0:T(256)S(1)} %fusion.54), channel_id=1, replica_groups=mesh['seq'=64,'mp'=8] {'mp'}, use_global_device_ids=true, to_apply=%region_3.0 | all-reduce | flops 512 | bytes 4096 | tf_op jit(solution)/shard_map/psum | solution.py:75
  55.4 18.0 %reduce-window.6 = s32[64,8,128]{2,1,0:T(8,128)S(1)} reduce-window(s32[64,8,128]{2,1,0:T(8,128)S(1)} %fusion.68, s32[]{:T(128)} %constant.187.clone.1), window={size=1x1x128 pad=0_0x0_0x127_0}, to_apply=%region_13.14 | reduce-window | flops 8323072 | bytes 524292 | tf_op jit(solution)/shard_map/reduce-window
  74.9 3.1 fusion.44
  78.0 16.7 %gather_fusion.3 = s32[4096]{0:T(1024)S(1)} fusion(s32[1024]{0:T(1024)S(1)} %copy-done, s32[4096]{0:T(1024)S(1)} %broadcast_clamp_fusion.2), kind=kCustom, calls=%fused_computation.3 | custom fusion | bytes 49152 | tf_op jit(solution)/shard_map/gather | solution.py:139
  95.4 1.4 bitcast_reduce_fusion
  101.6 1.4 fusion.83
  103.6 1.8 compare_reduce_fusion
  106.7 1.1 broadcast_compare_fusion.5
  107.9 1.5 and_reduce_fusion
  110.0 140.5 %all-reduce.4.cloned.1.call-done = bf16[256,3,128]{2,0,1:T(8,128)(2,1)} async-done(((bf16[256,3,128]{2,0,1:T(8,128)(2,1)}), bf16[256,3,128]{2,0,1:T(8,128)(2,1)}) %all-reduce.4.cloned.1.call-update) | async-done | bytes 196624 | tf_op jit(solution)/shard_map/psum | solution.py:96
  250.5 1.2 fusion.97
  251.7 125.7 %pmax.7 = f32[3,256]{1,0:T(4,128)S(1)} all-reduce(f32[3,256]{1,0:T(4,128)S(1)} %get-tuple-element.232), channel_id=1, replica_groups=mesh['seq'=64,'mp'=8] {'seq'}, use_global_device_ids=true, to_apply=%region_30.31 | all-reduce | flops 768 | bytes 6144 | tf_op jit(solution)/shard_map/pmax | solution.py:111
  378.5 128.0 %psum.39 = f32[3,256]{1,0:T(4,128)} all-reduce(f32[3,256]{1,0:T(4,128)S(1)} %fusion.60), channel_id=1, replica_groups=mesh['seq'=64,'mp'=8] {'seq'}, use_global_device_ids=true, to_apply=%region_34.35 | all-reduce | flops 768 | bytes 6144 | tf_op jit(solution)/shard_map/psum | solution.py:113
  506.6 3.6 copy.140
  510.2 255.5 %conditional.1 = (f32[3,256]{1,0:T(4,128)}, f32[3,256]{1,0:T(4,128)}, f32[3,256,128]{1,2,0:T(8,128)}) conditional(s32[]{:T(128)} %clamp.3, (s32[256]{0:T(256)}, s32[64]{0:T(128)}, pred[64,64]{1,0:T(8,128)(4,1)S(1)}, s32[64,64]{1,0:T(8,128)S(1)}, bf16[1024,2,768]{2,0,1:T(8,128)(2,1)S(1)}, ...), branch_computations={%region_18.21_spmd, %region_21.24_spmd, %region_24.27_spmd} | conditional | flops 3317778944 | bytes 254790080 | solution.py:162
  516.6 4.9 copy.142
  521.6 28.0 %gather_fusion.1 = bf16[2048,2,768]{2,1,0:T(2,128)(2,1)} fusion(bf16[1024,2,768]{2,1,0:T(2,128)(2,1)} %copy.142, s32[2048]{0:T(1024)S(1)} %broadcast_clamp_fusion), kind=kCustom, calls=%fused_computation.1 | custom fusion | bytes 12591104 | tf_op jit(solution)/shard_map/cond/branch_1_fun/jit(_take)/gather | solution.py:148
  549.6 11.0 %broadcast_select_fusion.1 = bf16[64,32,2,768]{3,2,1,0:T(2,128)(2,1)} fusion(pred[64,32]{1,0:T(8,128)(4,1)S(1)} %bitcast.127, bf16[64,32,2,768]{3,2,1,0:T(2,128)(2,1)} %bitcast.116, pred[64,32]{1,0:T(8,128)(4,1)S(1)} %copy-done.16), kind=kLoop, calls=%fused_computation.7 | loop fusion | flops 6291456 | bytes 12587008 | tf_op jit(solution)/shard_map/cond/branch_1_fun/jit(_where)/select_n | solution.py:146
  560.6 6.2 all-to-all-start.1
  567.5 1.9 broadcast_compare_fusion
  569.4 138.1 %all-to-all-done.1 = bf16[64,32,2,768]{3,2,1,0:T(2,128)(2,1)} async-done(((bf16[64,32,2,768]{3,2,1,0:T(2,128)(2,1)}), bf16[64,32,2,768]{3,2,1,0:T(2,128)(2,1)}, u32[]{:S(2)}, u32[]{:S(2)}) %all-to-all-start.1) | async-done | bytes 6291488 | tf_op jit(solution)/shard_map/cond/branch_1_fun/all_to_all | solution.py:151
  707.5 20.3 %reshape.461 = bf16[4096,2,3,128]{3,2,1,0:T(4,128)(2,1)} reshape(bf16[64,32,2,768]{3,2,1,0:T(2,128)(2,1)} %all-to-all-done.1) | data formatting | bytes 12582912 | tf_op jit(solution)/shard_map/cond/branch_1_fun/reshape | solution.py:152
  727.8 7.0 fusion.92
  734.8 3.9 fusion
  738.7 4.6 copy-done.2
  743.2 4.5 fusion.2
  747.8 10.5 %fusion.3 = f32[3,256,128]{1,2,0:T(8,128)} fusion(f32[3,4096,256]{2,1,0:T(8,128)} %copy-done.2, f32[3,256]{1,0:T(4,128)} %get-tuple-element.245, pred[256,4096]{0,1:T(8,128)(4,1)S(1)} %broadcast_compare_fusion, bf16[4096,1,3,128]{3,2,1,0:T(4,128)(2,1)} %get-tuple-element.204), kind=kOutput, calls=%fused_computation.11 | convolution fusion | flops 821035008 | bytes 17173504 | tf_op jit(solution)/shard_map/cond | solution.py:162
  766.6 1.7 fusion.49
  (111 shorter events, 17.6 us)
Async XLA Ops:
  11.2 20.5 %copy-start.21 = (s32[64,2]{0,1:T(2,128)S(1)}, s32[64,2]{0,1:T(2,128)}, u32[]{:S(2)}) copy-start(s32[64,2]{0,1:T(2,128)} %param.21) | copy-start | bytes 1540
  11.2 20.7 %copy-start.24 = (s32[128]{0:T(128)S(1)}, s32[128]{0:T(128)}, u32[]{:S(2)}) copy-start(s32[128]{0:T(128)} %param.22) | copy-start | bytes 1540
  11.2 21.6 %copy-start.6 = (bf16[256,384]{1,0:T(8,128)(2,1)S(1)}, bf16[256,384]{1,0:T(8,128)(2,1)}, u32[]{:S(2)}) copy-start(bf16[256,384]{1,0:T(8,128)(2,1)} %param.14) | copy-start | bytes 589828
  11.2 21.8 %copy-start.7 = (bf16[256,384]{1,0:T(8,128)(2,1)S(1)}, bf16[256,384]{1,0:T(8,128)(2,1)}, u32[]{:S(2)}) copy-start(bf16[256,384]{1,0:T(8,128)(2,1)} %param.15) | copy-start | bytes 589828
  11.5 37.2 %copy-start.22 = (f32[384]{0:T(512)S(1)}, f32[384]{0:T(512)}, u32[]{:S(2)}) copy-start(f32[384]{0:T(512)} %param.17) | copy-start | bytes 4612
  11.5 37.3 %copy-start.23 = (f32[384]{0:T(512)S(1)}, f32[384]{0:T(512)}, u32[]{:S(2)}) copy-start(f32[384]{0:T(512)} %param.18) | copy-start | bytes 4612
  16.5 38.1 %copy-start = (s32[1024]{0:T(1024)S(1)}, s32[1024]{0:T(1024)}, u32[]{:S(2)}) copy-start(s32[1024]{0:T(1024)} %param.23) | copy-start | bytes 12292
  16.5 490.0 %all-to-all-start.3 = ((bf16[16,64,2,768]{3,2,0,1:T(2,128)(2,1)}), bf16[16,64,2,768]{3,2,0,1:T(2,128)(2,1)}, u32[]{:S(2)}, u32[]{:S(2)}) async-start(bf16[16,64,2,768]{3,2,0,1:T(2,128)(2,1)} %copy.139), calls=%async_computation.3 | async-start | bytes 6291456 | tf_op jit(solution)/shard_map/all_to_all | solution.py:70
  31.7 218.8 %all-reduce.4.cloned.1.call-start = ((), (), s32[]{:S(2)}) async-start(), calls=%async_computation.4 | async-start | bytes 393216 | tf_op jit(solution)/shard_map/psum | solution.py:96
  54.0 712.5 %all-reduce.6.cloned.1.call-start = ((), (), s32[]{:S(2)}) async-start(), calls=%async_computation.5 | async-start | bytes 786432 | tf_op jit(solution)/shard_map/psum | solution.py:113
  78.0 22.0 %copy-start.8 = (bf16[256,384]{1,0:T(8,128)(2,1)S(1)}, bf16[256,384]{1,0:T(8,128)(2,1)}, u32[]{:S(2)}) copy-start(bf16[256,384]{1,0:T(8,128)(2,1)} %param.16) | copy-start | bytes 589828
  78.0 23.6 %copy-start.25 = (s32[2]{0:T(128)S(1)}, s32[2]{0:T(128)}, u32[]{:S(2)}) copy-start(s32[2]{0:T(128)} %constant.209.clone) | copy-start | bytes 28
  105.4 401.1 %copy-start.10 = (s32[1,256]{1,0:T(1,128)}, s32[1,256]{1,0:T(1,128)S(1)}, u32[]{:S(2)}) copy-start(s32[1,256]{1,0:T(1,128)S(1)} %get-tuple-element.201) | copy-start | bytes 3076
  105.5 401.0 %copy-start.4 = (pred[256,256]{0,1:T(8,128)(4,1)}, pred[256,256]{0,1:T(8,128)(4,1)S(1)}, u32[]{:S(2)}) copy-start(pred[256,256]{0,1:T(8,128)(4,1)S(1)} %fusion.64) | copy-start | bytes 196612
  105.9 2.0 copy-start.3
  105.9 400.7 %copy-start.14 = (f32[3,256]{1,0:T(4,128)}, f32[3,256]{1,0:T(4,128)S(1)}, u32[]{:S(2)}) copy-start(f32[3,256]{1,0:T(4,128)S(1)} %get-tuple-element.234) | copy-start | bytes 9220
  377.4 132.8 %copy-start.9 = (f32[3,256]{1,0:T(4,128)}, f32[3,256]{1,0:T(4,128)S(1)}, u32[]{:S(2)}) copy-start(f32[3,256]{1,0:T(4,128)S(1)} %pmax.7) | copy-start | bytes 9220
  510.2 256.3 %copy-start.5 = (pred[256,256]{0,1:T(8,128)(4,1)S(1)}, pred[256,256]{0,1:T(8,128)(4,1)}, u32[]{:S(2)}) copy-start(pred[256,256]{0,1:T(8,128)(4,1)} %copy-done.4) | copy-start | bytes 196612
  516.6 32.9 %copy-start.16 = (pred[64,32]{1,0:T(8,128)(4,1)S(1)}, pred[64,32]{1,0:T(8,128)(4,1)}, u32[]{:S(2)}) copy-start(pred[64,32]{1,0:T(8,128)(4,1)} %get-tuple-element.190) | copy-start | bytes 6148 | tf_op jit(solution)/shard_map/cond
  560.6 6.2 copy-start.19
  560.6 6.9 copy-start.12
  560.6 146.9 %all-to-all-start.1 = ((bf16[64,32,2,768]{3,2,1,0:T(2,128)(2,1)}), bf16[64,32,2,768]{3,2,1,0:T(2,128)(2,1)}, u32[]{:S(2)}, u32[]{:S(2)}) async-start(bf16[64,32,2,768]{3,2,1,0:T(2,128)(2,1)} %broadcast_select_fusion.1), calls=%async_computation.1 | async-start | bytes 12582912 | tf_op jit(solution)/shard_map/cond/branch_1_fun/all_to_all | solution.py:151
  738.7 4.6 copy-start.2
Sparse Core Ops, SparseCore 0:
  54.1 196.3 all-reduce.3
  378.6 189.2 all-reduce.5

commit v2 on v1

--- a/solution.py
+++ b/solution.py
@@ -93,52 +93,80 @@
 
     hot = jnp.argmax(prefix_blocks).astype(jnp.int32)
     hot_dev = hot // per_dev
-    hot_queries = lax.psum(
-        jnp.where(device == hot_dev, queries, jnp.zeros((), jnp.bfloat16)), "seq"
-    )
+    piece = tokens_here // slots
+    spread_q = lax.all_to_all(
+        queries.reshape(slots, piece, heads_here, HD), "seq", split_axis=0, concat_axis=0, tiled=True
+    )
+    mine_q = lax.dynamic_index_in_dim(spread_q, hot_dev, 0, keepdims=False)
+    hot_queries = lax.all_to_all(
+        jnp.broadcast_to(mine_q[None], (slots, piece, heads_here, HD)),
+        "seq",
+        split_axis=0,
+        concat_axis=0,
+        tiled=True,
+    ).reshape(tokens_here, heads_here, HD)
     owner_here = lax.dynamic_index_in_dim(
         block_req.reshape(slots, blocks_here), device, 0, keepdims=False
     )
     hot_slot = jnp.argmax(owner_here == hot).astype(jnp.int32)
     hot_keys = lax.dynamic_index_in_dim(cache_k, hot_slot, 0, keepdims=False)
     hot_values = lax.dynamic_index_in_dim(cache_v, hot_slot, 0, keepdims=False)
-    hot_scores = jnp.einsum(
-        "thd,khd->htk",
+    every = jnp.ones((tokens_here, block_len), bool)
+    hot_part = partial(
         hot_queries,
         hot_keys.reshape(block_len, heads_here, HD),
-        preferred_element_type=jnp.float32,
-    ) * HD ** (-0.5)
-    hot_best = lax.pmax(jnp.max(hot_scores, -1), "seq")
-    hot_weights = jnp.exp(hot_scores - hot_best[..., None])
-    hot_total, hot_accum = lax.psum(
-        (
-            jnp.sum(hot_weights, -1),
-            jnp.einsum(
-                "htk,khd->htd",
-                hot_weights.astype(jnp.bfloat16),
-                hot_values.reshape(block_len, heads_here, HD),
-                preferred_element_type=jnp.float32,
-            ),
-        ),
+        hot_values.reshape(block_len, heads_here, HD),
+        every,
+    )
+    packed = jnp.concatenate(
+        [hot_part[2], hot_part[0][..., None], hot_part[1][..., None]], -1
+    ).reshape(heads_here, slots, piece, HD + 2)
+    gathered = lax.all_to_all(
+        jnp.transpose(packed, (1, 0, 2, 3)), "seq", split_axis=0, concat_axis=0, tiled=True
+    )
+    piece_best = jnp.max(gathered[..., HD], 0)
+    piece_factor = jnp.exp(gathered[..., HD] - piece_best[None])
+    merged = jnp.concatenate(
+        [
+            jnp.sum(gathered[..., :HD] * piece_factor[..., None], 0),
+            piece_best[..., None],
+            jnp.sum(gathered[..., HD + 1] * piece_factor, 0)[..., None],
+        ],
+        -1,
+    )
+    returned = lax.all_to_all(
+        jnp.broadcast_to(merged[None], (slots,) + merged.shape),
         "seq",
-    )
-
-    dest = block_req // per_dev
-    onehot = (dest[:, None] == jnp.arange(slots, dtype=jnp.int32)[None, :]) & (
-        block_req != hot
-    )[:, None]
-    rank = jnp.sum(jnp.where(onehot, jnp.cumsum(onehot.astype(jnp.int32), 0) - 1, 0), 1)
-    counts = jnp.sum(onehot.astype(jnp.int32), 0)
+        split_axis=0,
+        concat_axis=0,
+        tiled=True,
+    )
+    returned = jnp.transpose(returned, (1, 0, 2, 3)).reshape(heads_here, tokens_here, HD + 2)
+    hot_accum = returned[..., :HD]
+    hot_best = returned[..., HD]
+    hot_total = returned[..., HD + 1]
+
+    targets = jnp.arange(slots, dtype=jnp.int32)
+    owner_table = block_req.reshape(slots, blocks_here)
+    usable = owner_table != hot
+    hit = ((owner_table // per_dev)[:, :, None] == targets[None, None, :]) & usable[:, :, None]
+    has = jnp.any(hit, 1)
+    slot_of = jnp.sum(jnp.where(hit, jnp.arange(blocks_here, dtype=jnp.int32)[None, :, None], 0), 1)
+    req_of = jnp.sum(jnp.where(hit, owner_table[:, :, None], 0), 1)
+    lower = (targets[:, None] > targets[None, :]).astype(jnp.bfloat16)
+    rank = jnp.einsum(
+        "st,td->sd", lower, has.astype(jnp.bfloat16), preferred_element_type=jnp.float32
+    ).astype(jnp.int32)
+    counts = jnp.sum(has.astype(jnp.int32), 0)
     widest = CAPACITIES[-1]
-    match = onehot.T[:, None, :] & (
-        rank[None, None, :] == jnp.arange(widest, dtype=jnp.int32)[None, :, None]
-    )
-    ids = jnp.arange(pool, dtype=jnp.int32)
-    table = jnp.sum(jnp.where(match, ids[None, None, :], 0), -1)
-    present = jnp.any(match, -1)
-    tags = jnp.where(present, block_req[table], -1)
+    match = has[None] & (rank[None] == jnp.arange(widest, dtype=jnp.int32)[:, None, None])
+    sources = targets[None, :, None]
+    source = jnp.transpose(
+        jnp.sum(jnp.where(match, slot_of[None] * slots + sources, 0), 1)
+    )
+    present = jnp.transpose(jnp.any(match, 1))
+    tags = jnp.transpose(jnp.where(jnp.any(match, 1), jnp.sum(jnp.where(match, req_of[None], 0), 1), -1))
     mine_tags = lax.dynamic_index_in_dim(tags, device, 0, keepdims=False)
-    source = (table % blocks_here) * slots + table // blocks_here
 
     def cached(capacity):
         def run(pieces, source, present, mine_tags, queries, query_req):

time: 784 us -> 491 us (0.63)
  blocking collectives: 269 us -> 43.1 us
  waiting for transfers between devices: 279 us -> 223 us
  starting transfers between devices: 22 us -> 42.9 us
  between operations: 19.3 us -> 6.24 us
  other arithmetic: 54.3 us -> 42.4 us
    psum x2 -> x0, waiting for transfers between devices: 141 us -> none  [the longest x1 140 us: shards(): lax.psum(jnp.where(device == hot_dev, queries, jnp.zeros((), jnp.bfloat16...]
    psum x1 -> x0, blocking collectives: 128 us -> none  [shards(): lax.psum((jnp.sum(hot_weights, -1), jnp.einsum('htk,khd->htd', hot_weight...]
    pmax x1 -> x0, blocking collectives: 126 us -> none  [shards(): hot_best = lax.pmax(jnp.max(hot_scores, -1), 'seq')]
    all_to_all x1, waiting for transfers between devices: 0.01 us -> 57.5 us  [shards(): lax.all_to_all(stacked, 'seq', split_axis=1, concat_axis=1, tiled=True)]
    all_to_all x0 -> x3, starting transfers between devices: none -> 30 us  [the longest x1 17.8 us: shards(): lax.all_to_all(queries.reshape(slots, piece, heads_here, HD), 'seq', spli...]
    all_to_all x0 -> x1, blocking collectives: none -> 28.4 us  [shards(): lax.all_to_all(jnp.transpose(packed, (1, 0, 2, 3)), 'seq', split_axis=0,...]
    all_to_all x0 -> x3, waiting for transfers between devices: none -> 28.2 us  [the longest x1 14.3 us: shards(): lax.all_to_all(jnp.broadcast_to(merged[None], (slots,) + merged.shape), '...]
    gather x2 -> x0, local copies, waits for them, and re-layouts: 16.8 us -> none  [shards(): tags = jnp.where(present, block_req[table], -1)]
  transfers between devices with their start and end apart: 4 -> 5, of which waited for: 2 -> 5; matrix products, arithmetic and copies ran while one was open for 20% -> 6% of each run, Pallas kernels for 0% -> 0%
where the time goes in v2:
time: 491 us; the launch traced here: 482 us
  waiting for transfers between devices  223 us (45%)
  local copies, waits for them, and re-layouts  94.2 us (19%)
  blocking collectives  43.1 us (9%)
  starting transfers between devices  42.9 us (9%)
  other arithmetic  42.4 us (9%)
  matrix products  17.1 us (3%)
  loops' own time  13 us (3%)
  between operations  6.24 us (1%)
    all_to_all x1, waiting for transfers between devices, run(): got = lax.all_to_all(send, 'seq', split_axis=0, concat_axis=0, tiled=True)  137 us
    all_to_all x1, waiting for transfers between devices, shards(): lax.all_to_all(stacked, 'seq', split_axis=1, concat_axis=1, tiled=True)  57.5 us
    all_to_all x1, blocking collectives, shards(): lax.all_to_all(jnp.transpose(packed, (1, 0, 2, 3)), 'seq', split_axis=0,...  28.4 us
    gather x1, local copies, waits for them, and re-layouts, run(): jnp.take(pieces, pick, axis=0)  28 us
    reshape x1, local copies, waits for them, and re-layouts, run(): got = got.reshape(slots * capacity * rows, 2, heads_here, HD)  20.3 us
    all_to_all x1, starting transfers between devices, shards(): lax.all_to_all(queries.reshape(slots, piece, heads_here, HD), 'seq', spli...  17.8 us
    psum x1, blocking collectives, shards(): lax.psum((jnp.sum(query_f * query_f, -1), jnp.sum(key_f * key_f, -1)), 'mp')  14.7 us
    all_to_all x1, waiting for transfers between devices, shards(): lax.all_to_all(jnp.broadcast_to(merged[None], (slots,) + merged.shape), '...  14.3 us
  transfers between devices with their start and end apart: 5, of which 5 were waited for; matrix products, arithmetic and copies ran while one was open for 6% of the time, Pallas kernels for 0%

profile of v2, /device:TPU:1, one launch (start us, length us, event | category | flops | bytes accessed | tf_op | source)
XLA Modules:
  0.0 481.7 jit_solution(14137580702659066413)
XLA Ops:
  5.9 14.7 %all-reduce = (f32[256]{0:T(256)S(1)}, f32[256]{0:T(256)S(1)}) all-reduce(f32[256]{0:T(256)S(1)} %fusion.43, f32[256]{0:T(256)S(1)} %fusion.45), channel_id=1, replica_groups=mesh['seq'=64,'mp'=8] {'mp'}, use_global_device_ids=true, to_apply=%region_3.0 | all-reduce | flops 512 | bytes 4096 | tf_op jit(solution)/shard_map/psum | solution.py:75
  25.9 2.0 subtract_convert_fusion
  28.9 17.8 %all-to-all-start.4 = ((bf16[64,4,3,128]{3,1,2,0:T(4,128)(2,1)}), bf16[64,4,3,128]{3,1,2,0:T(4,128)(2,1)S(1)}, u32[]{:S(2)}, u32[]{:S(2)}) async-start(bf16[64,4,3,128]{3,1,2,0:T(4,128)(2,1)} %copy.370), calls=%async_computation.4 | async-start | bytes 393216 | tf_op jit(solution)/shard_map/all_to_all | solution.py:97
  49.9 7.7 %all-to-all-done.4 = bf16[64,4,3,128]{3,1,2,0:T(4,128)(2,1)S(1)} async-done(((bf16[64,4,3,128]{3,1,2,0:T(4,128)(2,1)}), bf16[64,4,3,128]{3,1,2,0:T(4,128)(2,1)S(1)}, u32[]{:S(2)}, u32[]{:S(2)}) %all-to-all-start.4) | async-done | bytes 196640 | tf_op jit(solution)/shard_map/all_to_all | solution.py:97
  58.3 5.7 %all-to-all-start.5 = ((bf16[64,4,3,128]{3,1,2,0:T(4,128)(2,1)}), bf16[64,4,3,128]{3,1,2,0:T(4,128)(2,1)S(1)}, u32[]{:S(2)}, u32[]{:S(2)}) async-start(bf16[64,4,3,128]{3,1,2,0:T(4,128)(2,1)} %broadcast_in_dim.342), calls=%async_computation.5 | async-start | bytes 393216 | tf_op jit(solution)/shard_map/all_to_all | solution.py:101
  64.1 1.4 bitcast_reduce_fusion
  68.7 6.2 %all-to-all-done.5 = bf16[64,4,3,128]{3,1,2,0:T(4,128)(2,1)S(1)} async-done(((bf16[64,4,3,128]{3,1,2,0:T(4,128)(2,1)}), bf16[64,4,3,128]{3,1,2,0:T(4,128)(2,1)S(1)}, u32[]{:S(2)}, u32[]{:S(2)}) %all-to-all-start.5) | async-done | bytes 196640 | tf_op jit(solution)/shard_map/all_to_all | solution.py:101
  75.9 1.3 copy.351
  78.8 28.4 %all_to_all.37 = f32[64,3,4,130]{3,2,1,0:T(4,128)S(1)} all-to-all(f32[64,3,4,130]{3,2,1,0:T(4,128)S(1)} %maximum_bitcast_fusion), channel_id=1, replica_groups=mesh['seq'=64,'mp'=8] {'seq'}, dimensions={0} | all-to-all | bytes 798720 | tf_op jit(solution)/shard_map/all_to_all | solution.py:124
  109.9 6.5 %all-to-all-start.7 = ((f32[64,3,4,130]{3,2,1,0:T(4,128)}), f32[64,3,4,130]{3,2,1,0:T(4,128)S(1)}, u32[]{:S(2)}, u32[]{:S(2)}) async-start(f32[64,3,4,130]{3,2,1,0:T(4,128)} %broadcast_in_dim.345), calls=%async_computation.7 | async-start | bytes 1572864 | tf_op jit(solution)/shard_map/all_to_all | solution.py:137
  117.3 2.3 copy.329
  120.0 4.9 %copy.330 = bf16[16,64,2,768]{3,2,0,1:T(2,128)(2,1)} copy(bf16[16,64,2,768]{3,0,2,1:T(8,128)(2,1)S(1)} %bitcast.122) | data formatting | bytes 6291456 | tf_op jit(solution)/shard_map/reshape | solution.py:67
  125.0 14.3 %all-to-all-done.7 = f32[64,3,4,130]{3,2,1,0:T(4,128)S(1)} async-done(((f32[64,3,4,130]{3,2,1,0:T(4,128)}), f32[64,3,4,130]{3,2,1,0:T(4,128)S(1)}, u32[]{:S(2)}, u32[]{:S(2)}) %all-to-all-start.7) | async-done | bytes 399392 | tf_op jit(solution)/shard_map/all_to_all | solution.py:137
  139.2 6.4 %all-to-all-start.3 = ((bf16[16,64,2,768]{3,2,0,1:T(2,128)(2,1)}), bf16[16,64,2,768]{3,2,0,1:T(2,128)(2,1)}, u32[]{:S(2)}, u32[]{:S(2)}) async-start(bf16[16,64,2,768]{3,2,0,1:T(2,128)(2,1)} %copy.330), calls=%async_computation.3 | async-start | bytes 6291456 | tf_op jit(solution)/shard_map/all_to_all | solution.py:70
  150.7 2.6 compare_reduce_fusion
  157.7 1.4 fusion.34
  161.5 57.5 %all-to-all-done.3 = bf16[16,64,2,768]{3,2,0,1:T(2,128)(2,1)} async-done(((bf16[16,64,2,768]{3,2,0,1:T(2,128)(2,1)}), bf16[16,64,2,768]{3,2,0,1:T(2,128)(2,1)}, u32[]{:S(2)}, u32[]{:S(2)}) %all-to-all-start.3) | async-done | bytes 3145760 | tf_op jit(solution)/shard_map/all_to_all | solution.py:70
  219.0 3.6 copy.331
  222.7 1.6 broadcast_in_dim.335
  225.1 252.8 %conditional.1 = (f32[3,256]{1,0:T(4,128)}, f32[3,256]{1,0:T(4,128)}, f32[3,256,128]{1,2,0:T(8,128)}) conditional(s32[]{:T(128)} %clamp.3, (s32[256]{0:T(256)S(1)}, pred[64,64]{1,0:T(8,128)(4,1)S(1)}, pred[64,64]{0,1:T(8,128)(4,1)S(1)}, s32[64,64]{0,1:T(8,128)S(1)}, bf16[1024,2,768]{2,0,1:T(8,128)(2,1)S(1)}, ...), branch_computations={%region_19.22_spmd, %region_22.25_spmd, %region_25.28_spmd} | conditional | flops 3318381056 | bytes 262674464 | solution.py:190
  232.5 4.9 %copy.337 = bf16[1024,2,768]{2,1,0:T(2,128)(2,1)} copy(bf16[1024,2,768]{2,0,1:T(8,128)(2,1)S(1)} %get-tuple-element.133) | data formatting | bytes 6291456 | tf_op jit(solution)/shard_map
  237.5 28.0 %gather_fusion.1 = bf16[2048,2,768]{2,1,0:T(2,128)(2,1)} fusion(bf16[1024,2,768]{2,1,0:T(2,128)(2,1)} %copy.337, s32[2048]{0:T(1024)S(1)} %broadcast_clamp_fusion), kind=kCustom, calls=%fused_computation.1 | custom fusion | bytes 12591104 | tf_op jit(solution)/shard_map/cond/branch_1_fun/jit(_take)/gather | solution.py:176
  265.5 11.0 %broadcast_select_fusion.3 = bf16[64,32,2,768]{3,2,1,0:T(2,128)(2,1)} fusion(pred[64,32]{1,0:T(8,128)(4,1)S(1)} %bitcast.152, bf16[64,32,2,768]{3,2,1,0:T(2,128)(2,1)} %bitcast.120, pred[64,32]{1,0:T(8,128)(4,1)S(1)} %compare_and_fusion.1), kind=kLoop, calls=%fused_computation.31 | loop fusion | flops 6291456 | bytes 12587008 | tf_op jit(solution)/shard_map/cond/branch_1_fun/jit(_where)/select_n | solution.py:174
  276.5 6.6 %all-to-all-start.1 = ((bf16[64,32,2,768]{3,2,1,0:T(2,128)(2,1)}), bf16[64,32,2,768]{3,2,1,0:T(2,128)(2,1)}, u32[]{:S(2)}, u32[]{:S(2)}) async-start(bf16[64,32,2,768]{3,2,1,0:T(2,128)(2,1)} %broadcast_select_fusion.3), calls=%async_computation.1 | async-start | bytes 12582912 | tf_op jit(solution)/shard_map/cond/branch_1_fun/all_to_all | solution.py:179
  284.7 1.9 broadcast_compare_fusion.1
  286.6 137.1 %all-to-all-done.1 = bf16[64,32,2,768]{3,2,1,0:T(2,128)(2,1)} async-done(((bf16[64,32,2,768]{3,2,1,0:T(2,128)(2,1)}), bf16[64,32,2,768]{3,2,1,0:T(2,128)(2,1)}, u32[]{:S(2)}, u32[]{:S(2)}) %all-to-all-start.1) | async-done | bytes 6291488 | tf_op jit(solution)/shard_map/cond/branch_1_fun/all_to_all | solution.py:179
  423.7 20.3 %reshape.445 = bf16[4096,2,3,128]{3,2,1,0:T(4,128)(2,1)} reshape(bf16[64,32,2,768]{3,2,1,0:T(2,128)(2,1)} %all-to-all-done.1) | data formatting | bytes 12582912 | tf_op jit(solution)/shard_map/cond/branch_1_fun/reshape | solution.py:180
  444.0 7.0 %fusion.78 = (bf16[4096,1,3,128]{3,2,1,0:T(4,128)(2,1)}, bf16[4096,1,3,128]{3,2,1,0:T(4,128)(2,1)S(1)}) fusion(bf16[4096,2,3,128]{3,2,1,0:T(4,128)(2,1)} %reshape.445), kind=kLoop, calls=%fused_computation.184 | loop fusion | bytes 12582912 | tf_op jit(solution)/shard_map/cond/branch_1_fun/slice | solution.py:185
  451.0 3.9 fusion.12
  454.9 4.5 fusion.14
  459.5 10.5 %fusion.15 = f32[3,256,128]{1,2,0:T(8,128)} fusion(f32[3,4096,256]{2,1,0:T(8,128)} %copy-done.4, f32[3,256]{1,0:T(4,128)} %get-tuple-element.256, pred[256,4096]{0,1:T(8,128)(4,1)S(1)} %broadcast_compare_fusion.1, bf16[4096,1,3,128]{3,2,1,0:T(4,128)(2,1)} %get-tuple-element.218), kind=kOutput, calls=%fused_computation.35 | convolution fusion | flops 821035008 | bytes 17173504 | tf_op jit(solution)/shard_map/cond | solution.py:190
  478.6 1.7 fusion.39
  (123 shorter events, 38.9 us)
Async XLA Ops:
  0.0 46.6 %copy-start.23 = (s32[128]{0:T(128)S(1)}, s32[128]{0:T(128)}, u32[]{:S(2)}) copy-start(s32[128]{0:T(128)} %param.22) | copy-start | bytes 1540
  0.0 64.0 %copy-start.22 = (s32[1024]{0:T(1024)S(1)}, s32[1024]{0:T(1024)}, u32[]{:S(2)}) copy-start(s32[1024]{0:T(1024)} %param.23) | copy-start | bytes 12292
  0.0 67.5 %copy-start.12 = (bf16[16,128,384]{2,1,0:T(8,128)(2,1)S(1)}, bf16[16,128,384]{2,1,0:T(8,128)(2,1)}, u32[]{:S(2)}) copy-start(bf16[16,128,384]{2,1,0:T(8,128)(2,1)} %param.19) | copy-start | bytes 4718596
  28.9 28.7 %all-to-all-start.4 = ((bf16[64,4,3,128]{3,1,2,0:T(4,128)(2,1)}), bf16[64,4,3,128]{3,1,2,0:T(4,128)(2,1)S(1)}, u32[]{:S(2)}, u32[]{:S(2)}) async-start(bf16[64,4,3,128]{3,1,2,0:T(4,128)(2,1)} %copy.370), calls=%async_computation.4 | async-start | bytes 393216 | tf_op jit(solution)/shard_map/all_to_all | solution.py:97
  58.3 16.6 %all-to-all-start.5 = ((bf16[64,4,3,128]{3,1,2,0:T(4,128)(2,1)}), bf16[64,4,3,128]{3,1,2,0:T(4,128)(2,1)S(1)}, u32[]{:S(2)}, u32[]{:S(2)}) async-start(bf16[64,4,3,128]{3,1,2,0:T(4,128)(2,1)} %broadcast_in_dim.342), calls=%async_computation.5 | async-start | bytes 393216 | tf_op jit(solution)/shard_map/all_to_all | solution.py:101
  64.1 10.9 %copy-start.13 = (s32[64,16]{1,0:T(8,128)}, s32[64,16]{1,0:T(8,128)S(1)}, u32[]{:S(2)}) copy-start(s32[64,16]{1,0:T(8,128)S(1)} %reshape.462) | copy-start | bytes 12292
  109.9 29.4 %all-to-all-start.7 = ((f32[64,3,4,130]{3,2,1,0:T(4,128)}), f32[64,3,4,130]{3,2,1,0:T(4,128)S(1)}, u32[]{:S(2)}, u32[]{:S(2)}) async-start(f32[64,3,4,130]{3,2,1,0:T(4,128)} %broadcast_in_dim.345), calls=%async_computation.7 | async-start | bytes 1572864 | tf_op jit(solution)/shard_map/all_to_all | solution.py:137
  120.0 26.3 %copy-start.18 = (bf16[256,384]{1,0:T(8,128)(2,1)S(1)}, bf16[256,384]{1,0:T(8,128)(2,1)}, u32[]{:S(2)}) copy-start(bf16[256,384]{1,0:T(8,128)(2,1)} %param.16) | copy-start | bytes 589828
  120.0 27.1 %copy-start.14 = (s32[64,16]{1,0:T(8,128)S(1)}, s32[64,16]{1,0:T(8,128)}, u32[]{:S(2)}) copy-start(s32[64,16]{1,0:T(8,128)} %copy-done.13) | copy-start | bytes 12292
  120.0 28.9 %copy-start.24 = (s32[2]{0:T(128)S(1)}, s32[2]{0:T(128)}, u32[]{:S(2)}) copy-start(s32[2]{0:T(128)} %constant.180.clone) | copy-start | bytes 28
  120.0 33.9 %copy-start.15 = (bf16[256,3,64]{2,0,1:T(8,128)(2,1)S(1)}, bf16[256,3,64]{2,0,1:T(8,128)(2,1)}, u32[]{:S(2)}) copy-start(bf16[256,3,64]{2,0,1:T(8,128)(2,1)} %get-tuple-element.226) | copy-start | bytes 294916
  120.0 33.9 %copy-start.16 = (bf16[256,3,64]{2,0,1:T(8,128)(2,1)S(1)}, bf16[256,3,64]{2,0,1:T(8,128)(2,1)}, u32[]{:S(2)}) copy-start(bf16[256,3,64]{2,0,1:T(8,128)(2,1)} %get-tuple-element.227) | copy-start | bytes 294916
  139.2 79.8 %all-to-all-start.3 = ((bf16[16,64,2,768]{3,2,0,1:T(2,128)(2,1)}), bf16[16,64,2,768]{3,2,0,1:T(2,128)(2,1)}, u32[]{:S(2)}, u32[]{:S(2)}) async-start(bf16[16,64,2,768]{3,2,0,1:T(2,128)(2,1)} %copy.330), calls=%async_computation.3 | async-start | bytes 6291456 | tf_op jit(solution)/shard_map/all_to_all | solution.py:70
  153.9 5.2 %copy-start.17 = (pred[256,256]{0,1:T(8,128)(4,1)}, pred[256,256]{0,1:T(8,128)(4,1)S(1)}, u32[]{:S(2)}) copy-start(pred[256,256]{0,1:T(8,128)(4,1)S(1)} %fusion.54) | copy-start | bytes 196612
  154.2 0.9 copy-start.11
  154.2 0.9 copy-start.19
  225.1 252.8 %copy-start.20 = (f32[3,256]{1,0:T(4,128)S(1)}, f32[3,256]{1,0:T(4,128)}, u32[]{:S(2)}) copy-start(f32[3,256]{1,0:T(4,128)} %copy-done.19) | copy-start | bytes 9220
  276.5 6.6 %copy-start.6 = (s32[64,16,64]{2,1,0:T(8,128)S(1)}, s32[64,16,64]{2,1,0:T(8,128)}, u32[]{:S(2)}) copy-start(s32[64,16,64]{2,1,0:T(8,128)} %get-tuple-element.195) | copy-start | bytes 786436 | tf_op jit(solution)/shard_map/cond
  276.5 6.9 %copy-start.2 = (s32[64,64,64]{2,1,0:T(8,128)S(1)}, s32[64,64,64]{2,1,0:T(8,128)}, u32[]{:S(2)}) copy-start(s32[64,64,64]{2,1,0:T(8,128)} %get-tuple-element.177) | copy-start | bytes 3145732 | tf_op jit(solution)/shard_map/cond
  276.5 6.9 %copy-start.9 = (pred[64,64,64]{2,1,0:T(8,128)(4,1)S(1)}, pred[64,64,64]{2,1,0:T(8,128)(4,1)}, u32[]{:S(2)}) copy-start(pred[64,64,64]{2,1,0:T(8,128)(4,1)} %get-tuple-element.175) | copy-start | bytes 786436 | tf_op jit(solution)/shard_map/cond
  276.5 147.2 %all-to-all-start.1 = ((bf16[64,32,2,768]{3,2,1,0:T(2,128)(2,1)}), bf16[64,32,2,768]{3,2,1,0:T(2,128)(2,1)}, u32[]{:S(2)}, u32[]{:S(2)}) async-start(bf16[64,32,2,768]{3,2,1,0:T(2,128)(2,1)} %broadcast_select_fusion.3), calls=%async_computation.1 | async-start | bytes 12582912 | tf_op jit(solution)/shard_map/cond/branch_1_fun/all_to_all | solution.py:179
  454.9 4.6 copy-start.4

commit v3 on v0

v3 whole, which is shorter than its diff:
```python
import jax
import jax.numpy as jnp
from jax import lax
from jax.sharding import PartitionSpec as P

HD = 128


NEGATIVE = -1e30


def rotate(field, position):
    half = field.shape[-1] // 2
    freq = 500000.0 ** (-(jnp.arange(half, dtype=jnp.float32) / half))
    angle = position.astype(jnp.float32)[:, None] * freq[None, :]
    cosine = jnp.cos(angle)[:, None, :]
    sine = jnp.sin(angle)[:, None, :]
    first = field[..., :half]
    second = field[..., half:]
    return jnp.concatenate([first * cosine - second * sine, second * cosine + first * sine], -1)


def token_meta(counts, prefix, first_req, block_len, tokens_here):
    cumul = jnp.cumsum(counts, axis=1)
    starts = cumul - counts
    order = jnp.arange(tokens_here, dtype=jnp.int32)
    local = jnp.sum((order[None, :, None] >= cumul[:, None, :]).astype(jnp.int32), -1)
    picker = (
        local[:, :, None] == jnp.arange(counts.shape[1], dtype=jnp.int32)[None, None, :]
    ).astype(jnp.int32)
    offset = order[None, :] - jnp.sum(picker * starts[:, None, :], -1)
    before = jnp.sum(picker * prefix[:, None, :], -1)
    return (first_req[:, None] + local, before * block_len + offset)


def head_partial(queries, keys_in, values_in, allowed):
    scores = jnp.einsum(
        "td,kd->tk", queries, keys_in, preferred_element_type=jnp.float32
    ) * queries.shape[-1] ** (-0.5)
    scores = jnp.where(allowed, scores, NEGATIVE)
    best = jnp.max(scores, -1)
    weights = jnp.where(allowed, jnp.exp(scores - best[:, None]), 0.0)
    total = jnp.sum(weights, -1)
    return best, total, weights.astype(jnp.bfloat16)


def shards(
    q_new, k_new, v_new, q_gain, k_gain, cache_k, cache_v, new_count, prefix_blocks, block_req
):
    tokens_here = q_new.shape[0]
    width_all = q_new.shape[1] * lax.axis_size("mp")
    heads_here = q_new.shape[1] // HD
    block_len = cache_k.shape[1]
    blocks_here = cache_k.shape[0]
    slots = lax.axis_size("seq")
    device = lax.axis_index("seq")
    per_dev = new_count.shape[1]

    owner_table = block_req.reshape(slots, blocks_here)
    dest_table = owner_table // per_dev
    targets = jnp.arange(slots, dtype=jnp.int32)
    mine = lax.dynamic_index_in_dim(dest_table, device, 0, keepdims=False)
    hit = mine[None, :] == targets[:, None]
    arrive = dest_table == device
    picks = jnp.sum(jnp.where(hit, jnp.arange(blocks_here, dtype=jnp.int32)[None, :], 0), 1)
    got_keys = lax.all_to_all(
        jnp.take(cache_k, picks, axis=0), "seq", split_axis=0, concat_axis=0, tiled=True
    )
    got_values = lax.all_to_all(
        jnp.take(cache_v, picks, axis=0), "seq", split_axis=0, concat_axis=0, tiled=True
    )
    slot_req = jnp.where(jnp.any(arrive, 1), jnp.sum(jnp.where(arrive, owner_table, 0), 1), -1)
    key_req = jnp.repeat(slot_req, block_len)
    keys_all = got_keys.reshape(slots * block_len, -1)
    values_all = got_values.reshape(slots * block_len, -1)

    query_f = q_new.astype(jnp.float32)
    key_f = k_new.astype(jnp.float32)
    square_q, square_k = lax.psum(
        (jnp.sum(query_f * query_f, -1), jnp.sum(key_f * key_f, -1)), "mp"
    )
    first_all = jnp.arange(slots, dtype=jnp.int32) * per_dev
    req_all, pos_all = token_meta(
        new_count, prefix_blocks.reshape(slots, per_dev), first_all, block_len, tokens_here
    )
    query_req = lax.dynamic_index_in_dim(req_all, device, 0, keepdims=False)
    position = lax.dynamic_index_in_dim(pos_all, device, 0, keepdims=False)
    normed_q = query_f * lax.rsqrt(square_q / width_all + 1e-06)[:, None] * q_gain
    normed_k = key_f * lax.rsqrt(square_k / width_all + 1e-06)[:, None] * k_gain
    queries = rotate(normed_q.reshape(tokens_here, heads_here, HD), position).astype(jnp.bfloat16)
    keys_here = rotate(normed_k.reshape(tokens_here, heads_here, HD), position).astype(jnp.bfloat16)
    order = jnp.arange(tokens_here, dtype=jnp.int32)
    causal = (query_req[:, None] == query_req[None, :]) & (order[:, None] >= order[None, :])
    seen = query_req[:, None] == key_req[None, :]

    heads = []
    for head in range(heads_here):
        cols = slice(head * HD, (head + 1) * HD)
        query_h = queries[:, head]
        best_n, total_n, weights_n = head_partial(query_h, keys_here[:, head], None, causal)
        best_c, total_c, weights_c = head_partial(query_h, keys_all[:, cols], None, seen)
        best = jnp.maximum(best_n, best_c)
        factor_n = jnp.exp(best_n - best)
        factor_c = jnp.exp(best_c - best)
        total = total_n * factor_n + total_c * factor_c
        accum = jnp.einsum(
            "tk,kd->td", weights_n, v_new[:, cols], preferred_element_type=jnp.float32
        ) * factor_n[:, None] + jnp.einsum(
            "tk,kd->td", weights_c, values_all[:, cols], preferred_element_type=jnp.float32
        ) * factor_c[:, None]
        heads.append((accum / total[:, None]).astype(jnp.bfloat16))
    return jnp.concatenate(heads, -1)


def solution(mesh):
    return jax.shard_map(
        shards,
        mesh=mesh,
        in_specs=(
            P("seq", "mp"),
            P("seq", "mp"),
            P("seq", "mp"),
            P("mp"),
            P("mp"),
            P("seq", None, "mp"),
            P("seq", None, "mp"),
            P(),
            P(),
            P(),
        ),
        out_specs=P("seq", "mp"),
        check_vma=False,
    )
```

time: 393 us -> 337 us (0.86)
  local copies, waits for them, and re-layouts: 61.6 us -> 11.7 us
  matrix products: 35.5 us -> 26.7 us
    reshape x3 -> x0, local copies, waits for them, and re-layouts: 34.1 us -> none  [the longest x1 16.6 us: shards(): keys_all = got_keys.reshape(rounds, group * block_len, heads_here, HD)]
    while x11 -> x0, local copies, waits for them, and re-layouts: 15.5 us -> none  [the longest x3 15.5 us: shards(): carry, _ = lax.scan(visit, carry, (keys_all, values_all, owners_all))]
    select_n x1 -> x0, other arithmetic: 8.86 us -> none  [shards(): jnp.where(present, jnp.take(cache_v, picks, axis=0), jnp.zeros((), jnp.bf...]
    dot_general x18 -> x12, matrix products: 35.5 us -> 26.7 us  [the longest x3 13.5 us: shards(): jnp.einsum('tk,kd->td', weights_c, values_all[:, cols], preferred_element...]
    select_n x1 -> x2, other arithmetic: 0.01 us -> 8.63 us  [shards(): jnp.take(cache_k, picks, axis=0)]
    reduce_sum x9 -> x2, other arithmetic: 6.76 us -> 10.8 us  [head_partial(): total = jnp.sum(weights, -1)]
where the time goes in v3:
time: 337 us
  blocking collectives  171 us (51%)
  waiting for transfers between devices  98.8 us (29%)
  matrix products  26.7 us (8%)
  other arithmetic  21.6 us (6%)
  local copies, waits for them, and re-layouts  11.7 us (3%)
  starting transfers between devices  6.14 us (2%)
    all_to_all x1, blocking collectives, shards(): lax.all_to_all(jnp.take(cache_k, picks, axis=0), 'seq', split_axis=0, con...  156 us
    all_to_all x1, waiting for transfers between devices, shards(): lax.all_to_all(jnp.take(cache_v, picks, axis=0), 'seq', split_axis=0, con...  98.8 us
    psum x1, blocking collectives, shards(): lax.psum((jnp.sum(query_f * query_f, -1), jnp.sum(key_f * key_f, -1)), 'mp')  15.5 us
    dot_general x3, matrix products, shards(): jnp.einsum('tk,kd->td', weights_c, values_all[:, cols], preferred_element...  13.5 us
    dot_general x6, matrix products, head_partial(): jnp.einsum('td,kd->tk', queries, keys_in, preferred_element_type=jnp.floa...  12.4 us
    reduce_sum x2, other arithmetic, head_partial(): total = jnp.sum(weights, -1)  10.8 us
    select_n x2, other arithmetic, shards(): jnp.take(cache_k, picks, axis=0)  8.63 us
  transfers between devices with their start and end apart: 1, of which 1 were waited for; matrix products, arithmetic and copies ran while one was open for 8% of the time, Pallas kernels for 0%

profile of v3, /device:TPU:1, one launch (start us, length us, event | category | flops | bytes accessed | tf_op | source)
XLA Modules:
  0.0 336.6 jit_solution(16977366375277735498)
XLA Ops:
  0.0 0.9 reshape.174
  0.9 0.1 select_reduce_fusion.3
  1.2 0.2 copy-done
  1.4 4.1 %gather_fusion = bf16[64,128,384]{2,1,0:T(8,128)(2,1)} fusion(bf16[16,128,384]{2,1,0:T(8,128)(2,1)S(1)} %copy-done, s32[1024]{0:T(1024)S(1)} %pad_clamp_fusion), kind=kCustom, calls=%fused_computation.clone | custom fusion | bytes 12583168 | tf_op jit(solution)/shard_map/jit(_take)/gather | solution.py:67
  5.6 4.1 %gather_fusion.1 = bf16[64,128,384]{2,1,0:T(8,128)(2,1)} fusion(bf16[16,128,384]{2,1,0:T(8,128)(2,1)S(1)} %copy-done.2, s32[1024]{0:T(1024)S(1)} %pad_clamp_fusion), kind=kCustom, calls=%fused_computation.1.clone | custom fusion | bytes 12583168 | tf_op jit(solution)/shard_map/jit(_take)/gather | solution.py:70
  9.6 8.6 %broadcast_select_fusion.1 = (bf16[64,128,384]{2,1,0:T(8,128)(2,1)S(1)}, bf16[64,128,384]{2,1,0:T(8,128)(2,1)}) fusion(bf16[64,128,384]{2,1,0:T(8,128)(2,1)} %gather_fusion, pred[64]{0:T(512)(128)(4,1)S(1)} %compare_and_fusion, bf16[64,128,384]{2,1,0:T(8,128)(2,1)} %gather_fusion.1), kind=kLoop, calls=%fused_computation.18 | loop fusion | flops 6291456 | bytes 25165888 | tf_op jit(solution)/shard_map/jit(_take)/select_n | solution.py:67
  18.3 155.8 %all_to_all.10 = bf16[64,128,384]{2,1,0:T(8,128)(2,1)} all-to-all(bf16[64,128,384]{2,1,0:T(8,128)(2,1)S(1)} %get-tuple-element.36), channel_id=1, replica_groups=mesh['seq'=64,'mp'=8] {'seq'}, dimensions={0} | all-to-all | bytes 12582912 | tf_op jit(solution)/shard_map/all_to_all | solution.py:66
  174.1 6.1 %all-to-all-start.1 = ((bf16[64,128,384]{2,1,0:T(8,128)(2,1)}), bf16[64,128,384]{2,1,0:T(8,128)(2,1)}, u32[]{:S(2)}, u32[]{:S(2)}) async-start(bf16[64,128,384]{2,1,0:T(8,128)(2,1)} %get-tuple-element.37), calls=%async_computation.1 | async-start | bytes 12582912 | tf_op jit(solution)/shard_map/all_to_all | solution.py:69
  180.3 0.1 copy.28
  180.4 0.1 copy.25
  180.6 0.1 mul.266
  180.8 0.6 dynamic-slice
  181.7 15.5 %all-reduce = (f32[256]{0:T(256)S(1)}, f32[256]{0:T(256)S(1)}) all-reduce(f32[256]{0:T(256)S(1)} %fusion.45, f32[256]{0:T(256)S(1)} %fusion.47), channel_id=1, replica_groups=mesh['seq'=64,'mp'=8] {'mp'}, use_global_device_ids=true, to_apply=%region_3.4 | all-reduce | flops 512 | bytes 4096 | tf_op jit(solution)/shard_map/psum | solution.py:79
  197.3 0.7 dynamic-slice_add_fusion
  198.1 0.3 multiply_cosine_fusion
  198.8 0.3 fusion.120
  199.1 0.3 fusion.121
  199.3 0.3 fusion.122
  199.6 0.2 fusion.50
  199.8 7.1 %fusion.117 = (f32[256]{0:T(256)S(1)}, f32[256,8192]{1,0:T(8,128)}) fusion(bf16[8192,384]{1,0:T(8,128)(2,1)} %bitcast.60, bf16[256,3,64]{0,2,1:T(8,128)(2,1)S(1)} %get-tuple-element.32, bf16[256,3,64]{0,2,1:T(8,128)(2,1)S(1)} %get-tuple-element.33, s32[8192]{0:T(1024)S(1)} %broadcast_bitcast_fusion, s32[256]{0:T(256)S(1)} %bitcast.71), kind=kOutput, calls=%fused_computation.161 | convolution fusion | flops 545390336 | bytes 10717184 | tf_op jit(solution)/shard_map/td,kd->tk/dot_general | solution.py:37
  206.9 2.3 fusion.118
  209.2 2.3 fusion.119
  211.5 10.7 %fusion = (f32[256]{0:T(256)S(1)}, f32[256]{0:T(256)S(1)}, f32[256]{0:T(256)S(1)}) fusion(f32[256,8192]{1,0:T(8,128)S(1)} %get-tuple-element.41, f32[256]{0:T(256)S(1)} %get-tuple-element.40, s32[8192]{0:T(1024)S(1)} %broadcast_bitcast_fusion, s32[256]{0:T(256)S(1)} %bitcast.74, f32[256,8192]{1,0:T(8,128)S(1)} %get-tuple-element.43, ...), kind=kLoop, calls=%fused_computation.11 | loop fusion | flops 20970752 | bytes 25205760 | tf_op jit(solution)/shard_map/reduce_sum | solution.py:43
  222.2 98.8 %all-to-all-done.1 = bf16[64,128,384]{2,1,0:T(8,128)(2,1)} async-done(((bf16[64,128,384]{2,1,0:T(8,128)(2,1)}), bf16[64,128,384]{2,1,0:T(8,128)(2,1)}, u32[]{:S(2)}, u32[]{:S(2)}) %all-to-all-start.1) | async-done | bytes 6291488 | tf_op jit(solution)/shard_map/all_to_all | solution.py:69
  321.1 6.0 %fusion.37 = f32[256,128]{0,1:T(8,128)S(1)} fusion(bf16[8192,384]{1,0:T(8,128)(2,1)} %bitcast.9, f32[256,8192]{1,0:T(8,128)} %get-tuple-element.39, f32[256]{0:T(256)S(1)} %get-tuple-element.38, s32[8192]{0:T(1024)S(1)} %broadcast_bitcast_fusion, s32[256]{0:T(256)S(1)} %bitcast.75, f32[256]{0:T(256)S(1)} %get-tuple-element.24), kind=kOutput, calls=%fused_computation.45 | convolution fusion | flops 545292288 | bytes 10652672 | tf_op jit(solution)/shard_map/tk,kd->td/dot_general | solution.py:108
  327.1 0.3 copy-done.5
  327.4 3.8 %fusion.32 = f32[256,128]{0,1:T(8,128)S(1)} fusion(bf16[8192,384]{1,0:T(8,128)(2,1)} %bitcast.9, f32[256,8192]{1,0:T(8,128)S(1)} %copy-done.5, f32[256]{0:T(256)S(1)} %get-tuple-element.42, s32[8192]{0:T(1024)S(1)} %broadcast_bitcast_fusion, s32[256]{0:T(256)S(1)} %bitcast.76, f32[256]{0:T(256)S(1)} %get-tuple-element.21), kind=kOutput, calls=%fused_computation.44 | convolution fusion | flops 545292288 | bytes 10652672 | tf_op jit(solution)/shard_map/tk,kd->td/dot_general | solution.py:108
  331.3 3.7 %fusion.27 = f32[256,128]{0,1:T(8,128)S(1)} fusion(bf16[8192,384]{1,0:T(8,128)(2,1)} %bitcast.9, f32[256,8192]{1,0:T(8,128)S(1)} %bitcast.59, f32[256]{0:T(256)S(1)} %get-tuple-element.40, s32[8192]{0:T(1024)S(1)} %broadcast_bitcast_fusion, s32[256]{0:T(256)S(1)} %bitcast.77, f32[256]{0:T(256)S(1)} %get-tuple-element.18), kind=kOutput, calls=%fused_computation.43 | convolution fusion | flops 545292288 | bytes 10652672 | tf_op jit(solution)/shard_map/tk,kd->td/dot_general | solution.py:108
  335.0 0.3 fusion.42
  335.2 0.3 fusion.43
  335.5 0.3 fusion.44
  335.8 0.8 copy.34
  (60 shorter events, 1.3 us)
Async XLA Ops:
  0.0 1.4 copy-start
  0.0 5.5 %copy-start.2 = (bf16[16,128,384]{2,1,0:T(8,128)(2,1)S(1)}, bf16[16,128,384]{2,1,0:T(8,128)(2,1)}, u32[]{:S(2)}) copy-start(bf16[16,128,384]{2,1,0:T(8,128)(2,1)} %param.18) | copy-start | bytes 4718596
  174.1 6.2 %copy-start.6 = (bf16[256,384]{1,0:T(8,128)(2,1)S(1)}, bf16[256,384]{1,0:T(8,128)(2,1)}, u32[]{:S(2)}) copy-start(bf16[256,384]{1,0:T(8,128)(2,1)} %param.13) | copy-start | bytes 589828
  174.1 6.3 %copy-start.7 = (bf16[256,384]{1,0:T(8,128)(2,1)S(1)}, bf16[256,384]{1,0:T(8,128)(2,1)}, u32[]{:S(2)}) copy-start(bf16[256,384]{1,0:T(8,128)(2,1)} %param.12) | copy-start | bytes 589828
  174.1 6.5 %copy-start.11 = (s32[128]{0:T(128)S(1)}, s32[128]{0:T(128)}, u32[]{:S(2)}) copy-start(s32[128]{0:T(128)} %param.20) | copy-start | bytes 1540
  174.1 6.7 %copy-start.8 = (s32[64,2]{0,1:T(2,128)S(1)}, s32[64,2]{0,1:T(2,128)}, u32[]{:S(2)}) copy-start(s32[64,2]{0,1:T(2,128)} %param.19) | copy-start | bytes 1540
  174.1 24.3 %copy-start.9 = (f32[384]{0:T(512)S(1)}, f32[384]{0:T(512)}, u32[]{:S(2)}) copy-start(f32[384]{0:T(512)} %param.16) | copy-start | bytes 4612
  174.1 24.5 %copy-start.10 = (f32[384]{0:T(512)S(1)}, f32[384]{0:T(512)}, u32[]{:S(2)}) copy-start(f32[384]{0:T(512)} %param.15) | copy-start | bytes 4612
  174.1 147.0 %all-to-all-start.1 = ((bf16[64,128,384]{2,1,0:T(8,128)(2,1)}), bf16[64,128,384]{2,1,0:T(8,128)(2,1)}, u32[]{:S(2)}, u32[]{:S(2)}) async-start(bf16[64,128,384]{2,1,0:T(8,128)(2,1)} %get-tuple-element.37), calls=%async_computation.1 | async-start | bytes 12582912 | tf_op jit(solution)/shard_map/all_to_all | solution.py:69
  198.6 8.4 %slice-start.2 = ((s8[6291456]{0:T(1024)(128)(4,1)}), s8[4194304]{0:T(1024)(128)(4,1)S(1)}, s32[]{:S(2)}) async-start(s8[6291456]{0:T(1024)(128)(4,1)} %bitcast.61), calls=%async_computation.4 | async-start | bytes 8388608
  199.8 7.1 %slice-start.3 = ((s8[6291456]{0:T(1024)(128)(4,1)}), s8[2097152]{0:T(1024)(128)(4,1)S(1)}, s32[]{:S(2)}) async-start(s8[6291456]{0:T(1024)(128)(4,1)} %bitcast.61), calls=%async_computation.5 | async-start | bytes 4194304
  209.2 13.0 %copy-start.3 = (f32[256,8192]{1,0:T(8,128)}, f32[256,8192]{1,0:T(8,128)S(1)}, u32[]{:S(2)}) copy-start(f32[256,8192]{1,0:T(8,128)S(1)} %get-tuple-element.41) | copy-start | bytes 25165828
  211.5 10.7 %copy-start.4 = (f32[256,8192]{1,0:T(8,128)}, f32[256,8192]{1,0:T(8,128)S(1)}, u32[]{:S(2)}) copy-start(f32[256,8192]{1,0:T(8,128)S(1)} %get-tuple-element.43) | copy-start | bytes 25165828
  321.1 6.4 %copy-start.5 = (f32[256,8192]{1,0:T(8,128)S(1)}, f32[256,8192]{1,0:T(8,128)}, u32[]{:S(2)}) copy-start(f32[256,8192]{1,0:T(8,128)} %copy-done.4) | copy-start | bytes 25165828
  321.1 10.2 %slice-start = ((s8[8388608]{0:T(1024)(128)(4,1)}), s8[4194304]{0:T(1024)(128)(4,1)S(1)}, s32[]{:S(2)}) async-start(s8[8388608]{0:T(1024)(128)(4,1)} %bitcast.58), calls=%async_computation.2 | async-start | bytes 8388608
  327.4 3.8 %slice-start.1 = ((s8[8388608]{0:T(1024)(128)(4,1)}), s8[4194304]{0:T(1024)(128)(4,1)S(1)}, s32[]{:S(2)}) async-start(s8[8388608]{0:T(1024)(128)(4,1)} %bitcast.58), calls=%async_computation.3 | async-start | bytes 8388608
  331.2 3.8 %copy-start.12 = (bf16[256,384]{1,0:T(8,128)(2,1)S(1)}, bf16[256,384]{1,0:T(8,128)(2,1)}, u32[]{:S(2)}) copy-start(bf16[256,384]{1,0:T(8,128)(2,1)} %param.14) | copy-start | bytes 589828
  331.2 5.4 %copy-start.1 = (bf16[16,128,384]{2,1,0:T(8,128)(2,1)S(1)}, bf16[16,128,384]{2,1,0:T(8,128)(2,1)}, u32[]{:S(2)}) copy-start(bf16[16,128,384]{2,1,0:T(8,128)(2,1)} %param.17) | copy-start | bytes 4718596

commit v4 on v3

--- a/solution.py
+++ b/solution.py
@@ -64,10 +64,10 @@
     arrive = dest_table == device
     picks = jnp.sum(jnp.where(hit, jnp.arange(blocks_here, dtype=jnp.int32)[None, :], 0), 1)
     got_keys = lax.all_to_all(
-        jnp.take(cache_k, picks, axis=0), "seq", split_axis=0, concat_axis=0, tiled=True
+        jnp.take(cache_k, picks, axis=0, mode="clip"), "seq", split_axis=0, concat_axis=0, tiled=True
     )
     got_values = lax.all_to_all(
-        jnp.take(cache_v, picks, axis=0), "seq", split_axis=0, concat_axis=0, tiled=True
+        jnp.take(cache_v, picks, axis=0, mode="clip"), "seq", split_axis=0, concat_axis=0, tiled=True
     )
     slot_req = jnp.where(jnp.any(arrive, 1), jnp.sum(jnp.where(arrive, owner_table, 0), 1), -1)
     key_req = jnp.repeat(slot_req, block_len)

time: 337 us -> 324 us (0.961)
  blocking collectives: 171 us -> 15.5 us
  waiting for transfers between devices: 98.8 us -> 231 us
  starting transfers between devices: 6.14 us -> 21.1 us
  other arithmetic: 21.6 us -> 13 us
  matrix products: 26.7 us -> 31 us
    all_to_all x1 -> x0, blocking collectives: 156 us -> none  [shards(): lax.all_to_all(jnp.take(cache_k, picks, axis=0), 'seq', split_axis=0, con...]
    all_to_all x1 -> x2, waiting for transfers between devices: 98.8 us -> 231 us  [the longest x1 137 us: shards(): lax.all_to_all(jnp.take(cache_k, picks, axis=0, mode='clip'), 'seq', spli...]
    all_to_all x1 -> x2, starting transfers between devices: 6.14 us -> 21.1 us  [the longest x1 15.1 us: shards(): lax.all_to_all(jnp.take(cache_k, picks, axis=0, mode='clip'), 'seq', spli...]
    select_n x2 -> x0, other arithmetic: 8.63 us -> none  [shards(): jnp.take(cache_k, picks, axis=0)]
    dot_general x6, matrix products: 12.4 us -> 16.8 us  [head_partial(): jnp.einsum('td,kd->tk', queries, keys_in, preferred_element_type=jnp.floa...]
  transfers between devices with their start and end apart: 1 -> 2, of which waited for: 1 -> 2; matrix products, arithmetic and copies ran while one was open for 8% -> 11% of each run, Pallas kernels for 0% -> 0%
where the time goes in v4:
time: 324 us
  waiting for transfers between devices  231 us (71%)
  matrix products  31 us (10%)
  starting transfers between devices  21.1 us (7%)
  blocking collectives  15.5 us (5%)
  other arithmetic  13 us (4%)
  local copies, waits for them, and re-layouts  11.7 us (4%)
    all_to_all x1, waiting for transfers between devices, shards(): lax.all_to_all(jnp.take(cache_k, picks, axis=0, mode='clip'), 'seq', spli...  137 us
    all_to_all x1, waiting for transfers between devices, shards(): lax.all_to_all(jnp.take(cache_v, picks, axis=0, mode='clip'), 'seq', spli...  94.4 us
    dot_general x6, matrix products, head_partial(): jnp.einsum('td,kd->tk', queries, keys_in, preferred_element_type=jnp.floa...  16.8 us
    psum x1, blocking collectives, shards(): lax.psum((jnp.sum(query_f * query_f, -1), jnp.sum(key_f * key_f, -1)), 'mp')  15.5 us
    all_to_all x1, starting transfers between devices, shards(): lax.all_to_all(jnp.take(cache_k, picks, axis=0, mode='clip'), 'seq', spli...  15.1 us
    dot_general x3, matrix products, shards(): jnp.einsum('tk,kd->td', weights_c, values_all[:, cols], preferred_element...  13.4 us
    reduce_sum x2, other arithmetic, head_partial(): total = jnp.sum(weights, -1)  10.9 us
  transfers between devices with their start and end apart: 2, of which 2 were waited for; matrix products, arithmetic and copies ran while one was open for 11% of the time, Pallas kernels for 0%

profile of v4, /device:TPU:1, one launch (start us, length us, event | category | flops | bytes accessed | tf_op | source)
XLA Modules:
  0.0 323.7 jit_solution(9113614697387491801)
XLA Ops:
  0.0 0.9 reshape.169
  0.9 0.1 select_reduce_fusion.3
  1.1 0.3 copy-done
  1.4 4.1 %gather_fusion = bf16[64,128,384]{2,1,0:T(8,128)(2,1)} fusion(bf16[16,128,384]{2,1,0:T(8,128)(2,1)S(1)} %copy-done, s32[1024]{0:T(1024)S(1)} %pad_clamp_fusion), kind=kCustom, calls=%fused_computation | custom fusion | bytes 12583168 | tf_op jit(solution)/shard_map/jit(_take)/gather | solution.py:67
  5.5 15.1 %all-to-all-start = ((bf16[64,128,384]{2,1,0:T(8,128)(2,1)}), bf16[64,128,384]{2,1,0:T(8,128)(2,1)}, u32[]{:S(2)}, u32[]{:S(2)}) async-start(bf16[64,128,384]{2,1,0:T(8,128)(2,1)} %gather_fusion), calls=%async_computation | async-start | bytes 12582912 | tf_op jit(solution)/shard_map/all_to_all | solution.py:66
  20.6 4.1 %gather_fusion.1 = bf16[64,128,384]{2,1,0:T(8,128)(2,1)} fusion(bf16[16,128,384]{2,1,0:T(8,128)(2,1)S(1)} %copy-done.1, s32[1024]{0:T(1024)S(1)} %pad_clamp_fusion), kind=kCustom, calls=%fused_computation.1 | custom fusion | bytes 12583168 | tf_op jit(solution)/shard_map/jit(_take)/gather | solution.py:70
  24.8 136.6 %all-to-all-done = bf16[64,128,384]{2,1,0:T(8,128)(2,1)} async-done(((bf16[64,128,384]{2,1,0:T(8,128)(2,1)}), bf16[64,128,384]{2,1,0:T(8,128)(2,1)}, u32[]{:S(2)}, u32[]{:S(2)}) %all-to-all-start) | async-done | bytes 6291488 | tf_op jit(solution)/shard_map/all_to_all | solution.py:66
  161.4 6.0 %all-to-all-start.1 = ((bf16[64,128,384]{2,1,0:T(8,128)(2,1)}), bf16[64,128,384]{2,1,0:T(8,128)(2,1)}, u32[]{:S(2)}, u32[]{:S(2)}) async-start(bf16[64,128,384]{2,1,0:T(8,128)(2,1)} %gather_fusion.1), calls=%async_computation.1 | async-start | bytes 12582912 | tf_op jit(solution)/shard_map/all_to_all | solution.py:69
  167.4 0.1 copy.28
  167.6 0.1 copy.25
  167.7 0.1 mul.266
  168.0 0.6 dynamic-slice
  168.9 15.5 %all-reduce = (f32[256]{0:T(256)S(1)}, f32[256]{0:T(256)S(1)}) all-reduce(f32[256]{0:T(256)S(1)} %fusion.45, f32[256]{0:T(256)S(1)} %fusion.47), channel_id=1, replica_groups=mesh['seq'=64,'mp'=8] {'mp'}, use_global_device_ids=true, to_apply=%region_3.4 | all-reduce | flops 512 | bytes 4096 | tf_op jit(solution)/shard_map/psum | solution.py:79
  184.5 0.7 dynamic-slice_add_fusion
  185.3 0.3 multiply_cosine_fusion
  186.0 0.3 fusion.120
  186.2 0.3 fusion.121
  186.5 0.3 fusion.122
  186.8 0.2 fusion.50
  187.0 6.9 %fusion.117 = (f32[256]{0:T(256)S(1)}, f32[256,8192]{1,0:T(8,128)}) fusion(bf16[8192,384]{1,0:T(8,128)(2,1)} %bitcast.8, bf16[256,3,64]{0,2,1:T(8,128)(2,1)S(1)} %get-tuple-element.31, bf16[256,3,64]{0,2,1:T(8,128)(2,1)S(1)} %get-tuple-element.32, s32[8192]{0:T(1024)S(1)} %broadcast_bitcast_fusion, s32[256]{0:T(256)S(1)} %bitcast.66), kind=kOutput, calls=%fused_computation.157 | convolution fusion | flops 545390336 | bytes 10717184 | tf_op jit(solution)/shard_map/td,kd->tk/dot_general | solution.py:37
  193.9 3.8 %fusion.118 = (f32[256]{0:T(256)S(1)}, f32[256,8192]{1,0:T(8,128)S(1)}) fusion(bf16[8192,384]{1,0:T(8,128)(2,1)} %bitcast.8, bf16[256,3,64]{0,2,1:T(8,128)(2,1)S(1)} %get-tuple-element.32, bf16[256,3,64]{0,2,1:T(8,128)(2,1)S(1)} %get-tuple-element.31, s32[8192]{0:T(1024)S(1)} %broadcast_bitcast_fusion, s32[256]{0:T(256)S(1)} %bitcast.67), kind=kOutput, calls=%fused_computation.158 | convolution fusion | flops 545390336 | bytes 10717184 | tf_op jit(solution)/shard_map/td,kd->tk/dot_general | solution.py:37
  197.7 5.3 %fusion.119 = (f32[256]{0:T(256)S(1)}, f32[256,8192]{1,0:T(8,128)S(1)}) fusion(bf16[8192,384]{1,0:T(8,128)(2,1)} %bitcast.8, bf16[256,3,64]{0,2,1:T(8,128)(2,1)S(1)} %get-tuple-element.32, bf16[256,3,64]{0,2,1:T(8,128)(2,1)S(1)} %get-tuple-element.31, s32[8192]{0:T(1024)S(1)} %broadcast_bitcast_fusion, s32[256]{0:T(256)S(1)} %bitcast.68), kind=kOutput, calls=%fused_computation.159 | convolution fusion | flops 545390336 | bytes 10717184 | tf_op jit(solution)/shard_map/td,kd->tk/dot_general | solution.py:37
  203.1 10.7 %fusion = (f32[256]{0:T(256)S(1)}, f32[256]{0:T(256)S(1)}, f32[256]{0:T(256)S(1)}) fusion(f32[256,8192]{1,0:T(8,128)S(1)} %get-tuple-element.38, f32[256]{0:T(256)S(1)} %get-tuple-element.37, s32[8192]{0:T(1024)S(1)} %broadcast_bitcast_fusion, s32[256]{0:T(256)S(1)} %bitcast.69, f32[256,8192]{1,0:T(8,128)S(1)} %get-tuple-element.40, ...), kind=kLoop, calls=%fused_computation.11 | loop fusion | flops 20970752 | bytes 25205760 | tf_op jit(solution)/shard_map/reduce_sum | solution.py:43
  213.8 94.4 %all-to-all-done.1 = bf16[64,128,384]{2,1,0:T(8,128)(2,1)} async-done(((bf16[64,128,384]{2,1,0:T(8,128)(2,1)}), bf16[64,128,384]{2,1,0:T(8,128)(2,1)}, u32[]{:S(2)}, u32[]{:S(2)}) %all-to-all-start.1) | async-done | bytes 6291488 | tf_op jit(solution)/shard_map/all_to_all | solution.py:69
  308.2 6.0 %fusion.37 = f32[256,128]{0,1:T(8,128)S(1)} fusion(bf16[8192,384]{1,0:T(8,128)(2,1)} %bitcast.9, f32[256,8192]{1,0:T(8,128)} %get-tuple-element.36, f32[256]{0:T(256)S(1)} %get-tuple-element.35, s32[8192]{0:T(1024)S(1)} %broadcast_bitcast_fusion, s32[256]{0:T(256)S(1)} %bitcast.70, f32[256]{0:T(256)S(1)} %get-tuple-element.23), kind=kOutput, calls=%fused_computation.43 | convolution fusion | flops 545292288 | bytes 10652672 | tf_op jit(solution)/shard_map/tk,kd->td/dot_general | solution.py:108
  314.3 0.3 copy-done.4
  314.6 3.8 %fusion.32 = f32[256,128]{0,1:T(8,128)S(1)} fusion(bf16[8192,384]{1,0:T(8,128)(2,1)} %bitcast.9, f32[256,8192]{1,0:T(8,128)S(1)} %copy-done.4, f32[256]{0:T(256)S(1)} %get-tuple-element.39, s32[8192]{0:T(1024)S(1)} %broadcast_bitcast_fusion, s32[256]{0:T(256)S(1)} %bitcast.71, f32[256]{0:T(256)S(1)} %get-tuple-element.20), kind=kOutput, calls=%fused_computation.42 | convolution fusion | flops 545292288 | bytes 10652672 | tf_op jit(solution)/shard_map/tk,kd->td/dot_general | solution.py:108
  318.4 3.6 %fusion.27 = f32[256,128]{0,1:T(8,128)S(1)} fusion(bf16[8192,384]{1,0:T(8,128)(2,1)} %bitcast.9, f32[256,8192]{1,0:T(8,128)S(1)} %bitcast.59, f32[256]{0:T(256)S(1)} %get-tuple-element.37, s32[8192]{0:T(1024)S(1)} %broadcast_bitcast_fusion, s32[256]{0:T(256)S(1)} %bitcast.72, f32[256]{0:T(256)S(1)} %get-tuple-element.17), kind=kOutput, calls=%fused_computation.41 | convolution fusion | flops 545292288 | bytes 10652672 | tf_op jit(solution)/shard_map/tk,kd->td/dot_general | solution.py:108
  322.0 0.3 fusion.42
  322.3 0.3 fusion.43
  322.6 0.3 fusion.44
  322.9 0.8 copy.34
  (51 shorter events, 1.3 us)
Async XLA Ops:
  0.0 1.4 copy-start
  5.5 15.1 %copy-start.1 = (bf16[16,128,384]{2,1,0:T(8,128)(2,1)S(1)}, bf16[16,128,384]{2,1,0:T(8,128)(2,1)}, u32[]{:S(2)}) copy-start(bf16[16,128,384]{2,1,0:T(8,128)(2,1)} %param.16) | copy-start | bytes 4718596
  5.5 155.9 %all-to-all-start = ((bf16[64,128,384]{2,1,0:T(8,128)(2,1)}), bf16[64,128,384]{2,1,0:T(8,128)(2,1)}, u32[]{:S(2)}, u32[]{:S(2)}) async-start(bf16[64,128,384]{2,1,0:T(8,128)(2,1)} %gather_fusion), calls=%async_computation | async-start | bytes 12582912 | tf_op jit(solution)/shard_map/all_to_all | solution.py:66
  24.8 142.6 %copy-start.5 = (bf16[256,384]{1,0:T(8,128)(2,1)S(1)}, bf16[256,384]{1,0:T(8,128)(2,1)}, u32[]{:S(2)}) copy-start(bf16[256,384]{1,0:T(8,128)(2,1)} %param.11) | copy-start | bytes 589828
  24.8 142.8 %copy-start.6 = (bf16[256,384]{1,0:T(8,128)(2,1)S(1)}, bf16[256,384]{1,0:T(8,128)(2,1)}, u32[]{:S(2)}) copy-start(bf16[256,384]{1,0:T(8,128)(2,1)} %param.10) | copy-start | bytes 589828
  24.8 143.0 %copy-start.10 = (s32[128]{0:T(128)S(1)}, s32[128]{0:T(128)}, u32[]{:S(2)}) copy-start(s32[128]{0:T(128)} %param.18) | copy-start | bytes 1540
  24.8 143.2 %copy-start.7 = (s32[64,2]{0,1:T(2,128)S(1)}, s32[64,2]{0,1:T(2,128)}, u32[]{:S(2)}) copy-start(s32[64,2]{0,1:T(2,128)} %param.17) | copy-start | bytes 1540
  24.8 160.8 %copy-start.8 = (f32[384]{0:T(512)S(1)}, f32[384]{0:T(512)}, u32[]{:S(2)}) copy-start(f32[384]{0:T(512)} %param.14) | copy-start | bytes 4612
  24.8 160.9 %copy-start.9 = (f32[384]{0:T(512)S(1)}, f32[384]{0:T(512)}, u32[]{:S(2)}) copy-start(f32[384]{0:T(512)} %param.13) | copy-start | bytes 4612
  161.4 146.8 %all-to-all-start.1 = ((bf16[64,128,384]{2,1,0:T(8,128)(2,1)}), bf16[64,128,384]{2,1,0:T(8,128)(2,1)}, u32[]{:S(2)}, u32[]{:S(2)}) async-start(bf16[64,128,384]{2,1,0:T(8,128)(2,1)} %gather_fusion.1), calls=%async_computation.1 | async-start | bytes 12582912 | tf_op jit(solution)/shard_map/all_to_all | solution.py:69
  197.7 16.1 %copy-start.2 = (f32[256,8192]{1,0:T(8,128)}, f32[256,8192]{1,0:T(8,128)S(1)}, u32[]{:S(2)}) copy-start(f32[256,8192]{1,0:T(8,128)S(1)} %get-tuple-element.38) | copy-start | bytes 25165828
  203.1 10.8 %copy-start.3 = (f32[256,8192]{1,0:T(8,128)}, f32[256,8192]{1,0:T(8,128)S(1)}, u32[]{:S(2)}) copy-start(f32[256,8192]{1,0:T(8,128)S(1)} %get-tuple-element.40) | copy-start | bytes 25165828
  308.2 6.4 %copy-start.4 = (f32[256,8192]{1,0:T(8,128)S(1)}, f32[256,8192]{1,0:T(8,128)}, u32[]{:S(2)}) copy-start(f32[256,8192]{1,0:T(8,128)} %copy-done.3) | copy-start | bytes 25165828
  308.2 10.2 %slice-start = ((s8[8388608]{0:T(1024)(128)(4,1)}), s8[4194304]{0:T(1024)(128)(4,1)S(1)}, s32[]{:S(2)}) async-start(s8[8388608]{0:T(1024)(128)(4,1)} %bitcast.58), calls=%async_computation.2 | async-start | bytes 8388608
  314.6 3.8 %slice-start.1 = ((s8[8388608]{0:T(1024)(128)(4,1)}), s8[4194304]{0:T(1024)(128)(4,1)S(1)}, s32[]{:S(2)}) async-start(s8[8388608]{0:T(1024)(128)(4,1)} %bitcast.58), calls=%async_computation.3 | async-start | bytes 8388608
  318.4 3.7 %copy-start.11 = (bf16[256,384]{1,0:T(8,128)(2,1)S(1)}, bf16[256,384]{1,0:T(8,128)(2,1)}, u32[]{:S(2)}) copy-start(bf16[256,384]{1,0:T(8,128)(2,1)} %param.12) | copy-start | bytes 589828

commit v5 on v4

--- a/solution.py
+++ b/solution.py
@@ -44,6 +44,17 @@
     return best, total, weights.astype(jnp.bfloat16)
 
 
+def mp_sum(x):
+    size = lax.axis_size("mp")
+    if size & (size - 1):
+        return lax.psum(x, "mp")
+    step = 1
+    while step < size:
+        x = x + lax.ppermute(x, "mp", [(i, i ^ step) for i in range(size)])
+        step *= 2
+    return x
+
+
 def shards(
     q_new, k_new, v_new, q_gain, k_gain, cache_k, cache_v, new_count, prefix_blocks, block_req
 ):
@@ -76,8 +87,8 @@
 
     query_f = q_new.astype(jnp.float32)
     key_f = k_new.astype(jnp.float32)
-    square_q, square_k = lax.psum(
-        (jnp.sum(query_f * query_f, -1), jnp.sum(key_f * key_f, -1)), "mp"
+    square_q, square_k = mp_sum(
+        jnp.stack([jnp.sum(query_f * query_f, -1), jnp.sum(key_f * key_f, -1)])
     )
     first_all = jnp.arange(slots, dtype=jnp.int32) * per_dev
     req_all, pos_all = token_meta(

time: 324 us -> 326 us (level)
  blocking collectives: 15.5 us -> 0 us
  starting transfers between devices: 21.1 us -> 36.1 us
  matrix products: 31 us -> 34.9 us
  other arithmetic: 13 us -> 9.66 us
    psum x1 -> x0, blocking collectives: 15.5 us -> none  [shards(): lax.psum((jnp.sum(query_f * query_f, -1), jnp.sum(key_f * key_f, -1)), 'mp')]
    ppermute x0 -> x3, starting transfers between devices: none -> 15 us  [mp_sum(): x = x + lax.ppermute(x, 'mp', [(i, i ^ step) for i in range(size)])]
    reduce_sum x2, other arithmetic: 10.9 us -> 7.48 us  [head_partial(): total = jnp.sum(weights, -1)]
  transfers between devices with their start and end apart: 2 -> 5, of which waited for: 2 -> 5; matrix products, arithmetic and copies ran while one was open for 11% -> 10% of each run, Pallas kernels for 0% -> 0%
where the time goes in v5:
time: 326 us
  waiting for transfers between devices  233 us (71%)
  starting transfers between devices  36.1 us (11%)
  matrix products  34.9 us (11%)
  local copies, waits for them, and re-layouts  11.3 us (3%)
  other arithmetic  9.66 us (3%)
    all_to_all x1, waiting for transfers between devices, shards(): lax.all_to_all(jnp.take(cache_k, picks, axis=0, mode='clip'), 'seq', spli...  137 us
    all_to_all x1, waiting for transfers between devices, shards(): lax.all_to_all(jnp.take(cache_v, picks, axis=0, mode='clip'), 'seq', spli...  94.8 us
    dot_general x6, matrix products, head_partial(): jnp.einsum('td,kd->tk', queries, keys_in, preferred_element_type=jnp.floa...  18.4 us
    dot_general x3, matrix products, shards(): jnp.einsum('tk,kd->td', weights_c, values_all[:, cols], preferred_element...  15.7 us
    all_to_all x1, starting transfers between devices, shards(): lax.all_to_all(jnp.take(cache_k, picks, axis=0, mode='clip'), 'seq', spli...  15.1 us
    ppermute x3, starting transfers between devices, mp_sum(): x = x + lax.ppermute(x, 'mp', [(i, i ^ step) for i in range(size)])  15 us
    reduce_sum x2, other arithmetic, head_partial(): total = jnp.sum(weights, -1)  7.48 us
  transfers between devices with their start and end apart: 5, of which 5 were waited for; matrix products, arithmetic and copies ran while one was open for 10% of the time, Pallas kernels for 0%

profile of v5, /device:TPU:1, one launch (start us, length us, event | category | flops | bytes accessed | tf_op | source)
XLA Modules:
  0.0 325.7 jit_solution(11145503005588184638)
XLA Ops:
  0.0 0.9 reshape.191
  1.1 0.3 copy-done
  1.4 4.1 %gather_fusion = bf16[64,128,384]{2,1,0:T(8,128)(2,1)} fusion(bf16[16,128,384]{2,1,0:T(8,128)(2,1)S(1)} %copy-done, s32[1024]{0:T(1024)S(1)} %pad_clamp_fusion), kind=kCustom, calls=%fused_computation | custom fusion | bytes 12583168 | tf_op jit(solution)/shard_map/jit(_take)/gather | solution.py:78
  5.5 15.1 %all-to-all-start = ((bf16[64,128,384]{2,1,0:T(8,128)(2,1)}), bf16[64,128,384]{2,1,0:T(8,128)(2,1)}, u32[]{:S(2)}, u32[]{:S(2)}) async-start(bf16[64,128,384]{2,1,0:T(8,128)(2,1)} %gather_fusion), calls=%async_computation | async-start | bytes 12582912 | tf_op jit(solution)/shard_map/all_to_all | solution.py:77
  20.6 4.1 %gather_fusion.1 = bf16[64,128,384]{2,1,0:T(8,128)(2,1)} fusion(bf16[16,128,384]{2,1,0:T(8,128)(2,1)S(1)} %copy-done.1, s32[1024]{0:T(1024)S(1)} %pad_clamp_fusion), kind=kCustom, calls=%fused_computation.1 | custom fusion | bytes 12583168 | tf_op jit(solution)/shard_map/jit(_take)/gather | solution.py:81
  24.8 136.7 %all-to-all-done = bf16[64,128,384]{2,1,0:T(8,128)(2,1)} async-done(((bf16[64,128,384]{2,1,0:T(8,128)(2,1)}), bf16[64,128,384]{2,1,0:T(8,128)(2,1)}, u32[]{:S(2)}, u32[]{:S(2)}) %all-to-all-start) | async-done | bytes 6291488 | tf_op jit(solution)/shard_map/all_to_all | solution.py:77
  161.5 6.0 %all-to-all-start.1 = ((bf16[64,128,384]{2,1,0:T(8,128)(2,1)}), bf16[64,128,384]{2,1,0:T(8,128)(2,1)}, u32[]{:S(2)}, u32[]{:S(2)}) async-start(bf16[64,128,384]{2,1,0:T(8,128)(2,1)} %gather_fusion.1), calls=%async_computation.1 | async-start | bytes 12582912 | tf_op jit(solution)/shard_map/all_to_all | solution.py:80
  167.9 3.2 collective-permute-start
  171.8 0.3 multiply_cosine_fusion
  172.1 0.5 collective-permute-done
  172.6 4.2 %collective-permute-start.1 = (f32[2,256]{1,0:T(2,128)S(1)}, f32[2,256]{1,0:T(2,128)S(1)}, u32[]{:S(2)}, u32[]{:S(2)}) collective-permute-start(f32[2,256]{1,0:T(2,128)S(1)} %fusion.109), channel_id=1, source_target_pairs={{0,2},{1,3},{2,0},{3,1},{4,6},{5,7},{6,4},{7,5},{8,10},{9,11},{10,... | collective-permute-start | bytes 6152 | tf_op jit(solution)/shard_map/ppermute | solution.py:53
  176.9 0.6 dynamic-slice
  177.5 0.8 collective-permute-done.1
  178.3 7.6 %collective-permute-start.2 = (f32[2,256]{1,0:T(2,128)S(1)}, f32[2,256]{1,0:T(2,128)S(1)}, u32[]{:S(2)}, u32[]{:S(2)}) collective-permute-start(f32[2,256]{1,0:T(2,128)S(1)} %fusion.128), channel_id=1, source_target_pairs={{0,4},{1,5},{2,6},{3,7},{4,0},{5,1},{6,2},{7,3},{8,12},{9,13},{10,... | collective-permute-start | bytes 6152 | tf_op jit(solution)/shard_map/ppermute | solution.py:53
  185.9 0.7 dynamic-slice_add_fusion
  186.6 0.5 collective-permute-done.2
  187.5 0.3 fusion.125
  187.8 0.3 fusion.126
  188.0 0.3 fusion.127
  188.3 0.2 fusion.50
  188.5 3.8 %fusion.122 = (f32[256]{0:T(256)S(1)}, f32[256,8192]{1,0:T(8,128)S(1)}) fusion(bf16[8192,384]{1,0:T(8,128)(2,1)} %bitcast.12, bf16[256,3,64]{0,2,1:T(8,128)(2,1)S(1)} %get-tuple-element.29, bf16[256,3,64]{0,2,1:T(8,128)(2,1)S(1)} %get-tuple-element.30, s32[8192]{0:T(1024)S(1)} %broadcast_bitcast_fusion, s32[256]{0:T(256)S(1)} %bitcast.70), kind=kOutput, calls=%fused_computation.163 | convolution fusion | flops 545390336 | bytes 10717184 | tf_op jit(solution)/shard_map/td,kd->tk/dot_general | solution.py:37
  192.3 5.3 %fusion.123 = (f32[256]{0:T(256)S(1)}, f32[256,8192]{1,0:T(8,128)S(1)}) fusion(bf16[8192,384]{1,0:T(8,128)(2,1)} %bitcast.12, bf16[256,3,64]{0,2,1:T(8,128)(2,1)S(1)} %get-tuple-element.30, bf16[256,3,64]{0,2,1:T(8,128)(2,1)S(1)} %get-tuple-element.29, s32[8192]{0:T(1024)S(1)} %broadcast_bitcast_fusion, s32[256]{0:T(256)S(1)} %bitcast.71), kind=kOutput, calls=%fused_computation.164 | convolution fusion | flops 545390336 | bytes 10717184 | tf_op jit(solution)/shard_map/td,kd->tk/dot_general | solution.py:37
  197.6 8.5 %fusion.124 = (f32[256]{0:T(256)S(1)}, f32[256,8192]{1,0:T(8,128)}) fusion(bf16[8192,384]{1,0:T(8,128)(2,1)} %bitcast.12, bf16[256,3,64]{0,2,1:T(8,128)(2,1)S(1)} %get-tuple-element.30, bf16[256,3,64]{0,2,1:T(8,128)(2,1)S(1)} %get-tuple-element.29, s32[8192]{0:T(1024)S(1)} %broadcast_bitcast_fusion, s32[256]{0:T(256)S(1)} %bitcast.72), kind=kOutput, calls=%fused_computation.165 | convolution fusion | flops 545390336 | bytes 10717184 | tf_op jit(solution)/shard_map/td,kd->tk/dot_general | solution.py:37
  206.1 7.3 %fusion = (f32[256]{0:T(256)S(1)}, f32[256]{0:T(256)S(1)}, f32[256]{0:T(256)S(1)}) fusion(f32[256,8192]{1,0:T(8,128)S(1)} %get-tuple-element.38, f32[256]{0:T(256)S(1)} %get-tuple-element.37, s32[8192]{0:T(1024)S(1)} %broadcast_bitcast_fusion, s32[256]{0:T(256)S(1)} %bitcast.73, f32[256,8192]{1,0:T(8,128)} %get-tuple-element.40, ...), kind=kLoop, calls=%fused_computation.11 | loop fusion | flops 20970752 | bytes 25205760 | tf_op jit(solution)/shard_map/reduce_sum | solution.py:43
  213.4 94.8 %all-to-all-done.1 = bf16[64,128,384]{2,1,0:T(8,128)(2,1)} async-done(((bf16[64,128,384]{2,1,0:T(8,128)(2,1)}), bf16[64,128,384]{2,1,0:T(8,128)(2,1)}, u32[]{:S(2)}, u32[]{:S(2)}) %all-to-all-start.1) | async-done | bytes 6291488 | tf_op jit(solution)/shard_map/all_to_all | solution.py:80
  308.2 6.0 %fusion.37 = f32[256,128]{0,1:T(8,128)S(1)} fusion(bf16[8192,384]{1,0:T(8,128)(2,1)} %bitcast.13, f32[256,8192]{1,0:T(8,128)} %copy-done.3, f32[256]{0:T(256)S(1)} %get-tuple-element.35, s32[8192]{0:T(1024)S(1)} %broadcast_bitcast_fusion, s32[256]{0:T(256)S(1)} %bitcast.74, f32[256]{0:T(256)S(1)} %get-tuple-element.21), kind=kOutput, calls=%fused_computation.43 | convolution fusion | flops 545292288 | bytes 10652672 | tf_op jit(solution)/shard_map/tk,kd->td/dot_general | solution.py:119
  314.3 6.0 %fusion.32 = f32[256,128]{0,1:T(8,128)S(1)} fusion(bf16[8192,384]{1,0:T(8,128)(2,1)} %bitcast.13, f32[256,8192]{1,0:T(8,128)} %get-tuple-element.40, f32[256]{0:T(256)S(1)} %get-tuple-element.39, s32[8192]{0:T(1024)S(1)} %broadcast_bitcast_fusion, s32[256]{0:T(256)S(1)} %bitcast.75, f32[256]{0:T(256)S(1)} %get-tuple-element.48), kind=kOutput, calls=%fused_computation.42 | convolution fusion | flops 545292288 | bytes 10652672 | tf_op jit(solution)/shard_map/tk,kd->td/dot_general | solution.py:119
  320.4 3.6 %fusion.27 = f32[256,128]{0,1:T(8,128)S(1)} fusion(bf16[8192,384]{1,0:T(8,128)(2,1)} %bitcast.13, f32[256,8192]{1,0:T(8,128)S(1)} %bitcast.63, f32[256]{0:T(256)S(1)} %get-tuple-element.37, s32[8192]{0:T(1024)S(1)} %broadcast_bitcast_fusion, s32[256]{0:T(256)S(1)} %bitcast.76, f32[256]{0:T(256)S(1)} %get-tuple-element.15), kind=kOutput, calls=%fused_computation.41 | convolution fusion | flops 545292288 | bytes 10652672 | tf_op jit(solution)/shard_map/tk,kd->td/dot_general | solution.py:119
  324.0 0.3 fusion.42
  324.3 0.3 fusion.43
  324.6 0.3 fusion.44
  324.9 0.8 copy.34
  (57 shorter events, 1.8 us)
Async XLA Ops:
  0.0 1.4 copy-start
  5.5 15.1 %copy-start.1 = (bf16[16,128,384]{2,1,0:T(8,128)(2,1)S(1)}, bf16[16,128,384]{2,1,0:T(8,128)(2,1)}, u32[]{:S(2)}) copy-start(bf16[16,128,384]{2,1,0:T(8,128)(2,1)} %param.16) | copy-start | bytes 4718596
  5.5 155.9 %all-to-all-start = ((bf16[64,128,384]{2,1,0:T(8,128)(2,1)}), bf16[64,128,384]{2,1,0:T(8,128)(2,1)}, u32[]{:S(2)}, u32[]{:S(2)}) async-start(bf16[64,128,384]{2,1,0:T(8,128)(2,1)} %gather_fusion), calls=%async_computation | async-start | bytes 12582912 | tf_op jit(solution)/shard_map/all_to_all | solution.py:77
  24.7 142.7 %copy-start.4 = (bf16[256,384]{1,0:T(8,128)(2,1)S(1)}, bf16[256,384]{1,0:T(8,128)(2,1)}, u32[]{:S(2)}) copy-start(bf16[256,384]{1,0:T(8,128)(2,1)} %param.11) | copy-start | bytes 589828
  24.7 142.9 %copy-start.5 = (bf16[256,384]{1,0:T(8,128)(2,1)S(1)}, bf16[256,384]{1,0:T(8,128)(2,1)}, u32[]{:S(2)}) copy-start(bf16[256,384]{1,0:T(8,128)(2,1)} %param.10) | copy-start | bytes 589828
  24.7 146.4 %copy-start.9 = (s32[128]{0:T(128)S(1)}, s32[128]{0:T(128)}, u32[]{:S(2)}) copy-start(s32[128]{0:T(128)} %param.18) | copy-start | bytes 1540
  24.7 146.6 %copy-start.6 = (s32[64,2]{0,1:T(2,128)S(1)}, s32[64,2]{0,1:T(2,128)}, u32[]{:S(2)}) copy-start(s32[64,2]{0,1:T(2,128)} %param.17) | copy-start | bytes 1540
  24.7 162.4 %copy-start.7 = (f32[384]{0:T(512)S(1)}, f32[384]{0:T(512)}, u32[]{:S(2)}) copy-start(f32[384]{0:T(512)} %param.14) | copy-start | bytes 4612
  24.7 162.5 %copy-start.8 = (f32[384]{0:T(512)S(1)}, f32[384]{0:T(512)}, u32[]{:S(2)}) copy-start(f32[384]{0:T(512)} %param.13) | copy-start | bytes 4612
  161.5 146.8 %all-to-all-start.1 = ((bf16[64,128,384]{2,1,0:T(8,128)(2,1)}), bf16[64,128,384]{2,1,0:T(8,128)(2,1)}, u32[]{:S(2)}, u32[]{:S(2)}) async-start(bf16[64,128,384]{2,1,0:T(8,128)(2,1)} %gather_fusion.1), calls=%async_computation.1 | async-start | bytes 12582912 | tf_op jit(solution)/shard_map/all_to_all | solution.py:80
  167.9 4.7 %collective-permute-start = (f32[2,256]{1,0:T(2,128)S(1)}, f32[2,256]{1,0:T(2,128)S(1)}, u32[]{:S(2)}, u32[]{:S(2)}) collective-permute-start(f32[2,256]{1,0:T(2,128)S(1)} %pad_maximum_fusion.3), channel_id=1, source_target_pairs={{0,1},{1,0},{2,3},{3,2},{4,5},{5,4},{6,7},{7,6},{8,9},{9,8},{10,11... | collective-permute-start | bytes 6152 | tf_op jit(solution)/shard_map/ppermute | solution.py:53
  172.6 5.6 %collective-permute-start.1 = (f32[2,256]{1,0:T(2,128)S(1)}, f32[2,256]{1,0:T(2,128)S(1)}, u32[]{:S(2)}, u32[]{:S(2)}) collective-permute-start(f32[2,256]{1,0:T(2,128)S(1)} %fusion.109), channel_id=1, source_target_pairs={{0,2},{1,3},{2,0},{3,1},{4,6},{5,7},{6,4},{7,5},{8,10},{9,11},{10,... | collective-permute-start | bytes 6152 | tf_op jit(solution)/shard_map/ppermute | solution.py:53
  178.3 8.8 %collective-permute-start.2 = (f32[2,256]{1,0:T(2,128)S(1)}, f32[2,256]{1,0:T(2,128)S(1)}, u32[]{:S(2)}, u32[]{:S(2)}) collective-permute-start(f32[2,256]{1,0:T(2,128)S(1)} %fusion.128), channel_id=1, source_target_pairs={{0,4},{1,5},{2,6},{3,7},{4,0},{5,1},{6,2},{7,3},{8,12},{9,13},{10,... | collective-permute-start | bytes 6152 | tf_op jit(solution)/shard_map/ppermute | solution.py:53
  192.2 13.8 %copy-start.3 = (f32[256,8192]{1,0:T(8,128)}, f32[256,8192]{1,0:T(8,128)S(1)}, u32[]{:S(2)}) copy-start(f32[256,8192]{1,0:T(8,128)S(1)} %get-tuple-element.36) | copy-start | bytes 25165828
  197.6 15.8 %copy-start.2 = (f32[256,8192]{1,0:T(8,128)}, f32[256,8192]{1,0:T(8,128)S(1)}, u32[]{:S(2)}) copy-start(f32[256,8192]{1,0:T(8,128)S(1)} %get-tuple-element.38) | copy-start | bytes 25165828
  308.2 12.1 %slice-start = ((s8[8388608]{0:T(1024)(128)(4,1)}), s8[4194304]{0:T(1024)(128)(4,1)S(1)}, s32[]{:S(2)}) async-start(s8[8388608]{0:T(1024)(128)(4,1)} %bitcast.62), calls=%async_computation.2 | async-start | bytes 8388608
  314.3 6.1 %slice-start.1 = ((s8[8388608]{0:T(1024)(128)(4,1)}), s8[4194304]{0:T(1024)(128)(4,1)S(1)}, s32[]{:S(2)}) async-start(s8[8388608]{0:T(1024)(128)(4,1)} %bitcast.62), calls=%async_computation.3 | async-start | bytes 8388608
  320.4 3.7 %copy-start.10 = (bf16[256,384]{1,0:T(8,128)(2,1)S(1)}, bf16[256,384]{1,0:T(8,128)(2,1)}, u32[]{:S(2)}) copy-start(bf16[256,384]{1,0:T(8,128)(2,1)} %param.12) | copy-start | bytes 589828

commit v6 on v4

--- a/solution.py
+++ b/solution.py
@@ -66,13 +66,16 @@
     got_keys = lax.all_to_all(
         jnp.take(cache_k, picks, axis=0, mode="clip"), "seq", split_axis=0, concat_axis=0, tiled=True
     )
-    got_values = lax.all_to_all(
-        jnp.take(cache_v, picks, axis=0, mode="clip"), "seq", split_axis=0, concat_axis=0, tiled=True
-    )
+    send_values = jnp.take(cache_v, picks, axis=0, mode="clip")
+    split = (heads_here - 1) * HD
+    got_values = [
+        lax.all_to_all(part, "seq", split_axis=0, concat_axis=0, tiled=True)
+        for part in (send_values[..., :split], send_values[..., split:])
+    ]
     slot_req = jnp.where(jnp.any(arrive, 1), jnp.sum(jnp.where(arrive, owner_table, 0), 1), -1)
     key_req = jnp.repeat(slot_req, block_len)
     keys_all = got_keys.reshape(slots * block_len, -1)
-    values_all = got_values.reshape(slots * block_len, -1)
+    values_all = [part.reshape(slots * block_len, -1) for part in got_values]
 
     query_f = q_new.astype(jnp.float32)
     key_f = k_new.astype(jnp.float32)
@@ -106,7 +109,10 @@
         accum = jnp.einsum(
             "tk,kd->td", weights_n, v_new[:, cols], preferred_element_type=jnp.float32
         ) * factor_n[:, None] + jnp.einsum(
-            "tk,kd->td", weights_c, values_all[:, cols], preferred_element_type=jnp.float32
+            "tk,kd->td",
+            weights_c,
+            values_all[0][:, cols] if head < heads_here - 1 else values_all[1],
+            preferred_element_type=jnp.float32,
         ) * factor_c[:, None]
         heads.append((accum / total[:, None]).astype(jnp.bfloat16))
     return jnp.concatenate(heads, -1)

time: 324 us -> 329 us (1.015)
  local copies, waits for them, and re-layouts: 11.7 us -> 19.3 us
  waiting for transfers between devices: 231 us -> 224 us
  starting transfers between devices: 21.1 us -> 27 us
    slice x0 -> x2, local copies, waits for them, and re-layouts: none -> 7.92 us  [the longest x1 4.76 us: shards(): send_values[..., :split]]
    all_to_all x1 -> x2, starting transfers between devices: 5.96 us -> 11.9 us  [shards(): lax.all_to_all(part, 'seq', split_axis=0, concat_axis=0, tiled=True)]
    all_to_all x1, waiting for transfers between devices: 137 us -> 132 us  [shards(): lax.all_to_all(jnp.take(cache_k, picks, axis=0, mode='clip'), 'seq', spli...]
    all_to_all x1 -> x2, waiting for transfers between devices: 94.4 us -> 91.8 us  [shards(): lax.all_to_all(part, 'seq', split_axis=0, concat_axis=0, tiled=True)]
  transfers between devices with their start and end apart: 2 -> 3, of which waited for: 2 -> 3; matrix products, arithmetic and copies ran while one was open for 11% -> 15% of each run, Pallas kernels for 0% -> 0%
where the time goes in v6:
time: 329 us; the launch traced here: 328 us
  waiting for transfers between devices  224 us (68%)
  matrix products  32.3 us (10%)
  starting transfers between devices  27 us (8%)
  local copies, waits for them, and re-layouts  19.3 us (6%)
  blocking collectives  15.5 us (5%)
  other arithmetic  9.77 us (3%)
    all_to_all x1, waiting for transfers between devices, shards(): lax.all_to_all(jnp.take(cache_k, picks, axis=0, mode='clip'), 'seq', spli...  132 us
    all_to_all x2, waiting for transfers between devices, shards(): lax.all_to_all(part, 'seq', split_axis=0, concat_axis=0, tiled=True)  91.8 us
    dot_general x6, matrix products, head_partial(): jnp.einsum('td,kd->tk', queries, keys_in, preferred_element_type=jnp.floa...  18.6 us
    psum x1, blocking collectives, shards(): lax.psum((jnp.sum(query_f * query_f, -1), jnp.sum(key_f * key_f, -1)), 'mp')  15.5 us
    all_to_all x1, starting transfers between devices, shards(): lax.all_to_all(jnp.take(cache_k, picks, axis=0, mode='clip'), 'seq', spli...  15.1 us
    dot_general x3, matrix products, shards(): jnp.einsum('tk,kd->td', weights_c, values_all[0][:, cols] if head < heads...  12.9 us
    all_to_all x2, starting transfers between devices, shards(): lax.all_to_all(part, 'seq', split_axis=0, concat_axis=0, tiled=True)  11.9 us
    reduce_sum x2, other arithmetic, head_partial(): total = jnp.sum(weights, -1)  7.63 us
  transfers between devices with their start and end apart: 3, of which 3 were waited for; matrix products, arithmetic and copies ran while one was open for 15% of the time, Pallas kernels for 0%

profile of v6, /device:TPU:1, one launch (start us, length us, event | category | flops | bytes accessed | tf_op | source)
XLA Modules:
  0.0 327.9 jit_solution(630550233788571591)
XLA Ops:
  0.0 0.9 reshape.172
  1.1 0.3 copy-done
  1.4 4.1 %gather_fusion = bf16[64,128,384]{2,1,0:T(8,128)(2,1)} fusion(bf16[16,128,384]{2,1,0:T(8,128)(2,1)S(1)} %copy-done, s32[1024]{0:T(1024)S(1)} %pad_clamp_fusion), kind=kCustom, calls=%fused_computation | custom fusion | bytes 12583168 | tf_op jit(solution)/shard_map/jit(_take)/gather | solution.py:67
  5.5 15.1 %all-to-all-start = ((bf16[64,128,384]{2,1,0:T(8,128)(2,1)}), bf16[64,128,384]{2,1,0:T(8,128)(2,1)}, u32[]{:S(2)}, u32[]{:S(2)}) async-start(bf16[64,128,384]{2,1,0:T(8,128)(2,1)} %gather_fusion), calls=%async_computation | async-start | bytes 12582912 | tf_op jit(solution)/shard_map/all_to_all | solution.py:66
  20.6 4.1 %gather_fusion.1 = bf16[64,128,384]{2,1,0:T(8,128)(2,1)} fusion(bf16[16,128,384]{2,1,0:T(8,128)(2,1)S(1)} %copy-done.1, s32[1024]{0:T(1024)S(1)} %pad_clamp_fusion), kind=kCustom, calls=%fused_computation.1 | custom fusion | bytes 12583168 | tf_op jit(solution)/shard_map/jit(_take)/gather | solution.py:69
  24.7 4.8 %slice.93 = bf16[64,128,256]{2,1,0:T(8,128)(2,1)} slice(bf16[64,128,384]{2,1,0:T(8,128)(2,1)} %gather_fusion.1), slice={[0:64], [0:128], [0:256]} | slice | bytes 8388608 | tf_op jit(solution)/shard_map/slice | solution.py:73
  29.5 131.9 %all-to-all-done = bf16[64,128,384]{2,1,0:T(8,128)(2,1)} async-done(((bf16[64,128,384]{2,1,0:T(8,128)(2,1)}), bf16[64,128,384]{2,1,0:T(8,128)(2,1)}, u32[]{:S(2)}, u32[]{:S(2)}) %all-to-all-start) | async-done | bytes 6291488 | tf_op jit(solution)/shard_map/all_to_all | solution.py:66
  161.4 6.0 %all-to-all-start.1 = ((bf16[64,128,256]{2,1,0:T(8,128)(2,1)}), bf16[64,128,256]{2,1,0:T(8,128)(2,1)}, u32[]{:S(2)}, u32[]{:S(2)}) async-start(bf16[64,128,256]{2,1,0:T(8,128)(2,1)} %slice.93), calls=%async_computation.1 | async-start | bytes 8388608 | tf_op jit(solution)/shard_map/all_to_all | solution.py:72
  167.4 3.2 slice.102
  170.6 0.6 dynamic-slice
  171.4 0.2 copy.25
  172.0 15.5 %all-reduce = (f32[256]{0:T(256)S(1)}, f32[256]{0:T(256)S(1)}) all-reduce(f32[256]{0:T(256)S(1)} %fusion.42, f32[256]{0:T(256)S(1)} %fusion.44), channel_id=1, replica_groups=mesh['seq'=64,'mp'=8] {'mp'}, use_global_device_ids=true, to_apply=%region_3.4 | all-reduce | flops 512 | bytes 4096 | tf_op jit(solution)/shard_map/psum | solution.py:82
  187.6 0.7 dynamic-slice_add_fusion
  188.4 0.3 multiply_cosine_fusion
  189.1 0.3 fusion.117
  189.4 0.3 fusion.119
  189.6 0.3 fusion.118
  189.9 0.2 fusion.47
  190.1 6.9 %fusion.114 = (f32[256]{0:T(256)S(1)}, f32[256,8192]{1,0:T(8,128)}) fusion(bf16[8192,384]{1,0:T(8,128)(2,1)} %bitcast.8, bf16[256,3,64]{0,2,1:T(8,128)(2,1)S(1)} %get-tuple-element.31, bf16[256,3,64]{0,2,1:T(8,128)(2,1)S(1)} %get-tuple-element.32, s32[8192]{0:T(1024)S(1)} %broadcast_bitcast_fusion, s32[256]{0:T(256)S(1)} %bitcast.66), kind=kOutput, calls=%fused_computation.156 | convolution fusion | flops 545390336 | bytes 10717184 | tf_op jit(solution)/shard_map/td,kd->tk/dot_general | solution.py:37
  197.1 6.9 %fusion.116 = (f32[256]{0:T(256)S(1)}, f32[256,8192]{1,0:T(8,128)}) fusion(bf16[8192,384]{1,0:T(8,128)(2,1)} %bitcast.8, bf16[256,3,64]{0,2,1:T(8,128)(2,1)S(1)} %get-tuple-element.32, bf16[256,3,64]{0,2,1:T(8,128)(2,1)S(1)} %get-tuple-element.31, s32[8192]{0:T(1024)S(1)} %broadcast_bitcast_fusion, s32[256]{0:T(256)S(1)} %bitcast.67), kind=kOutput, calls=%fused_computation.158 | convolution fusion | flops 545390336 | bytes 10717184 | tf_op jit(solution)/shard_map/td,kd->tk/dot_general | solution.py:37
  204.0 59.3 %all-to-all-done.1 = bf16[64,128,256]{2,1,0:T(8,128)(2,1)} async-done(((bf16[64,128,256]{2,1,0:T(8,128)(2,1)}), bf16[64,128,256]{2,1,0:T(8,128)(2,1)}, u32[]{:S(2)}, u32[]{:S(2)}) %all-to-all-start.1) | async-done | bytes 4194336 | tf_op jit(solution)/shard_map/all_to_all | solution.py:72
  263.3 5.9 %all-to-all-start.2 = ((bf16[64,128,128]{2,1,0:T(8,128)(2,1)}), bf16[64,128,128]{2,1,0:T(8,128)(2,1)}, u32[]{:S(2)}, u32[]{:S(2)}) async-start(bf16[64,128,128]{2,1,0:T(8,128)(2,1)} %slice.102), calls=%async_computation.2 | async-start | bytes 4194304 | tf_op jit(solution)/shard_map/all_to_all | solution.py:72
  269.3 3.9 %fusion.115 = (f32[256]{0:T(256)S(1)}, f32[256,8192]{1,0:T(8,128)S(1)}) fusion(bf16[8192,384]{1,0:T(8,128)(2,1)} %bitcast.8, bf16[256,3,64]{0,2,1:T(8,128)(2,1)S(1)} %get-tuple-element.32, bf16[256,3,64]{0,2,1:T(8,128)(2,1)S(1)} %get-tuple-element.31, s32[8192]{0:T(1024)S(1)} %broadcast_bitcast_fusion, s32[256]{0:T(256)S(1)} %bitcast.68), kind=kOutput, calls=%fused_computation.157 | convolution fusion | flops 545390336 | bytes 10717184 | tf_op jit(solution)/shard_map/td,kd->tk/dot_general | solution.py:37
  273.3 7.5 %fusion = (f32[256]{0:T(256)S(1)}, f32[256]{0:T(256)S(1)}, f32[256]{0:T(256)S(1)}) fusion(f32[256,8192]{1,0:T(8,128)S(1)} %get-tuple-element.38, f32[256]{0:T(256)S(1)} %get-tuple-element.37, s32[8192]{0:T(1024)S(1)} %broadcast_bitcast_fusion, s32[256]{0:T(256)S(1)} %bitcast.69, f32[256,8192]{1,0:T(8,128)S(1)} %copy-done.2, f32[256]{0:T(256)S(1)} %get-tuple-element.39, ...), kind=kLoop, calls=%fused_computation.11 | loop fusion | flops 20970752 | bytes 25205760 | tf_op jit(solution)/shard_map/reduce_sum | solution.py:43
  280.8 3.5 %fusion.26 = f32[256,128]{0,1:T(8,128)S(1)} fusion(bf16[8192,256]{1,0:T(8,128)(2,1)} %bitcast.9, f32[256,8192]{1,0:T(8,128)S(1)} %get-tuple-element.38, f32[256]{0:T(256)S(1)} %get-tuple-element.37, s32[8192]{0:T(1024)S(1)} %broadcast_bitcast_fusion, s32[256]{0:T(256)S(1)} %bitcast.70, f32[256]{0:T(256)S(1)} %get-tuple-element.17), kind=kOutput, calls=%fused_computation.40 | convolution fusion | flops 545292288 | bytes 10652672 | tf_op jit(solution)/shard_map/tk,kd->td/dot_general | solution.py:111
  284.3 3.5 %fusion.31 = f32[256,128]{0,1:T(8,128)S(1)} fusion(bf16[8192,256]{1,0:T(8,128)(2,1)} %bitcast.9, f32[256,8192]{1,0:T(8,128)S(1)} %copy-done.2, f32[256]{0:T(256)S(1)} %get-tuple-element.39, s32[8192]{0:T(1024)S(1)} %broadcast_bitcast_fusion, s32[256]{0:T(256)S(1)} %bitcast.71, f32[256]{0:T(256)S(1)} %get-tuple-element.20), kind=kOutput, calls=%fused_computation.41 | convolution fusion | flops 545292288 | bytes 10652672 | tf_op jit(solution)/shard_map/tk,kd->td/dot_general | solution.py:111
  287.8 32.5 %all-to-all-done.2 = bf16[64,128,128]{2,1,0:T(8,128)(2,1)} async-done(((bf16[64,128,128]{2,1,0:T(8,128)(2,1)}), bf16[64,128,128]{2,1,0:T(8,128)(2,1)}, u32[]{:S(2)}, u32[]{:S(2)}) %all-to-all-start.2) | async-done | bytes 2097184 | tf_op jit(solution)/shard_map/all_to_all | solution.py:72
  320.4 5.9 %fusion.36 = f32[256,128]{0,1:T(8,128)S(1)} fusion(bf16[8192,128]{1,0:T(8,128)(2,1)} %bitcast.14, f32[256,8192]{1,0:T(8,128)} %get-tuple-element.36, f32[256]{0:T(256)S(1)} %get-tuple-element.35, s32[8192]{0:T(1024)S(1)} %broadcast_bitcast_fusion, s32[256]{0:T(256)S(1)} %bitcast.72, f32[256]{0:T(256)S(1)} %get-tuple-element.23), kind=kOutput, calls=%fused_computation.42 | convolution fusion | flops 545292288 | bytes 10652672 | tf_op jit(solution)/shard_map/tk,kd->td/dot_general | solution.py:111
  326.3 0.3 fusion.41
  326.5 0.3 fusion.40
  326.8 0.3 fusion.39
  327.1 0.8 copy.34
  (46 shorter events, 1.7 us)
Async XLA Ops:
  0.0 1.4 copy-start
  5.5 15.1 %copy-start.1 = (bf16[16,128,384]{2,1,0:T(8,128)(2,1)S(1)}, bf16[16,128,384]{2,1,0:T(8,128)(2,1)}, u32[]{:S(2)}) copy-start(bf16[16,128,384]{2,1,0:T(8,128)(2,1)} %param.16) | copy-start | bytes 4718596
  5.5 155.9 %all-to-all-start = ((bf16[64,128,384]{2,1,0:T(8,128)(2,1)}), bf16[64,128,384]{2,1,0:T(8,128)(2,1)}, u32[]{:S(2)}, u32[]{:S(2)}) async-start(bf16[64,128,384]{2,1,0:T(8,128)(2,1)} %gather_fusion), calls=%async_computation | async-start | bytes 12582912 | tf_op jit(solution)/shard_map/all_to_all | solution.py:66
  29.5 141.7 %copy-start.5 = (s32[64,2]{0,1:T(2,128)S(1)}, s32[64,2]{0,1:T(2,128)}, u32[]{:S(2)}) copy-start(s32[64,2]{0,1:T(2,128)} %param.17) | copy-start | bytes 1540
  29.5 141.7 %copy-start.8 = (s32[128]{0:T(128)S(1)}, s32[128]{0:T(128)}, u32[]{:S(2)}) copy-start(s32[128]{0:T(128)} %param.18) | copy-start | bytes 1540
  29.5 142.0 %copy-start.3 = (bf16[256,384]{1,0:T(8,128)(2,1)S(1)}, bf16[256,384]{1,0:T(8,128)(2,1)}, u32[]{:S(2)}) copy-start(bf16[256,384]{1,0:T(8,128)(2,1)} %param.10) | copy-start | bytes 589828
  29.5 142.1 %copy-start.4 = (bf16[256,384]{1,0:T(8,128)(2,1)S(1)}, bf16[256,384]{1,0:T(8,128)(2,1)}, u32[]{:S(2)}) copy-start(bf16[256,384]{1,0:T(8,128)(2,1)} %param.11) | copy-start | bytes 589828
  29.5 159.2 %copy-start.6 = (f32[384]{0:T(512)S(1)}, f32[384]{0:T(512)}, u32[]{:S(2)}) copy-start(f32[384]{0:T(512)} %param.14) | copy-start | bytes 4612
  29.5 159.3 %copy-start.7 = (f32[384]{0:T(512)S(1)}, f32[384]{0:T(512)}, u32[]{:S(2)}) copy-start(f32[384]{0:T(512)} %param.13) | copy-start | bytes 4612
  161.4 101.8 %all-to-all-start.1 = ((bf16[64,128,256]{2,1,0:T(8,128)(2,1)}), bf16[64,128,256]{2,1,0:T(8,128)(2,1)}, u32[]{:S(2)}, u32[]{:S(2)}) async-start(bf16[64,128,256]{2,1,0:T(8,128)(2,1)} %slice.93), calls=%async_computation.1 | async-start | bytes 8388608 | tf_op jit(solution)/shard_map/all_to_all | solution.py:72
  263.3 57.1 %all-to-all-start.2 = ((bf16[64,128,128]{2,1,0:T(8,128)(2,1)}), bf16[64,128,128]{2,1,0:T(8,128)(2,1)}, u32[]{:S(2)}, u32[]{:S(2)}) async-start(bf16[64,128,128]{2,1,0:T(8,128)(2,1)} %slice.102), calls=%async_computation.2 | async-start | bytes 4194304 | tf_op jit(solution)/shard_map/all_to_all | solution.py:72
  269.2 4.0 %copy-start.2 = (f32[256,8192]{1,0:T(8,128)S(1)}, f32[256,8192]{1,0:T(8,128)}, u32[]{:S(2)}) copy-start(f32[256,8192]{1,0:T(8,128)} %get-tuple-element.40) | copy-start | bytes 25165828
  287.8 38.5 %copy-start.9 = (bf16[256,384]{1,0:T(8,128)(2,1)S(1)}, bf16[256,384]{1,0:T(8,128)(2,1)}, u32[]{:S(2)}) copy-start(bf16[256,384]{1,0:T(8,128)(2,1)} %param.12) | copy-start | bytes 589828

commit v7 on v4

--- a/solution.py
+++ b/solution.py
@@ -41,7 +41,7 @@
     best = jnp.max(scores, -1)
     weights = jnp.where(allowed, jnp.exp(scores - best[:, None]), 0.0)
     total = jnp.sum(weights, -1)
-    return best, total, weights.astype(jnp.bfloat16)
+    return lax.optimization_barrier((best, total, weights.astype(jnp.bfloat16)))
 
 
 def shards(

time: 324 us -> 320 us (0.988)
  waiting for transfers between devices: 231 us -> 227 us
    all_to_all x1, waiting for transfers between devices: 94.4 us -> 90.4 us  [shards(): lax.all_to_all(jnp.take(cache_v, picks, axis=0, mode='clip'), 'seq', spli...]
  transfers between devices with their start and end apart: 2 -> 2, of which waited for: 2 -> 2; matrix products, arithmetic and copies ran while one was open for 11% -> 12% of each run, Pallas kernels for 0% -> 0%
where the time goes in v7:
time: 320 us
  waiting for transfers between devices  227 us (71%)
  matrix products  30.1 us (9%)
  starting transfers between devices  21.1 us (7%)
  blocking collectives  15.6 us (5%)
  other arithmetic  14.6 us (5%)
  local copies, waits for them, and re-layouts  11.4 us (4%)
    all_to_all x1, waiting for transfers between devices, shards(): lax.all_to_all(jnp.take(cache_k, picks, axis=0, mode='clip'), 'seq', spli...  137 us
    all_to_all x1, waiting for transfers between devices, shards(): lax.all_to_all(jnp.take(cache_v, picks, axis=0, mode='clip'), 'seq', spli...  90.4 us
    dot_general x6, matrix products, head_partial(): jnp.einsum('td,kd->tk', queries, keys_in, preferred_element_type=jnp.floa...  18.5 us
    psum x1, blocking collectives, shards(): lax.psum((jnp.sum(query_f * query_f, -1), jnp.sum(key_f * key_f, -1)), 'mp')  15.6 us
    all_to_all x1, starting transfers between devices, shards(): lax.all_to_all(jnp.take(cache_k, picks, axis=0, mode='clip'), 'seq', spli...  15.1 us
    reduce_sum x2, other arithmetic, head_partial(): total = jnp.sum(weights, -1)  12.5 us
    dot_general x3, matrix products, shards(): jnp.einsum('tk,kd->td', weights_c, values_all[:, cols], preferred_element...  10.9 us
  transfers between devices with their start and end apart: 2, of which 2 were waited for; matrix products, arithmetic and copies ran while one was open for 12% of the time, Pallas kernels for 0%

profile of v7, /device:TPU:1, one launch (start us, length us, event | category | flops | bytes accessed | tf_op | source)
XLA Modules:
  0.0 320.1 jit_solution(12038743918591365608)
XLA Ops:
  0.0 0.9 reshape.106
  0.9 0.1 select_reduce_fusion.3
  1.1 0.3 copy-done
  1.4 4.1 %gather_fusion = bf16[64,128,384]{2,1,0:T(8,128)(2,1)} fusion(bf16[16,128,384]{2,1,0:T(8,128)(2,1)S(1)} %copy-done, s32[1024]{0:T(1024)S(1)} %pad_clamp_fusion), kind=kCustom, calls=%fused_computation | custom fusion | bytes 12583168 | tf_op jit(solution)/shard_map/jit(_take)/gather | solution.py:67
  5.5 15.1 %all-to-all-start = ((bf16[64,128,384]{2,1,0:T(8,128)(2,1)}), bf16[64,128,384]{2,1,0:T(8,128)(2,1)}, u32[]{:S(2)}, u32[]{:S(2)}) async-start(bf16[64,128,384]{2,1,0:T(8,128)(2,1)} %gather_fusion), calls=%async_computation | async-start | bytes 12582912 | tf_op jit(solution)/shard_map/all_to_all | solution.py:66
  20.6 4.1 %gather_fusion.1 = bf16[64,128,384]{2,1,0:T(8,128)(2,1)} fusion(bf16[16,128,384]{2,1,0:T(8,128)(2,1)S(1)} %copy-done.2, s32[1024]{0:T(1024)S(1)} %pad_clamp_fusion), kind=kCustom, calls=%fused_computation.1 | custom fusion | bytes 12583168 | tf_op jit(solution)/shard_map/jit(_take)/gather | solution.py:70
  24.8 136.7 %all-to-all-done = bf16[64,128,384]{2,1,0:T(8,128)(2,1)} async-done(((bf16[64,128,384]{2,1,0:T(8,128)(2,1)}), bf16[64,128,384]{2,1,0:T(8,128)(2,1)}, u32[]{:S(2)}, u32[]{:S(2)}) %all-to-all-start) | async-done | bytes 6291488 | tf_op jit(solution)/shard_map/all_to_all | solution.py:66
  161.5 6.0 %all-to-all-start.1 = ((bf16[64,128,384]{2,1,0:T(8,128)(2,1)}), bf16[64,128,384]{2,1,0:T(8,128)(2,1)}, u32[]{:S(2)}, u32[]{:S(2)}) async-start(bf16[64,128,384]{2,1,0:T(8,128)(2,1)} %gather_fusion.1), calls=%async_computation.1 | async-start | bytes 12582912 | tf_op jit(solution)/shard_map/all_to_all | solution.py:69
  167.5 0.1 mul.242
  167.7 0.2 copy.25
  167.9 0.1 copy.28
  168.0 0.6 dynamic-slice
  168.8 15.6 %all-reduce = (f32[256]{0:T(256)S(1)}, f32[256]{0:T(256)S(1)}) all-reduce(f32[256]{0:T(256)S(1)} %fusion.56, f32[256]{0:T(256)S(1)} %fusion.54), channel_id=1, replica_groups=mesh['seq'=64,'mp'=8] {'mp'}, use_global_device_ids=true, to_apply=%region_7.8 | all-reduce | flops 512 | bytes 4096 | tf_op jit(solution)/shard_map/psum | solution.py:79
  184.5 0.7 dynamic-slice_add_fusion
  185.3 0.3 multiply_cosine_fusion
  185.6 0.1 fusion.57
  186.0 0.3 fusion.110
  186.2 0.3 fusion.109
  186.5 0.3 fusion.108
  186.8 0.2 fusion.60
  187.1 3.8 %fusion.112 = (f32[256]{0:T(256)S(1)}, f32[256,8192]{1,0:T(8,128)S(1)}) fusion(bf16[8192,384]{1,0:T(8,128)(2,1)} %bitcast.8, bf16[256,3,64]{0,2,1:T(8,128)(2,1)S(1)} %get-tuple-element.66, bf16[256,3,64]{0,2,1:T(8,128)(2,1)S(1)} %get-tuple-element.67, s32[8192]{0:T(1024)S(1)} %broadcast_bitcast_fusion, s32[256]{0:T(256)S(1)} %bitcast.70), kind=kOutput, calls=%fused_computation.149 | convolution fusion | flops 545390336 | bytes 10717184 | tf_op jit(solution)/shard_map/td,kd->tk/dot_general | solution.py:37
  190.9 6.9 %fusion.113 = (f32[256]{0:T(256)S(1)}, f32[256,8192]{1,0:T(8,128)}) fusion(bf16[8192,384]{1,0:T(8,128)(2,1)} %bitcast.8, bf16[256,3,64]{0,2,1:T(8,128)(2,1)S(1)} %get-tuple-element.66, bf16[256,3,64]{0,2,1:T(8,128)(2,1)S(1)} %get-tuple-element.67, s32[8192]{0:T(1024)S(1)} %broadcast_bitcast_fusion, s32[256]{0:T(256)S(1)} %bitcast.71), kind=kOutput, calls=%fused_computation.150 | convolution fusion | flops 545390336 | bytes 10717184 | tf_op jit(solution)/shard_map/td,kd->tk/dot_general | solution.py:37
  197.9 6.9 %fusion.111 = (f32[256]{0:T(256)S(1)}, f32[256,8192]{1,0:T(8,128)}) fusion(bf16[8192,384]{1,0:T(8,128)(2,1)} %bitcast.8, bf16[256,3,64]{0,2,1:T(8,128)(2,1)S(1)} %get-tuple-element.67, bf16[256,3,64]{0,2,1:T(8,128)(2,1)S(1)} %get-tuple-element.66, s32[8192]{0:T(1024)S(1)} %broadcast_bitcast_fusion, s32[256]{0:T(256)S(1)} %bitcast.72), kind=kOutput, calls=%fused_computation.148 | convolution fusion | flops 545390336 | bytes 10717184 | tf_op jit(solution)/shard_map/td,kd->tk/dot_general | solution.py:37
  204.8 12.3 %fusion.1 = (f32[256]{0:T(256)S(1)}, f32[256]{0:T(256)S(1)}, f32[256]{0:T(256)S(1)}, bf16[256,8192]{1,0:T(8,128)(2,1)}, bf16[256,8192]{1,0:T(8,128)(2,1)}, /*index=5*/bf16[256,8192]{1,0:T(8,128)(2,1)}) fusion(f32[256,8192]{1,0:T(8,128)S(1)} %get-tuple-element.86, f32[256]{0:T(256)S(1)} %get-tuple-element.25, s32[8192]{0:T(1024)S(1)} %broadcast_bitcast_fusion, ...), kind=kLoop, calls=%fused_computation.12 | loop fusion | flops 27262208 | bytes 37788672 | tf_op jit(solution)/shard_map/reduce_sum | solution.py:43
  217.2 0.2 convolution_multiply_fusion.8
  217.4 0.2 convolution_multiply_fusion.7
  217.6 0.2 convolution_multiply_fusion.6
  217.9 90.4 %all-to-all-done.1 = bf16[64,128,384]{2,1,0:T(8,128)(2,1)} async-done(((bf16[64,128,384]{2,1,0:T(8,128)(2,1)}), bf16[64,128,384]{2,1,0:T(8,128)(2,1)}, u32[]{:S(2)}, u32[]{:S(2)}) %all-to-all-start.1) | async-done | bytes 6291488 | tf_op jit(solution)/shard_map/all_to_all | solution.py:69
  308.2 4.5 %fusion.51 = bf16[256,128]{0,1:T(8,128)(2,1)S(1)} fusion(f32[256,128]{0,1:T(8,128)S(1)} %convolution_multiply_fusion.8, bf16[256,8192]{1,0:T(8,128)(2,1)} %get-tuple-element.26, bf16[8192,384]{1,0:T(8,128)(2,1)} %bitcast.9, f32[256]{0:T(256)S(1)} %get-tuple-element.51, f32[256]{0:T(256)S(1)} %get-tuple-element.52), kind=kOutput, calls=%fused_computation.46 | convolution fusion | flops 537001984 | bytes 6490112 | tf_op jit(solution)/shard_map/tk,kd->td/dot_general | solution.py:108
  312.8 3.3 %fusion.48 = bf16[256,128]{0,1:T(8,128)(2,1)S(1)} fusion(f32[256,128]{0,1:T(8,128)S(1)} %convolution_multiply_fusion.7, bf16[256,8192]{1,0:T(8,128)(2,1)S(1)} %copy-done.4, bf16[8192,384]{1,0:T(8,128)(2,1)} %bitcast.9, f32[256]{0:T(256)S(1)} %get-tuple-element.54, f32[256]{0:T(256)S(1)} %get-tuple-element.55), kind=kOutput, calls=%fused_computation.45 | convolution fusion | flops 537001984 | bytes 6490112 | tf_op jit(solution)/shard_map/tk,kd->td/dot_general | solution.py:108
  316.1 3.1 fusion.45
  319.3 0.8 copy.34
  (46 shorter events, 1.1 us)
Async XLA Ops:
  0.0 1.4 copy-start
  5.5 15.1 %copy-start.2 = (bf16[16,128,384]{2,1,0:T(8,128)(2,1)S(1)}, bf16[16,128,384]{2,1,0:T(8,128)(2,1)}, u32[]{:S(2)}) copy-start(bf16[16,128,384]{2,1,0:T(8,128)(2,1)} %param.16) | copy-start | bytes 4718596
  5.5 155.9 %all-to-all-start = ((bf16[64,128,384]{2,1,0:T(8,128)(2,1)}), bf16[64,128,384]{2,1,0:T(8,128)(2,1)}, u32[]{:S(2)}, u32[]{:S(2)}) async-start(bf16[64,128,384]{2,1,0:T(8,128)(2,1)} %gather_fusion), calls=%async_computation | async-start | bytes 12582912 | tf_op jit(solution)/shard_map/all_to_all | solution.py:66
  24.7 142.7 %copy-start.8 = (s32[64,2]{0,1:T(2,128)S(1)}, s32[64,2]{0,1:T(2,128)}, u32[]{:S(2)}) copy-start(s32[64,2]{0,1:T(2,128)} %param.17) | copy-start | bytes 1540
  24.7 142.8 %copy-start.11 = (s32[128]{0:T(128)S(1)}, s32[128]{0:T(128)}, u32[]{:S(2)}) copy-start(s32[128]{0:T(128)} %param.18) | copy-start | bytes 1540
  24.7 143.0 %copy-start.6 = (bf16[256,384]{1,0:T(8,128)(2,1)S(1)}, bf16[256,384]{1,0:T(8,128)(2,1)}, u32[]{:S(2)}) copy-start(bf16[256,384]{1,0:T(8,128)(2,1)} %param.10) | copy-start | bytes 589828
  24.7 143.1 %copy-start.7 = (bf16[256,384]{1,0:T(8,128)(2,1)S(1)}, bf16[256,384]{1,0:T(8,128)(2,1)}, u32[]{:S(2)}) copy-start(bf16[256,384]{1,0:T(8,128)(2,1)} %param.11) | copy-start | bytes 589828
  24.7 160.9 %copy-start.9 = (f32[384]{0:T(512)S(1)}, f32[384]{0:T(512)}, u32[]{:S(2)}) copy-start(f32[384]{0:T(512)} %param.14) | copy-start | bytes 4612
  24.7 161.0 %copy-start.10 = (f32[384]{0:T(512)S(1)}, f32[384]{0:T(512)}, u32[]{:S(2)}) copy-start(f32[384]{0:T(512)} %param.13) | copy-start | bytes 4612
  161.5 146.8 %all-to-all-start.1 = ((bf16[64,128,384]{2,1,0:T(8,128)(2,1)}), bf16[64,128,384]{2,1,0:T(8,128)(2,1)}, u32[]{:S(2)}, u32[]{:S(2)}) async-start(bf16[64,128,384]{2,1,0:T(8,128)(2,1)} %gather_fusion.1), calls=%async_computation.1 | async-start | bytes 12582912 | tf_op jit(solution)/shard_map/all_to_all | solution.py:69
  204.8 12.4 %copy-start.5 = (bf16[256,384]{1,0:T(8,128)(2,1)S(1)}, bf16[256,384]{1,0:T(8,128)(2,1)}, u32[]{:S(2)}) copy-start(bf16[256,384]{1,0:T(8,128)(2,1)} %param.12) | copy-start | bytes 589828
  308.2 4.6 %copy-start.4 = (bf16[256,8192]{1,0:T(8,128)(2,1)S(1)}, bf16[256,8192]{1,0:T(8,128)(2,1)}, u32[]{:S(2)}) copy-start(bf16[256,8192]{1,0:T(8,128)(2,1)} %get-tuple-element.32) | copy-start | bytes 12582916
  308.2 7.8 %copy-start.3 = (bf16[256,8192]{1,0:T(8,128)(2,1)S(1)}, bf16[256,8192]{1,0:T(8,128)(2,1)}, u32[]{:S(2)}) copy-start(bf16[256,8192]{1,0:T(8,128)(2,1)} %get-tuple-element.38) | copy-start | bytes 12582916
  312.8 7.3 %copy-start.1 = (bf16[16,128,384]{2,1,0:T(8,128)(2,1)S(1)}, bf16[16,128,384]{2,1,0:T(8,128)(2,1)}, u32[]{:S(2)}) copy-start(bf16[16,128,384]{2,1,0:T(8,128)(2,1)} %param.15) | copy-start | bytes 4718596

commit v8 on v7

--- a/solution.py
+++ b/solution.py
@@ -103,9 +103,17 @@
         factor_n = jnp.exp(best_n - best)
         factor_c = jnp.exp(best_c - best)
         total = total_n * factor_n + total_c * factor_c
-        accum = jnp.einsum(
-            "tk,kd->td", weights_n, v_new[:, cols], preferred_element_type=jnp.float32
-        ) * factor_n[:, None] + jnp.einsum(
+        accum_n, factor_c, total = lax.optimization_barrier(
+            (
+                jnp.einsum(
+                    "tk,kd->td", weights_n, v_new[:, cols], preferred_element_type=jnp.float32
+                )
+                * factor_n[:, None],
+                factor_c,
+                total,
+            )
+        )
+        accum = accum_n + jnp.einsum(
             "tk,kd->td", weights_c, values_all[:, cols], preferred_element_type=jnp.float32
         ) * factor_c[:, None]
         heads.append((accum / total[:, None]).astype(jnp.bfloat16))

time: 320 us -> 320 us (level)
  no operation moved by 1% of the time
where the time goes in v8:
time: 320 us; the launch traced here: 319 us
  waiting for transfers between devices  227 us (71%)
  matrix products  29.6 us (9%)
  starting transfers between devices  21.1 us (7%)
  blocking collectives  15.6 us (5%)
  other arithmetic  15.3 us (5%)
  local copies, waits for them, and re-layouts  10.5 us (3%)
    all_to_all x1, waiting for transfers between devices, shards(): lax.all_to_all(jnp.take(cache_k, picks, axis=0, mode='clip'), 'seq', spli...  137 us
    all_to_all x1, waiting for transfers between devices, shards(): lax.all_to_all(jnp.take(cache_v, picks, axis=0, mode='clip'), 'seq', spli...  90.3 us
    dot_general x6, matrix products, head_partial(): jnp.einsum('td,kd->tk', queries, keys_in, preferred_element_type=jnp.floa...  18.5 us
    psum x1, blocking collectives, shards(): lax.psum((jnp.sum(query_f * query_f, -1), jnp.sum(key_f * key_f, -1)), 'mp')  15.6 us
    all_to_all x1, starting transfers between devices, shards(): lax.all_to_all(jnp.take(cache_k, picks, axis=0, mode='clip'), 'seq', spli...  15.1 us
    reduce_sum x2, other arithmetic, head_partial(): total = jnp.sum(weights, -1)  12.5 us
    dot_general x3, matrix products, shards(): jnp.einsum('tk,kd->td', weights_c, values_all[:, cols], preferred_element...  10.5 us
  transfers between devices with their start and end apart: 2, of which 2 were waited for; matrix products, arithmetic and copies ran while one was open for 12% of the time, Pallas kernels for 0%

profile of v8, /device:TPU:1, one launch (start us, length us, event | category | flops | bytes accessed | tf_op | source)
XLA Modules:
  0.0 319.5 jit_solution(15651001523860183907)
XLA Ops:
  0.0 0.9 reshape.106
  0.9 0.1 select_reduce_fusion.3
  1.1 0.3 copy-done
  1.4 4.1 %gather_fusion = bf16[64,128,384]{2,1,0:T(8,128)(2,1)} fusion(bf16[16,128,384]{2,1,0:T(8,128)(2,1)S(1)} %copy-done, s32[1024]{0:T(1024)S(1)} %pad_clamp_fusion), kind=kCustom, calls=%fused_computation | custom fusion | bytes 12583168 | tf_op jit(solution)/shard_map/jit(_take)/gather | solution.py:67
  5.5 15.1 %all-to-all-start = ((bf16[64,128,384]{2,1,0:T(8,128)(2,1)}), bf16[64,128,384]{2,1,0:T(8,128)(2,1)}, u32[]{:S(2)}, u32[]{:S(2)}) async-start(bf16[64,128,384]{2,1,0:T(8,128)(2,1)} %gather_fusion), calls=%async_computation | async-start | bytes 12582912 | tf_op jit(solution)/shard_map/all_to_all | solution.py:66
  20.6 4.1 %gather_fusion.1 = bf16[64,128,384]{2,1,0:T(8,128)(2,1)} fusion(bf16[16,128,384]{2,1,0:T(8,128)(2,1)S(1)} %copy-done.2, s32[1024]{0:T(1024)S(1)} %pad_clamp_fusion), kind=kCustom, calls=%fused_computation.1 | custom fusion | bytes 12583168 | tf_op jit(solution)/shard_map/jit(_take)/gather | solution.py:70
  24.8 136.7 %all-to-all-done = bf16[64,128,384]{2,1,0:T(8,128)(2,1)} async-done(((bf16[64,128,384]{2,1,0:T(8,128)(2,1)}), bf16[64,128,384]{2,1,0:T(8,128)(2,1)}, u32[]{:S(2)}, u32[]{:S(2)}) %all-to-all-start) | async-done | bytes 6291488 | tf_op jit(solution)/shard_map/all_to_all | solution.py:66
  161.5 6.0 %all-to-all-start.1 = ((bf16[64,128,384]{2,1,0:T(8,128)(2,1)}), bf16[64,128,384]{2,1,0:T(8,128)(2,1)}, u32[]{:S(2)}, u32[]{:S(2)}) async-start(bf16[64,128,384]{2,1,0:T(8,128)(2,1)} %gather_fusion.1), calls=%async_computation.1 | async-start | bytes 12582912 | tf_op jit(solution)/shard_map/all_to_all | solution.py:69
  167.5 0.1 mul.242
  167.7 0.2 copy.29
  167.9 0.1 copy.32
  168.0 0.6 dynamic-slice
  168.8 15.6 %all-reduce = (f32[256]{0:T(256)S(1)}, f32[256]{0:T(256)S(1)}) all-reduce(f32[256]{0:T(256)S(1)} %fusion.56, f32[256]{0:T(256)S(1)} %fusion.54), channel_id=1, replica_groups=mesh['seq'=64,'mp'=8] {'mp'}, use_global_device_ids=true, to_apply=%region_7.8 | all-reduce | flops 512 | bytes 4096 | tf_op jit(solution)/shard_map/psum | solution.py:79
  184.5 0.7 dynamic-slice_add_fusion
  185.3 0.3 multiply_cosine_fusion
  185.6 0.1 fusion.57
  186.0 0.3 fusion.110
  186.2 0.3 fusion.109
  186.5 0.3 fusion.108
  186.8 0.2 fusion.60
  187.1 3.8 %fusion.112 = (f32[256]{0:T(256)S(1)}, f32[256,8192]{1,0:T(8,128)S(1)}) fusion(bf16[8192,384]{1,0:T(8,128)(2,1)} %bitcast.8, bf16[256,3,64]{0,2,1:T(8,128)(2,1)S(1)} %get-tuple-element.84, bf16[256,3,64]{0,2,1:T(8,128)(2,1)S(1)} %get-tuple-element.85, s32[8192]{0:T(1024)S(1)} %broadcast_bitcast_fusion, s32[256]{0:T(256)S(1)} %bitcast.70), kind=kOutput, calls=%fused_computation.149 | convolution fusion | flops 545390336 | bytes 10717184 | tf_op jit(solution)/shard_map/td,kd->tk/dot_general | solution.py:37
  190.9 6.9 %fusion.113 = (f32[256]{0:T(256)S(1)}, f32[256,8192]{1,0:T(8,128)}) fusion(bf16[8192,384]{1,0:T(8,128)(2,1)} %bitcast.8, bf16[256,3,64]{0,2,1:T(8,128)(2,1)S(1)} %get-tuple-element.84, bf16[256,3,64]{0,2,1:T(8,128)(2,1)S(1)} %get-tuple-element.85, s32[8192]{0:T(1024)S(1)} %broadcast_bitcast_fusion, s32[256]{0:T(256)S(1)} %bitcast.71), kind=kOutput, calls=%fused_computation.150 | convolution fusion | flops 545390336 | bytes 10717184 | tf_op jit(solution)/shard_map/td,kd->tk/dot_general | solution.py:37
  197.9 6.9 %fusion.111 = (f32[256]{0:T(256)S(1)}, f32[256,8192]{1,0:T(8,128)}) fusion(bf16[8192,384]{1,0:T(8,128)(2,1)} %bitcast.8, bf16[256,3,64]{0,2,1:T(8,128)(2,1)S(1)} %get-tuple-element.85, bf16[256,3,64]{0,2,1:T(8,128)(2,1)S(1)} %get-tuple-element.84, s32[8192]{0:T(1024)S(1)} %broadcast_bitcast_fusion, s32[256]{0:T(256)S(1)} %bitcast.72), kind=kOutput, calls=%fused_computation.148 | convolution fusion | flops 545390336 | bytes 10717184 | tf_op jit(solution)/shard_map/td,kd->tk/dot_general | solution.py:37
  204.8 12.3 %fusion.1 = (f32[256]{0:T(256)S(1)}, f32[256]{0:T(256)S(1)}, f32[256]{0:T(256)S(1)}, bf16[256,8192]{1,0:T(8,128)(2,1)}, bf16[256,8192]{1,0:T(8,128)(2,1)}, /*index=5*/bf16[256,8192]{1,0:T(8,128)(2,1)}) fusion(f32[256,8192]{1,0:T(8,128)S(1)} %get-tuple-element.104, f32[256]{0:T(256)S(1)} %get-tuple-element.34, s32[8192]{0:T(1024)S(1)} %broadcast_bitcast_fusion, ...), kind=kLoop, calls=%fused_computation.12 | loop fusion | flops 27262208 | bytes 37788672 | tf_op jit(solution)/shard_map/reduce_sum | solution.py:43
  217.2 0.2 convolution_multiply_fusion.8
  217.4 0.2 convolution_multiply_fusion.7
  217.7 0.2 convolution_multiply_fusion.6
  217.9 90.3 %all-to-all-done.1 = bf16[64,128,384]{2,1,0:T(8,128)(2,1)} async-done(((bf16[64,128,384]{2,1,0:T(8,128)(2,1)}), bf16[64,128,384]{2,1,0:T(8,128)(2,1)}, u32[]{:S(2)}, u32[]{:S(2)}) %all-to-all-start.1) | async-done | bytes 6291488 | tf_op jit(solution)/shard_map/all_to_all | solution.py:69
  308.2 4.2 %fusion.51 = bf16[256,128]{1,0:T(8,128)(2,1)S(1)} fusion(f32[256,128]{1,0:T(8,128)S(1)} %convolution_multiply_fusion.8, bf16[256,8192]{1,0:T(8,128)(2,1)} %get-tuple-element.38, bf16[8192,384]{1,0:T(8,128)(2,1)} %bitcast.9, f32[256]{0:T(256)S(1)} %get-tuple-element.40, f32[256]{0:T(256)S(1)} %get-tuple-element.39), kind=kOutput, calls=%fused_computation.46 | convolution fusion | flops 537001984 | bytes 6490112 | tf_op jit(solution)/shard_map/tk,kd->td/dot_general | solution.py:116
  312.5 3.4 %fusion.48 = bf16[256,128]{1,0:T(8,128)(2,1)S(1)} fusion(f32[256,128]{1,0:T(8,128)S(1)} %convolution_multiply_fusion.7, bf16[256,8192]{1,0:T(8,128)(2,1)S(1)} %copy-done.4, bf16[8192,384]{1,0:T(8,128)(2,1)} %bitcast.9, f32[256]{0:T(256)S(1)} %get-tuple-element.49, f32[256]{0:T(256)S(1)} %get-tuple-element.48), kind=kOutput, calls=%fused_computation.45 | convolution fusion | flops 537001984 | bytes 6490112 | tf_op jit(solution)/shard_map/tk,kd->td/dot_general | solution.py:116
  315.9 2.9 fusion.45
  318.8 0.7 pad_maximum_fusion
  (45 shorter events, 1.1 us)
Async XLA Ops:
  0.0 1.4 copy-start
  5.5 15.1 %copy-start.2 = (bf16[16,128,384]{2,1,0:T(8,128)(2,1)S(1)}, bf16[16,128,384]{2,1,0:T(8,128)(2,1)}, u32[]{:S(2)}) copy-start(bf16[16,128,384]{2,1,0:T(8,128)(2,1)} %param.16) | copy-start | bytes 4718596
  5.5 155.9 %all-to-all-start = ((bf16[64,128,384]{2,1,0:T(8,128)(2,1)}), bf16[64,128,384]{2,1,0:T(8,128)(2,1)}, u32[]{:S(2)}, u32[]{:S(2)}) async-start(bf16[64,128,384]{2,1,0:T(8,128)(2,1)} %gather_fusion), calls=%async_computation | async-start | bytes 12582912 | tf_op jit(solution)/shard_map/all_to_all | solution.py:66
  24.7 142.7 %copy-start.8 = (s32[64,2]{0,1:T(2,128)S(1)}, s32[64,2]{0,1:T(2,128)}, u32[]{:S(2)}) copy-start(s32[64,2]{0,1:T(2,128)} %param.17) | copy-start | bytes 1540
  24.7 142.8 %copy-start.11 = (s32[128]{0:T(128)S(1)}, s32[128]{0:T(128)}, u32[]{:S(2)}) copy-start(s32[128]{0:T(128)} %param.18) | copy-start | bytes 1540
  24.7 143.0 %copy-start.6 = (bf16[256,384]{1,0:T(8,128)(2,1)S(1)}, bf16[256,384]{1,0:T(8,128)(2,1)}, u32[]{:S(2)}) copy-start(bf16[256,384]{1,0:T(8,128)(2,1)} %param.10) | copy-start | bytes 589828
  24.7 143.1 %copy-start.7 = (bf16[256,384]{1,0:T(8,128)(2,1)S(1)}, bf16[256,384]{1,0:T(8,128)(2,1)}, u32[]{:S(2)}) copy-start(bf16[256,384]{1,0:T(8,128)(2,1)} %param.11) | copy-start | bytes 589828
  24.7 160.9 %copy-start.9 = (f32[384]{0:T(512)S(1)}, f32[384]{0:T(512)}, u32[]{:S(2)}) copy-start(f32[384]{0:T(512)} %param.14) | copy-start | bytes 4612
  24.7 161.0 %copy-start.10 = (f32[384]{0:T(512)S(1)}, f32[384]{0:T(512)}, u32[]{:S(2)}) copy-start(f32[384]{0:T(512)} %param.13) | copy-start | bytes 4612
  161.5 146.8 %all-to-all-start.1 = ((bf16[64,128,384]{2,1,0:T(8,128)(2,1)}), bf16[64,128,384]{2,1,0:T(8,128)(2,1)}, u32[]{:S(2)}, u32[]{:S(2)}) async-start(bf16[64,128,384]{2,1,0:T(8,128)(2,1)} %gather_fusion.1), calls=%async_computation.1 | async-start | bytes 12582912 | tf_op jit(solution)/shard_map/all_to_all | solution.py:69
  204.8 12.4 %copy-start.5 = (bf16[256,384]{1,0:T(8,128)(2,1)S(1)}, bf16[256,384]{1,0:T(8,128)(2,1)}, u32[]{:S(2)}) copy-start(bf16[256,384]{1,0:T(8,128)(2,1)} %param.12) | copy-start | bytes 589828
  308.2 4.3 %copy-start.4 = (bf16[256,8192]{1,0:T(8,128)(2,1)S(1)}, bf16[256,8192]{1,0:T(8,128)(2,1)}, u32[]{:S(2)}) copy-start(bf16[256,8192]{1,0:T(8,128)(2,1)} %get-tuple-element.47) | copy-start | bytes 12582916
  308.2 7.6 %copy-start.3 = (bf16[256,8192]{1,0:T(8,128)(2,1)S(1)}, bf16[256,8192]{1,0:T(8,128)(2,1)}, u32[]{:S(2)}) copy-start(bf16[256,8192]{1,0:T(8,128)(2,1)} %get-tuple-element.56) | copy-start | bytes 12582916
  308.2 11.2 %copy-start.1 = (bf16[16,128,384]{2,1,0:T(8,128)(2,1)S(1)}, bf16[16,128,384]{2,1,0:T(8,128)(2,1)}, u32[]{:S(2)}) copy-start(bf16[16,128,384]{2,1,0:T(8,128)(2,1)} %param.15) | copy-start | bytes 4718596

commit v9 on v8

--- a/solution.py
+++ b/solution.py
@@ -116,8 +116,10 @@
         accum = accum_n + jnp.einsum(
             "tk,kd->td", weights_c, values_all[:, cols], preferred_element_type=jnp.float32
         ) * factor_c[:, None]
-        heads.append((accum / total[:, None]).astype(jnp.bfloat16))
-    return jnp.concatenate(heads, -1)
+        heads.append((accum, jnp.broadcast_to(total[:, None], accum.shape)))
+    accum = jnp.concatenate([part[0] for part in heads], -1)
+    total = jnp.concatenate([part[1] for part in heads], -1)
+    return (accum / total).astype(jnp.bfloat16)
 
 
 def solution(mesh):

time: 320 us -> 320 us (level)
  no operation moved by 1% of the time
where the time goes in v9:
time: 320 us
  waiting for transfers between devices  227 us (71%)
  matrix products  29.6 us (9%)
  starting transfers between devices  21.1 us (7%)
  blocking collectives  15.6 us (5%)
  other arithmetic  15.4 us (5%)
  local copies, waits for them, and re-layouts  10.8 us (3%)
    all_to_all x1, waiting for transfers between devices, shards(): lax.all_to_all(jnp.take(cache_k, picks, axis=0, mode='clip'), 'seq', spli...  137 us
    all_to_all x1, waiting for transfers between devices, shards(): lax.all_to_all(jnp.take(cache_v, picks, axis=0, mode='clip'), 'seq', spli...  90.3 us
    dot_general x6, matrix products, head_partial(): jnp.einsum('td,kd->tk', queries, keys_in, preferred_element_type=jnp.floa...  18.5 us
    psum x1, blocking collectives, shards(): lax.psum((jnp.sum(query_f * query_f, -1), jnp.sum(key_f * key_f, -1)), 'mp')  15.6 us
    all_to_all x1, starting transfers between devices, shards(): lax.all_to_all(jnp.take(cache_k, picks, axis=0, mode='clip'), 'seq', spli...  15.1 us
    reduce_sum x2, other arithmetic, head_partial(): total = jnp.sum(weights, -1)  12.5 us
    dot_general x3, matrix products, shards(): jnp.einsum('tk,kd->td', weights_c, values_all[:, cols], preferred_element...  10.5 us
  transfers between devices with their start and end apart: 2, of which 2 were waited for; matrix products, arithmetic and copies ran while one was open for 12% of the time, Pallas kernels for 0%

profile of v9, /device:TPU:1, one launch (start us, length us, event | category | flops | bytes accessed | tf_op | source)
XLA Modules:
  0.0 319.8 jit_solution(12469880382348561589)
XLA Ops:
  0.0 0.9 reshape.106
  0.9 0.1 select_reduce_fusion.3
  1.1 0.3 copy-done
  1.4 4.1 %gather_fusion = bf16[64,128,384]{2,1,0:T(8,128)(2,1)} fusion(bf16[16,128,384]{2,1,0:T(8,128)(2,1)S(1)} %copy-done, s32[1024]{0:T(1024)S(1)} %pad_clamp_fusion), kind=kCustom, calls=%fused_computation | custom fusion | bytes 12583168 | tf_op jit(solution)/shard_map/jit(_take)/gather | solution.py:67
  5.5 15.1 %all-to-all-start = ((bf16[64,128,384]{2,1,0:T(8,128)(2,1)}), bf16[64,128,384]{2,1,0:T(8,128)(2,1)}, u32[]{:S(2)}, u32[]{:S(2)}) async-start(bf16[64,128,384]{2,1,0:T(8,128)(2,1)} %gather_fusion), calls=%async_computation | async-start | bytes 12582912 | tf_op jit(solution)/shard_map/all_to_all | solution.py:66
  20.6 4.1 %gather_fusion.1 = bf16[64,128,384]{2,1,0:T(8,128)(2,1)} fusion(bf16[16,128,384]{2,1,0:T(8,128)(2,1)S(1)} %copy-done.2, s32[1024]{0:T(1024)S(1)} %pad_clamp_fusion), kind=kCustom, calls=%fused_computation.1 | custom fusion | bytes 12583168 | tf_op jit(solution)/shard_map/jit(_take)/gather | solution.py:70
  24.8 136.7 %all-to-all-done = bf16[64,128,384]{2,1,0:T(8,128)(2,1)} async-done(((bf16[64,128,384]{2,1,0:T(8,128)(2,1)}), bf16[64,128,384]{2,1,0:T(8,128)(2,1)}, u32[]{:S(2)}, u32[]{:S(2)}) %all-to-all-start) | async-done | bytes 6291488 | tf_op jit(solution)/shard_map/all_to_all | solution.py:66
  161.5 6.0 %all-to-all-start.1 = ((bf16[64,128,384]{2,1,0:T(8,128)(2,1)}), bf16[64,128,384]{2,1,0:T(8,128)(2,1)}, u32[]{:S(2)}, u32[]{:S(2)}) async-start(bf16[64,128,384]{2,1,0:T(8,128)(2,1)} %gather_fusion.1), calls=%async_computation.1 | async-start | bytes 12582912 | tf_op jit(solution)/shard_map/all_to_all | solution.py:69
  167.5 0.1 mul.242
  167.7 0.2 copy.29
  167.9 0.1 copy.32
  168.0 0.6 dynamic-slice
  168.8 15.6 %all-reduce = (f32[256]{0:T(256)S(1)}, f32[256]{0:T(256)S(1)}) all-reduce(f32[256]{0:T(256)S(1)} %fusion.38, f32[256]{0:T(256)S(1)} %fusion.36), channel_id=1, replica_groups=mesh['seq'=64,'mp'=8] {'mp'}, use_global_device_ids=true, to_apply=%region_7.8 | all-reduce | flops 512 | bytes 4096 | tf_op jit(solution)/shard_map/psum | solution.py:79
  184.5 0.7 dynamic-slice_add_fusion
  185.3 0.3 multiply_cosine_fusion
  185.6 0.1 fusion.39
  186.0 0.3 fusion.93
  186.2 0.3 fusion.92
  186.5 0.3 fusion.91
  186.8 0.2 fusion.43
  187.1 3.8 %fusion.95 = (f32[256]{0:T(256)S(1)}, f32[256,8192]{1,0:T(8,128)S(1)}) fusion(bf16[8192,384]{1,0:T(8,128)(2,1)} %bitcast.8, bf16[256,3,64]{0,2,1:T(8,128)(2,1)S(1)} %get-tuple-element.84, bf16[256,3,64]{0,2,1:T(8,128)(2,1)S(1)} %get-tuple-element.85, s32[8192]{0:T(1024)S(1)} %broadcast_bitcast_fusion, s32[256]{0:T(256)S(1)} %bitcast.70), kind=kOutput, calls=%fused_computation.144 | convolution fusion | flops 545390336 | bytes 10717184 | tf_op jit(solution)/shard_map/td,kd->tk/dot_general | solution.py:37
  190.9 6.9 %fusion.96 = (f32[256]{0:T(256)S(1)}, f32[256,8192]{1,0:T(8,128)}) fusion(bf16[8192,384]{1,0:T(8,128)(2,1)} %bitcast.8, bf16[256,3,64]{0,2,1:T(8,128)(2,1)S(1)} %get-tuple-element.84, bf16[256,3,64]{0,2,1:T(8,128)(2,1)S(1)} %get-tuple-element.85, s32[8192]{0:T(1024)S(1)} %broadcast_bitcast_fusion, s32[256]{0:T(256)S(1)} %bitcast.71), kind=kOutput, calls=%fused_computation.145 | convolution fusion | flops 545390336 | bytes 10717184 | tf_op jit(solution)/shard_map/td,kd->tk/dot_general | solution.py:37
  197.9 6.9 %fusion.94 = (f32[256]{0:T(256)S(1)}, f32[256,8192]{1,0:T(8,128)}) fusion(bf16[8192,384]{1,0:T(8,128)(2,1)} %bitcast.8, bf16[256,3,64]{0,2,1:T(8,128)(2,1)S(1)} %get-tuple-element.85, bf16[256,3,64]{0,2,1:T(8,128)(2,1)S(1)} %get-tuple-element.84, s32[8192]{0:T(1024)S(1)} %broadcast_bitcast_fusion, s32[256]{0:T(256)S(1)} %bitcast.72), kind=kOutput, calls=%fused_computation.143 | convolution fusion | flops 545390336 | bytes 10717184 | tf_op jit(solution)/shard_map/td,kd->tk/dot_general | solution.py:37
  204.8 12.3 %fusion.1 = (f32[256]{0:T(256)S(1)}, f32[256]{0:T(256)S(1)}, f32[256]{0:T(256)S(1)}, bf16[256,8192]{1,0:T(8,128)(2,1)}, bf16[256,8192]{1,0:T(8,128)(2,1)}, /*index=5*/bf16[256,8192]{1,0:T(8,128)(2,1)}) fusion(f32[256,8192]{1,0:T(8,128)S(1)} %get-tuple-element.104, f32[256]{0:T(256)S(1)} %get-tuple-element.34, s32[8192]{0:T(1024)S(1)} %broadcast_bitcast_fusion, ...), kind=kLoop, calls=%fused_computation.12 | loop fusion | flops 27262208 | bytes 37788672 | tf_op jit(solution)/shard_map/reduce_sum | solution.py:43
  217.2 0.2 convolution_multiply_fusion.8
  217.4 0.2 convolution_multiply_fusion.7
  217.7 0.2 convolution_multiply_fusion.6
  217.9 90.3 %all-to-all-done.1 = bf16[64,128,384]{2,1,0:T(8,128)(2,1)} async-done(((bf16[64,128,384]{2,1,0:T(8,128)(2,1)}), bf16[64,128,384]{2,1,0:T(8,128)(2,1)}, u32[]{:S(2)}, u32[]{:S(2)}) %all-to-all-start.1) | async-done | bytes 6291488 | tf_op jit(solution)/shard_map/all_to_all | solution.py:69
  308.2 4.3 %fusion.21 = f32[256,128]{1,0:T(8,128)S(1)} fusion(f32[256,128]{1,0:T(8,128)S(1)} %convolution_multiply_fusion.8, bf16[256,8192]{1,0:T(8,128)(2,1)} %get-tuple-element.38, bf16[8192,384]{1,0:T(8,128)(2,1)} %bitcast.9, f32[256]{0:T(256)S(1)} %get-tuple-element.39), kind=kOutput, calls=%fused_computation.33 | convolution fusion | flops 536936448 | bytes 6554624 | tf_op jit(solution)/shard_map/tk,kd->td/dot_general | solution.py:116
  312.5 3.3 %fusion.27 = f32[256,128]{1,0:T(8,128)S(1)} fusion(f32[256,128]{1,0:T(8,128)S(1)} %convolution_multiply_fusion.7, bf16[256,8192]{1,0:T(8,128)(2,1)S(1)} %copy-done.4, bf16[8192,384]{1,0:T(8,128)(2,1)} %bitcast.9, f32[256]{0:T(256)S(1)} %get-tuple-element.47), kind=kOutput, calls=%fused_computation.35 | convolution fusion | flops 536936448 | bytes 6554624 | tf_op jit(solution)/shard_map/tk,kd->td/dot_general | solution.py:116
  315.9 2.9 fusion.33
  319.1 0.8 fusion.40
  (48 shorter events, 1.4 us)
Async XLA Ops:
  0.0 1.4 copy-start
  5.5 15.1 %copy-start.2 = (bf16[16,128,384]{2,1,0:T(8,128)(2,1)S(1)}, bf16[16,128,384]{2,1,0:T(8,128)(2,1)}, u32[]{:S(2)}) copy-start(bf16[16,128,384]{2,1,0:T(8,128)(2,1)} %param.16) | copy-start | bytes 4718596
  5.5 155.9 %all-to-all-start = ((bf16[64,128,384]{2,1,0:T(8,128)(2,1)}), bf16[64,128,384]{2,1,0:T(8,128)(2,1)}, u32[]{:S(2)}, u32[]{:S(2)}) async-start(bf16[64,128,384]{2,1,0:T(8,128)(2,1)} %gather_fusion), calls=%async_computation | async-start | bytes 12582912 | tf_op jit(solution)/shard_map/all_to_all | solution.py:66
  24.7 142.7 %copy-start.8 = (s32[64,2]{0,1:T(2,128)S(1)}, s32[64,2]{0,1:T(2,128)}, u32[]{:S(2)}) copy-start(s32[64,2]{0,1:T(2,128)} %param.17) | copy-start | bytes 1540
  24.7 142.8 %copy-start.11 = (s32[128]{0:T(128)S(1)}, s32[128]{0:T(128)}, u32[]{:S(2)}) copy-start(s32[128]{0:T(128)} %param.18) | copy-start | bytes 1540
  24.7 143.0 %copy-start.6 = (bf16[256,384]{1,0:T(8,128)(2,1)S(1)}, bf16[256,384]{1,0:T(8,128)(2,1)}, u32[]{:S(2)}) copy-start(bf16[256,384]{1,0:T(8,128)(2,1)} %param.10) | copy-start | bytes 589828
  24.7 143.1 %copy-start.7 = (bf16[256,384]{1,0:T(8,128)(2,1)S(1)}, bf16[256,384]{1,0:T(8,128)(2,1)}, u32[]{:S(2)}) copy-start(bf16[256,384]{1,0:T(8,128)(2,1)} %param.11) | copy-start | bytes 589828
  24.7 160.9 %copy-start.9 = (f32[384]{0:T(512)S(1)}, f32[384]{0:T(512)}, u32[]{:S(2)}) copy-start(f32[384]{0:T(512)} %param.14) | copy-start | bytes 4612
  24.7 161.0 %copy-start.10 = (f32[384]{0:T(512)S(1)}, f32[384]{0:T(512)}, u32[]{:S(2)}) copy-start(f32[384]{0:T(512)} %param.13) | copy-start | bytes 4612
  161.5 146.8 %all-to-all-start.1 = ((bf16[64,128,384]{2,1,0:T(8,128)(2,1)}), bf16[64,128,384]{2,1,0:T(8,128)(2,1)}, u32[]{:S(2)}, u32[]{:S(2)}) async-start(bf16[64,128,384]{2,1,0:T(8,128)(2,1)} %gather_fusion.1), calls=%async_computation.1 | async-start | bytes 12582912 | tf_op jit(solution)/shard_map/all_to_all | solution.py:69
  204.8 12.4 %copy-start.5 = (bf16[256,384]{1,0:T(8,128)(2,1)S(1)}, bf16[256,384]{1,0:T(8,128)(2,1)}, u32[]{:S(2)}) copy-start(bf16[256,384]{1,0:T(8,128)(2,1)} %param.12) | copy-start | bytes 589828
  308.2 4.3 %copy-start.4 = (bf16[256,8192]{1,0:T(8,128)(2,1)S(1)}, bf16[256,8192]{1,0:T(8,128)(2,1)}, u32[]{:S(2)}) copy-start(bf16[256,8192]{1,0:T(8,128)(2,1)} %get-tuple-element.46) | copy-start | bytes 12582916
  308.2 7.6 %copy-start.3 = (bf16[256,8192]{1,0:T(8,128)(2,1)S(1)}, bf16[256,8192]{1,0:T(8,128)(2,1)}, u32[]{:S(2)}) copy-start(bf16[256,8192]{1,0:T(8,128)(2,1)} %get-tuple-element.54) | copy-start | bytes 12582916
  308.2 11.6 %copy-start.1 = (bf16[16,128,384]{2,1,0:T(8,128)(2,1)S(1)}, bf16[16,128,384]{2,1,0:T(8,128)(2,1)}, u32[]{:S(2)}) copy-start(bf16[16,128,384]{2,1,0:T(8,128)(2,1)} %param.15) | copy-start | bytes 4718596
